TPU v7x, 512 devices: a whole 4x4x16 slice. The times are simulated.
512 devices in a mesh: lat: 32 (over z, core), lon: 16 (over x, y).
Axes of the slice: x: 4, y: 4, z: 16, core: 2. Of those that a mesh axis runs over, the one named last changes fastest.
Arguments:
- source: float32 [8, 1024, 2048], P(None, 'lat', 'lon'), may hold values from -6 to 6
- kappa_lon: bfloat16 [8, 1024, 2048], P(None, 'lat', 'lon'), may hold values from 32768 to 262144
- kappa_lat: bfloat16 [8, 1024, 2048], P(None, 'lat', 'lon'), may hold values from 2048 to 16384
- sea_mask: int32 [8, 1024, 2048], P(None, 'lat', 'lon'), may hold values 0 or 1
Outputs:
- analysis: float32 [8, 1024, 2048], P(None, 'lat', 'lon')
All inputs are finite; a program needn't handle non-finite values. No bound on the sum of `sea_mask` on one device may be relied on, other than what follows from the above.
Results may differ from a plain program's by a relative error of at most 0.0003.
Values sent between devices are 32-bit elements; how exact they have to be, the bound alone decides.
No kernel may reach another device: no remote copies, remote signals or barrier semaphores. Data moves between devices by JAX's collectives and lax.ppermute only.
A program may use at most 64 MiB of HBM per device.

v0:
```python
import jax
import jax.numpy as jnp
from jax import lax
from jax.sharding import PartitionSpec as P


def padded(array, sides, width):
    for axis, dim in sides:
        peers, length = (lax.axis_size(axis), array.shape[dim])
        up = [(i, (i + 1) % peers) for i in range(peers)]
        down = [(j, i) for i, j in up]
        last = lax.slice_in_dim(array, length - width, length, axis=dim)
        leading = lax.slice_in_dim(array, 0, width, axis=dim)
        before = lax.ppermute(last, axis, up)
        after = lax.ppermute(leading, axis, down)
        array = jnp.concatenate([before, array, after], axis=dim)
    return array


def earlier(values, stride, axis):
    length = values.shape[axis]
    padding = jnp.zeros_like(lax.slice_in_dim(values, 0, stride, axis=axis))
    return jnp.concatenate([padding, lax.slice_in_dim(values, 0, length - stride, axis=axis)], axis)


def following(values, stride, axis):
    length = values.shape[axis]
    padding = jnp.zeros_like(lax.slice_in_dim(values, 0, stride, axis=axis))
    return jnp.concatenate([lax.slice_in_dim(values, stride, length, axis=axis), padding], axis)


def local_solve(lower_band, upper_band, excess, sources, axis):
    length = lower_band.shape[axis]
    stride = 1
    while stride < length:
        inverse = 1.0 / (excess - lower_band - upper_band)
        left_weight = -lower_band * earlier(inverse, stride, axis)
        right_coefficient = -upper_band * following(inverse, stride, axis)
        new_lower = left_weight * earlier(lower_band, stride, axis)
        new_upper = right_coefficient * following(upper_band, stride, axis)
        excess = (
            excess
            + left_weight * earlier(excess, stride, axis)
            + right_coefficient * following(excess, stride, axis)
        )
        sources = (
            sources
            + left_weight * earlier(sources, stride, axis + 1)
            + right_coefficient * following(sources, stride, axis + 1)
        )
        lower_band, upper_band = (new_lower, new_upper)
        stride = stride * 2
    return sources / (excess - lower_band - upper_band)


def reduced_from(own_terms, next_terms):
    coupling, own_source, own_excess, upper_end = own_terms
    next_particular, next_right, next_deficit = next_terms
    return (
        coupling,
        upper_end * next_right,
        own_excess - upper_end * next_deficit,
        own_source - upper_end * next_particular,
    )


def parallel_cyclic_reduction_update(tridiagonal_system, leading_terms, trailing_terms):
    lower_band, upper_band, excess, sources = tridiagonal_system
    lower_b, upper_b, excess_b, source_b = leading_terms
    lower_a, upper_a, excess_a, source_a = trailing_terms
    left_weight = -lower_band / (excess_b - lower_b - upper_b)
    right_coefficient = -upper_band / (excess_a - lower_a - upper_a)
    return (
        left_weight * lower_b,
        right_coefficient * upper_a,
        excess + left_weight * excess_b + right_coefficient * excess_a,
        sources + left_weight * source_b + right_coefficient * source_a,
    )


def circular_solve(tridiagonal_system):
    devices = tridiagonal_system[0].shape[0]
    stride = 1
    while stride < devices:
        leading_terms = tuple(
            (jnp.roll(ensemble_member, stride, 0) for ensemble_member in tridiagonal_system)
        )
        trailing_terms = tuple(
            (jnp.roll(ensemble_member, -stride, 0) for ensemble_member in tridiagonal_system)
        )
        tridiagonal_system = parallel_cyclic_reduction_update(
            tridiagonal_system, leading_terms, trailing_terms
        )
        stride = stride * 2
    return tridiagonal_system[3] / tridiagonal_system[2]


def gathered_solve(gathered, device_index):
    own_terms = gathered[:4]
    next_terms = tuple((jnp.roll(ensemble_member, -1, 0) for ensemble_member in gathered[4:]))
    interface = circular_solve(reduced_from(own_terms, next_terms))
    devices = interface.shape[0]
    here_value = lax.dynamic_index_in_dim(interface, device_index, 0, keepdims=False)
    before_value = lax.dynamic_index_in_dim(
        interface, (device_index + devices - 1) % devices, 0, keepdims=False
    )
    return (before_value, here_value)


def lon_gathered(own_terms, head_terms):
    gathered = (
        lax.all_gather(own_terms[0][None], "lon", axis=0, tiled=True),
        lax.all_gather(own_terms[1][None], "lon", axis=0, tiled=True),
        lax.all_gather(own_terms[2][None], "lon", axis=0, tiled=True),
        lax.all_gather(own_terms[3][None], "lon", axis=0, tiled=True),
        lax.all_gather(head_terms[0][None], "lon", axis=0, tiled=True),
        lax.all_gather(head_terms[1][None], "lon", axis=0, tiled=True),
        lax.all_gather(head_terms[2][None], "lon", axis=0, tiled=True),
    )
    return gathered_solve(gathered, lax.axis_index("lon"))


def lat_gathered(own_terms, head_terms):
    gathered = (
        lax.all_gather(own_terms[0][None], "lat", axis=0, tiled=True),
        lax.all_gather(own_terms[1][None], "lat", axis=0, tiled=True),
        lax.all_gather(own_terms[2][None], "lat", axis=0, tiled=True),
        lax.all_gather(own_terms[3][None], "lat", axis=0, tiled=True),
        lax.all_gather(head_terms[0][None], "lat", axis=0, tiled=True),
        lax.all_gather(head_terms[1][None], "lat", axis=0, tiled=True),
        lax.all_gather(head_terms[2][None], "lat", axis=0, tiled=True),
    )
    return gathered_solve(gathered, lax.axis_index("lat"))


def line_pass(values, left_face, right_face, axis, reduce_edges):
    length = values.shape[axis]
    position = lax.broadcasted_iota(jnp.int32, values.shape, axis)
    is_first = position == 0
    is_last = position == length - 1
    is_penult = position == length - 2
    lower_band = jnp.where(is_first | is_last, 0.0, -left_face)
    upper_band = jnp.where(is_penult | is_last, 0.0, -right_face)
    excess = 1.0 + jnp.where(is_first, left_face, 0.0) + jnp.where(is_penult, right_face, 0.0)
    sources = jnp.stack(
        [
            jnp.where(is_last, 0.0, values),
            jnp.where(is_first, left_face, 0.0),
            jnp.where(is_penult, right_face, 0.0) + jnp.where(is_last, 1.0, 0.0),
            jnp.where(is_last, 0.0, 1.0),
        ],
        0,
    )
    solved = local_solve(lower_band, upper_band, excess, sources, axis)
    particular, from_left, right_contribution, deficit = (
        solved[0],
        solved[1],
        solved[2],
        solved[3],
    )

    def row_at(ensemble_member, place):
        return lax.index_in_dim(ensemble_member, place, axis, keepdims=False)

    lower_end = -row_at(left_face, length - 1)
    upper_end = -row_at(right_face, length - 1)
    own_terms = (
        lower_end * row_at(from_left, length - 2),
        row_at(values, length - 1) - lower_end * row_at(particular, length - 2),
        1.0 - lower_end * row_at(deficit, length - 2),
        upper_end,
    )
    head_terms = (row_at(particular, 0), row_at(right_contribution, 0), row_at(deficit, 0))
    before_value, here_value = reduce_edges(own_terms, head_terms)
    return (
        particular
        + from_left * jnp.expand_dims(before_value, axis)
        + right_contribution * jnp.expand_dims(here_value, axis)
    )


def shards(source, kappa_lon, kappa_lat, sea_mask):
    wet_cells = sea_mask.astype(jnp.float32)
    lon_kappa = kappa_lon.astype(jnp.float32)
    lat_kappa = kappa_lat.astype(jnp.float32)
    wet_pad, lon_pad, lat_pad = (
        padded(wet_cells, (("lat", 1), ("lon", 2)), 1),
        padded(lon_kappa, (("lat", 1), ("lon", 2)), 1),
        padded(lat_kappa, (("lat", 1), ("lon", 2)), 1),
    )
    lon_wet = wet_pad[:, 1:-1, :]
    lon_faces = lon_pad[:, 1:-1, :-1] * lon_wet[:, :, :-1] * lon_wet[:, :, 1:]
    lon_pass = line_pass(source, lon_faces[:, :, :-1], lon_faces[:, :, 1:], 2, lon_gathered)
    lat_wet = wet_pad[:, :, 1:-1]
    lat_faces = lat_pad[:, :-1, 1:-1] * lat_wet[:, :-1, :] * lat_wet[:, 1:, :]
    device_index = lax.axis_index("lat")
    devices = lax.axis_size("lat")
    position = lax.broadcasted_iota(jnp.int32, lat_faces.shape, 1)
    outer_face = (position == 0) & (device_index == 0) | (position == lat_faces.shape[1] - 1) & (
        device_index == devices - 1
    )
    lat_faces = jnp.where(outer_face, 0.0, lat_faces)
    lat_pass = line_pass(lon_pass, lat_faces[:, :-1, :], lat_faces[:, 1:, :], 1, lat_gathered)
    return wet_cells * 4.0 * jnp.sqrt(jnp.sqrt(lon_kappa * lat_kappa)) * lat_pass


def solution(mesh):
    return jax.shard_map(
        shards,
        mesh=mesh,
        in_specs=(
            P(None, "lat", "lon"),
            P(None, "lat", "lon"),
            P(None, "lat", "lon"),
            P(None, "lat", "lon"),
        ),
        out_specs=P(None, "lat", "lon"),
        check_vma=False,
    )
```

profile of v0, /device:TPU:1, one launch (start us, length us, event | category | flops | bytes accessed | tf_op | source)
XLA Modules:
  0.0 489.6 jit_solution(17990874060258347863)
XLA Ops:
  0.0 0.9 copy_convert_fusion.1
  0.9 3.0 collective-permute-start.7
  3.9 1.0 copy_convert_fusion
  4.9 3.8 collective-permute-start.4
  8.8 0.9 copy_convert_fusion.2
  9.7 3.6 collective-permute-start.1
  13.3 0.6 broadcast_select_fusion
  13.9 0.5 iota_compare_fusion.5
  14.4 1.0 fusion.143
  15.6 6.8 %collective-permute-start.6 = (f32[8,34,1]{2,0,1:T(8,128)S(1)}, f32[8,34,1]{2,0,1:T(8,128)S(1)}, u32[]{:S(2)}, u32[]{:S(2)}) collective-permute-start(f32[8,34,1]{2,0,1:T(8,128)S(1)} %get-tuple-element.145), channel_id=1, source_target_pairs={{1,0},{2,1},{3,2},{4,3},{5,4},{6,5},{7,6},{8,7},{9,8},{10,9},{11,1... | collective-permute-start | bytes 3272 | tf_op jit(solution)/shard_map/ppermute | solution.py:15
  22.5 1.9 collective-permute-start.5
  24.5 1.9 collective-permute-start.2
  26.6 0.2 subtract_divide_fusion.4
  26.9 0.8 subtract_divide_fusion.3
  27.8 0.8 subtract_divide_fusion.2
  28.7 0.8 subtract_divide_fusion.1
  29.5 0.8 subtract_divide_fusion
  30.4 0.8 multiply_subtract_fusion
  31.1 0.8 collective-permute-done.5
  32.0 3.5 collective-permute-done.2
  36.5 0.2 multiply_add_fusion.9
  42.4 0.9 fusion.4
  43.3 26.5 %all-gather.5 = f32[128,32,1]{2,0,1:T(8,128)S(1)} all-gather(f32[8,32,1]{2,0,1:T(8,128)S(1)} %get-tuple-element.263), channel_id=7, replica_groups=mesh['lat'=32,'lon'=16] {'lon'}, dimensions={0}, use_global_device_ids=true | all-gather | bytes 17408 | tf_op jit(solution)/shard_map/all_gather | solution.py:118
  69.8 1.4 copy-done
  71.2 24.5 %all-gather.6 = f32[128,32,1]{2,0,1:T(8,128)S(1)} all-gather(f32[8,32,1]{2,0,1:T(8,128)S(1)} %bitcast.109), channel_id=8, replica_groups=mesh['lat'=32,'lon'=16] {'lon'}, dimensions={0}, use_global_device_ids=true | all-gather | bytes 17408 | tf_op jit(solution)/shard_map/all_gather | solution.py:117
  95.7 1.4 copy-done.1
  97.0 23.1 %all-gather.2 = f32[128,32,1]{2,0,1:T(8,128)S(1)} all-gather(f32[8,32,1]{2,0,1:T(8,128)S(1)} %get-tuple-element.153), channel_id=4, replica_groups=mesh['lat'=32,'lon'=16] {'lon'}, dimensions={0}, use_global_device_ids=true | all-gather | bytes 17408 | tf_op jit(solution)/shard_map/all_gather | solution.py:116
  120.1 0.7 slice.1271
  120.8 1.5 slice.1270
  122.4 0.6 slice-done.1
  123.0 1.4 copy.166
  124.4 22.4 %all-gather.4 = f32[128,32,1]{2,0,1:T(8,128)S(1)} all-gather(f32[8,32,1]{2,0,1:T(8,128)S(1)} %get-tuple-element.140), channel_id=6, replica_groups=mesh['lat'=32,'lon'=16] {'lon'}, dimensions={0}, use_global_device_ids=true | all-gather | bytes 17408 | tf_op jit(solution)/shard_map/all_gather | solution.py:114
  146.9 1.1 copy.165
  148.0 25.6 %all-gather.1 = f32[128,32,1]{2,0,1:T(8,128)} all-gather(f32[8,32,1]{2,0,1:T(8,128)S(1)} %get-tuple-element.142), channel_id=3, replica_groups=mesh['lat'=32,'lon'=16] {'lon'}, dimensions={0}, use_global_device_ids=true | all-gather | bytes 17408 | tf_op jit(solution)/shard_map/all_gather | solution.py:115
  173.7 2.6 copy.161
  176.4 1.4 copy.170
  178.0 2.9 copy.162
  180.9 24.8 %all-gather = f32[128,32,1]{2,0,1:T(8,128)S(1)} all-gather(f32[8,32,1]{2,0,1:T(8,128)S(1)} %get-tuple-element.143), channel_id=2, replica_groups=mesh['lat'=32,'lon'=16] {'lon'}, dimensions={0}, use_global_device_ids=true | all-gather | bytes 17408 | tf_op jit(solution)/shard_map/all_gather | solution.py:113
  205.8 1.1 copy.160
  206.9 0.9 fusion.40
  207.9 0.7 fusion.184
  208.5 0.6 fusion.182
  209.2 0.6 fusion.183
  209.7 29.7 %all-gather.3 = f32[128,32,1]{2,0,1:T(8,128)S(1)} all-gather(f32[8,32,1]{2,0,1:T(8,128)} %get-tuple-element.141), channel_id=5, replica_groups=mesh['lat'=32,'lon'=16] {'lon'}, dimensions={0}, use_global_device_ids=true | all-gather | bytes 17408 | tf_op jit(solution)/shard_map/all_gather | solution.py:112
  239.4 2.2 fusion.84
  241.6 0.7 fusion.85
  242.3 0.6 fusion.180
  243.1 2.3 copy.169
  245.4 1.0 copy.168
  246.5 1.7 copy.164
  248.2 1.1 copy.173
  249.3 2.3 copy.172
  253.5 0.7 copy-done.13
  254.7 0.7 copy-done.7
  255.8 0.8 fusion.63
  256.6 61.3 %all-gather.12 = f32[256,1,128]{2,0,1:T(8,128)S(1)} all-gather(f32[8,1,128]{2,0,1:T(8,128)S(1)} %get-tuple-element.238), channel_id=14, replica_groups=mesh['lat'=32,'lon'=16] {'lat'}, dimensions={0}, use_global_device_ids=true | all-gather | bytes 135168 | tf_op jit(solution)/shard_map/all_gather | solution.py:131
  317.9 27.5 %all-gather.13 = f32[256,1,128]{2,0,1:T(8,128)S(1)} all-gather(f32[8,1,128]{2,0,1:T(8,128)S(1)} %slice.1405), channel_id=15, replica_groups=mesh['lat'=32,'lon'=16] {'lat'}, dimensions={0}, use_global_device_ids=true | all-gather | bytes 135168 | tf_op jit(solution)/shard_map/all_gather | solution.py:130
  345.4 28.8 %all-gather.9 = f32[256,1,128]{2,0,1:T(8,128)S(1)} all-gather(f32[8,1,128]{2,0,1:T(8,128)S(1)} %get-tuple-element.152), channel_id=11, replica_groups=mesh['lat'=32,'lon'=16] {'lat'}, dimensions={0}, use_global_device_ids=true | all-gather | bytes 135168 | tf_op jit(solution)/shard_map/all_gather | solution.py:129
  374.2 27.5 %all-gather.11 = f32[256,1,128]{2,0,1:T(8,128)S(1)} all-gather(f32[8,1,128]{2,0,1:T(8,128)S(1)} %get-tuple-element.148), channel_id=13, replica_groups=mesh['lat'=32,'lon'=16] {'lat'}, dimensions={0}, use_global_device_ids=true | all-gather | bytes 135168 | tf_op jit(solution)/shard_map/all_gather | solution.py:127
  401.6 28.8 %all-gather.8 = f32[256,1,128]{2,0,1:T(8,128)S(1)} all-gather(f32[8,1,128]{2,0,1:T(8,128)S(1)} %get-tuple-element.150), channel_id=10, replica_groups=mesh['lat'=32,'lon'=16] {'lat'}, dimensions={0}, use_global_device_ids=true | all-gather | bytes 135168 | tf_op jit(solution)/shard_map/all_gather | solution.py:128
  430.4 27.4 %all-gather.7 = f32[256,1,128]{2,0,1:T(8,128)S(1)} all-gather(f32[8,1,128]{2,0,1:T(8,128)S(1)} %get-tuple-element.151), channel_id=9, replica_groups=mesh['lat'=32,'lon'=16] {'lat'}, dimensions={0}, use_global_device_ids=true | all-gather | bytes 135168 | tf_op jit(solution)/shard_map/all_gather | solution.py:126
  457.9 28.8 %all-gather.10 = f32[256,1,128]{2,0,1:T(8,128)S(1)} all-gather(f32[8,1,128]{2,0,1:T(8,128)S(1)} %get-tuple-element.149), channel_id=12, replica_groups=mesh['lat'=32,'lon'=16] {'lat'}, dimensions={0}, use_global_device_ids=true | all-gather | bytes 135168 | tf_op jit(solution)/shard_map/all_gather | solution.py:125
  488.2 0.6 copy-done.9
  488.9 0.7 copy.178
  (255 shorter events, 11.4 us)
Async XLA Ops:
  0.9 25.6 %collective-permute-start.7 = (f32[8,1,128]{2,0,1:T(8,128)S(1)}, f32[8,1,128]{2,0,1:T(8,128)S(1)}, u32[]{:S(2)}, u32[]{:S(2)}) collective-permute-start(f32[8,1,128]{2,0,1:T(8,128)S(1)} %slice.1338), channel_id=1, source_target_pairs={{0,16},{16,32},{32,48},{48,64},{64,80},{80,96},{96,112},{112,128},... | collective-permute-start | bytes 12296 | tf_op jit(solution)/shard_map/ppermute | solution.py:14
  4.9 10.6 %collective-permute-start.3 = (f32[8,1,128]{2,0,1:T(8,128)S(1)}, f32[8,1,128]{2,0,1:T(8,128)S(1)}, u32[]{:S(2)}, u32[]{:S(2)}) collective-permute-start(f32[8,1,128]{2,0,1:T(8,128)S(1)} %get-tuple-element.297), channel_id=1, source_target_pairs={{0,16},{16,32},{32,48},{48,64},{64,80},{80,96},{96,112},{112,128},... | collective-permute-start | bytes 12296 | tf_op jit(solution)/shard_map/ppermute | solution.py:14
  4.9 10.6 %collective-permute-start.4 = (f32[8,1,128]{2,0,1:T(8,128)S(1)}, f32[8,1,128]{2,0,1:T(8,128)S(1)}, u32[]{:S(2)}, u32[]{:S(2)}) collective-permute-start(f32[8,1,128]{2,0,1:T(8,128)S(1)} %get-tuple-element.296), channel_id=1, source_target_pairs={{16,0},{32,16},{48,32},{64,48},{80,64},{96,80},{112,96},{128,112},... | collective-permute-start | bytes 12296 | tf_op jit(solution)/shard_map/ppermute | solution.py:15
  9.7 14.7 %collective-permute-start.1 = (f32[8,1,128]{2,0,1:T(8,128)S(1)}, f32[8,1,128]{2,0,1:T(8,128)S(1)}, u32[]{:S(2)}, u32[]{:S(2)}) collective-permute-start(f32[8,1,128]{2,0,1:T(8,128)S(1)} %get-tuple-element.295), channel_id=1, source_target_pairs={{16,0},{32,16},{48,32},{64,48},{80,64},{96,80},{112,96},{128,112},... | collective-permute-start | bytes 12296 | tf_op jit(solution)/shard_map/ppermute | solution.py:15
  13.3 11.2 %collective-permute-start = (f32[8,1,128]{2,0,1:T(8,128)S(1)}, f32[8,1,128]{2,0,1:T(8,128)S(1)}, u32[]{:S(2)}, u32[]{:S(2)}) collective-permute-start(f32[8,1,128]{2,0,1:T(8,128)S(1)} %get-tuple-element.294), channel_id=1, source_target_pairs={{0,16},{16,32},{32,48},{48,64},{64,80},{80,96},{96,112},{112,128},... | collective-permute-start | bytes 12296 | tf_op jit(solution)/shard_map/ppermute | solution.py:14
  15.6 15.5 %collective-permute-start.6 = (f32[8,34,1]{2,0,1:T(8,128)S(1)}, f32[8,34,1]{2,0,1:T(8,128)S(1)}, u32[]{:S(2)}, u32[]{:S(2)}) collective-permute-start(f32[8,34,1]{2,0,1:T(8,128)S(1)} %get-tuple-element.145), channel_id=1, source_target_pairs={{1,0},{2,1},{3,2},{4,3},{5,4},{6,5},{7,6},{8,7},{9,8},{10,9},{11,1... | collective-permute-start | bytes 3272 | tf_op jit(solution)/shard_map/ppermute | solution.py:15
  22.5 9.5 %collective-permute-start.5 = (f32[8,34,1]{2,0,1:T(8,128)S(1)}, f32[8,34,1]{2,0,1:T(8,128)S(1)}, u32[]{:S(2)}, u32[]{:S(2)}) collective-permute-start(f32[8,34,1]{2,0,1:T(8,128)S(1)} %get-tuple-element.144), channel_id=1, source_target_pairs={{0,1},{1,2},{2,3},{3,4},{4,5},{5,6},{6,7},{7,8},{8,9},{9,10},{10,1... | collective-permute-start | bytes 3272 | tf_op jit(solution)/shard_map/ppermute | solution.py:14
  24.5 10.9 %collective-permute-start.2 = (f32[8,34,1]{2,0,1:T(8,128)S(1)}, f32[8,34,1]{2,0,1:T(8,128)S(1)}, u32[]{:S(2)}, u32[]{:S(2)}) collective-permute-start(f32[8,34,1]{2,0,1:T(8,128)S(1)} %pad_maximum_fusion.11), channel_id=1, source_target_pairs={{0,1},{1,2},{2,3},{3,4},{4,5},{5,6},{6,7},{7,8},{8,9},{9,10},{10,1... | collective-permute-start | bytes 3272 | tf_op jit(solution)/shard_map/ppermute | solution.py:14
  42.3 0.9 copy-start.3
  42.4 28.8 %copy-start.4 = (f32[8,32,128]{2,0,1:T(8,128)}, f32[8,32,128]{2,0,1:T(8,128)S(1)}, u32[]{:S(2)}) copy-start(f32[8,32,128]{2,0,1:T(8,128)S(1)} %get-tuple-element.121) | copy-start | bytes 393220
  69.8 1.4 copy-start
  95.7 1.4 copy-start.1
  120.1 2.2 slice-start
  120.8 2.3 slice-start.1
  148.0 28.3 %slice-start.2 = ((f32[128,32,1]{2,0,1:T(8,128)}), f32[8,32,1]{2,0,1:T(8,128)S(1)}, s32[]{:S(2)}) async-start(f32[128,32,1]{2,0,1:T(8,128)} %copy-done.1), calls=%async_computation.2 | async-start | bytes 262144 | tf_op jit(solution)/shard_map/jit(_roll_static)/slice | solution.py:100
  148.0 28.4 %slice-start.3 = ((f32[128,32,1]{2,0,1:T(8,128)}), f32[120,32,1]{2,0,1:T(8,128)S(1)}, s32[]{:S(2)}) async-start(f32[128,32,1]{2,0,1:T(8,128)} %copy-done.1), calls=%async_computation.3 | async-start | bytes 3932160 | tf_op jit(solution)/shard_map/jit(_roll_static)/slice | solution.py:100
  173.7 4.2 copy-start.10
  248.2 3.4 copy-start.2
  248.2 3.4 copy-start.18
  248.2 3.4 copy-start.21
  248.2 3.4 copy-start.22
  248.2 3.4 copy-start.23
  248.2 3.4 copy-start.24
  252.0 0.6 copy-start.26
  252.1 0.8 copy-start.25
  252.3 0.9 copy-start.11
  252.4 1.0 copy-start.12
  253.3 0.9 copy-start.13
  253.3 1.0 copy-start.14
  253.5 1.0 copy-start.5
  253.5 1.0 copy-start.6
  254.4 0.9 copy-start.7
  254.5 1.0 copy-start.8
  254.6 1.0 copy-start.15
  254.6 1.0 copy-start.16
  254.6 1.0 copy-start.17
  487.8 0.9 copy-start.9
  487.8 0.9 copy-start.19
  487.8 0.9 copy-start.20
where the time goes:
time: 490 us
  blocking collectives  407 us (83%)
  local copies, waits for them, and re-layouts  38.8 us (8%)
  starting transfers between devices  21.2 us (4%)
  other arithmetic  17.1 us (3%)
    all_gather x1, blocking collectives, lat_gathered(): lax.all_gather(head_terms[2][None], 'lat', axis=0, tiled=True)  61.3 us
    all_gather x1, blocking collectives, lon_gathered(): lax.all_gather(own_terms[0][None], 'lon', axis=0, tiled=True)  29.7 us
    all_gather x1, blocking collectives, lat_gathered(): lax.all_gather(head_terms[0][None], 'lat', axis=0, tiled=True)  28.8 us
    all_gather x1, blocking collectives, lat_gathered(): lax.all_gather(own_terms[0][None], 'lat', axis=0, tiled=True)  28.8 us
    all_gather x1, blocking collectives, lat_gathered(): lax.all_gather(own_terms[3][None], 'lat', axis=0, tiled=True)  28.8 us
    all_gather x1, blocking collectives, lat_gathered(): lax.all_gather(own_terms[2][None], 'lat', axis=0, tiled=True)  27.5 us
    all_gather x1, blocking collectives, lat_gathered(): lax.all_gather(head_terms[1][None], 'lat', axis=0, tiled=True)  27.5 us
    all_gather x1, blocking collectives, lat_gathered(): lax.all_gather(own_terms[1][None], 'lat', axis=0, tiled=True)  27.4 us
  transfers between devices with their start and end apart: 8, of which 2 were waited for; matrix products, arithmetic and copies ran while one was open for 2% of the time, Pallas kernels for 0%

commit v1 on v0

--- a/solution.py
+++ b/solution.py
@@ -107,30 +107,19 @@
     return (before_value, here_value)
 
 
+def axis_gathered(own_terms, head_terms, axis):
+    stacked = jnp.stack(tuple(own_terms) + tuple(head_terms), 0)
+    gathered = lax.all_gather(stacked[None], axis, axis=0, tiled=True)
+    gathered = tuple(gathered[:, k] for k in range(stacked.shape[0]))
+    return gathered_solve(gathered, lax.axis_index(axis))
+
+
 def lon_gathered(own_terms, head_terms):
-    gathered = (
-        lax.all_gather(own_terms[0][None], "lon", axis=0, tiled=True),
-        lax.all_gather(own_terms[1][None], "lon", axis=0, tiled=True),
-        lax.all_gather(own_terms[2][None], "lon", axis=0, tiled=True),
-        lax.all_gather(own_terms[3][None], "lon", axis=0, tiled=True),
-        lax.all_gather(head_terms[0][None], "lon", axis=0, tiled=True),
-        lax.all_gather(head_terms[1][None], "lon", axis=0, tiled=True),
-        lax.all_gather(head_terms[2][None], "lon", axis=0, tiled=True),
-    )
-    return gathered_solve(gathered, lax.axis_index("lon"))
+    return axis_gathered(own_terms, head_terms, "lon")
 
 
 def lat_gathered(own_terms, head_terms):
-    gathered = (
-        lax.all_gather(own_terms[0][None], "lat", axis=0, tiled=True),
-        lax.all_gather(own_terms[1][None], "lat", axis=0, tiled=True),
-        lax.all_gather(own_terms[2][None], "lat", axis=0, tiled=True),
-        lax.all_gather(own_terms[3][None], "lat", axis=0, tiled=True),
-        lax.all_gather(head_terms[0][None], "lat", axis=0, tiled=True),
-        lax.all_gather(head_terms[1][None], "lat", axis=0, tiled=True),
-        lax.all_gather(head_terms[2][None], "lat", axis=0, tiled=True),
-    )
-    return gathered_solve(gathered, lax.axis_index("lat"))
+    return axis_gathered(own_terms, head_terms, "lat")
 
 
 def line_pass(values, left_face, right_face, axis, reduce_edges):

time: 490 us -> 104 us (0.21)
  blocking collectives: 407 us -> 54.9 us
  local copies, waits for them, and re-layouts: 38.8 us -> 8.92 us
  other arithmetic: 17.1 us -> 9.97 us
    all_gather x14 -> x2, blocking collectives: 407 us -> 54.9 us  [axis_gathered(): gathered = lax.all_gather(stacked[None], axis, axis=0, tiled=True)]
    slice x22 -> x0, local copies, waits for them, and re-layouts: 8.99 us -> none  [gathered_solve(): jnp.roll(ensemble_member, -1, 0)]
    slice x40 -> x38, local copies, waits for them, and re-layouts: 9.13 us -> 0.35 us  [circular_solve(): jnp.roll(ensemble_member, -stride, 0)]
    all_gather x3 -> x0, local copies, waits for them, and re-layouts: 4.93 us -> none  [the longest x1 2.63 us: lon_gathered(): lax.all_gather(own_terms[3][None], 'lon', axis=0, tiled=True)]
  transfers between devices with their start and end apart: 8 -> 8, of which waited for: 2 -> 2; matrix products, arithmetic and copies ran while one was open for 2% -> 4% of each run, Pallas kernels for 0% -> 0%
where the time goes in v1:
time: 104 us
  blocking collectives  54.9 us (53%)
  starting transfers between devices  21.2 us (20%)
  other arithmetic  9.97 us (10%)
  local copies, waits for them, and re-layouts  8.92 us (9%)
  waiting for transfers between devices  7.07 us (7%)
  between operations  1.52 us (1%)
    all_gather x2, blocking collectives, axis_gathered(): gathered = lax.all_gather(stacked[None], axis, axis=0, tiled=True)  54.9 us
    ppermute x3, starting transfers between devices, padded(): after = lax.ppermute(leading, axis, down)  14.3 us
    ppermute x5, waiting for transfers between devices, padded(): before = lax.ppermute(last, axis, up)  7.06 us
    ppermute x5, starting transfers between devices, padded(): before = lax.ppermute(last, axis, up)  6.91 us
    slice x29, local copies, waits for them, and re-layouts, earlier(): lax.slice_in_dim(values, 0, length - stride, axis=axis)  2.49 us
    unnamed x32, local copies, waits for them, and re-layouts  2.28 us
  transfers between devices with their start and end apart: 8, of which 2 were waited for; matrix products, arithmetic and copies ran while one was open for 4% of the time, Pallas kernels for 0%

profile of v1, /device:TPU:1, one launch (start us, length us, event | category | flops | bytes accessed | tf_op | source)
XLA Modules:
  0.0 103.6 jit_solution(15214035839957971282)
XLA Ops:
  0.0 0.9 copy_convert_fusion.1
  0.9 3.0 %collective-permute-start.7 = (f32[8,1,128]{2,0,1:T(8,128)S(1)}, f32[8,1,128]{2,0,1:T(8,128)S(1)}, u32[]{:S(2)}, u32[]{:S(2)}) collective-permute-start(f32[8,1,128]{2,0,1:T(8,128)S(1)} %slice.1460), channel_id=1, source_target_pairs={{0,16},{16,32},{32,48},{48,64},{64,80},{80,96},{96,112},{112,128},... | collective-permute-start | bytes 12296 | tf_op jit(solution)/shard_map/ppermute | solution.py:14
  4.1 3.8 %collective-permute-start.4 = (f32[8,1,128]{2,0,1:T(8,128)S(1)}, f32[8,1,128]{2,0,1:T(8,128)S(1)}, u32[]{:S(2)}, u32[]{:S(2)}) collective-permute-start(f32[8,1,128]{2,0,1:T(8,128)S(1)} %get-tuple-element.305), channel_id=1, source_target_pairs={{16,0},{32,16},{48,32},{64,48},{80,64},{96,80},{112,96},{128,112},... | collective-permute-start | bytes 12296 | tf_op jit(solution)/shard_map/ppermute | solution.py:15
  8.0 3.6 %collective-permute-start.1 = (f32[8,1,128]{2,0,1:T(8,128)S(1)}, f32[8,1,128]{2,0,1:T(8,128)S(1)}, u32[]{:S(2)}, u32[]{:S(2)}) collective-permute-start(f32[8,1,128]{2,0,1:T(8,128)S(1)} %get-tuple-element.304), channel_id=1, source_target_pairs={{16,0},{32,16},{48,32},{64,48},{80,64},{96,80},{112,96},{128,112},... | collective-permute-start | bytes 12296 | tf_op jit(solution)/shard_map/ppermute | solution.py:15
  11.6 0.5 iota_compare_fusion.3
  12.2 0.6 iota_compare_fusion.2
  12.7 0.5 broadcast_select_fusion.3
  13.6 6.8 %collective-permute-start.6 = (f32[8,34,1]{2,0,1:T(8,128)S(1)}, f32[8,34,1]{2,0,1:T(8,128)S(1)}, u32[]{:S(2)}, u32[]{:S(2)}) collective-permute-start(f32[8,34,1]{2,0,1:T(8,128)S(1)} %get-tuple-element.167), channel_id=1, source_target_pairs={{1,0},{2,1},{3,2},{4,3},{5,4},{6,5},{7,6},{8,7},{9,8},{10,9},{11,1... | collective-permute-start | bytes 3272 | tf_op jit(solution)/shard_map/ppermute | solution.py:15
  20.4 1.9 %collective-permute-start.5 = (f32[8,34,1]{2,0,1:T(8,128)S(1)}, f32[8,34,1]{2,0,1:T(8,128)S(1)}, u32[]{:S(2)}, u32[]{:S(2)}) collective-permute-start(f32[8,34,1]{2,0,1:T(8,128)S(1)} %get-tuple-element.166), channel_id=1, source_target_pairs={{0,1},{1,2},{2,3},{3,4},{4,5},{5,6},{6,7},{7,8},{8,9},{9,10},{10,1... | collective-permute-start | bytes 3272 | tf_op jit(solution)/shard_map/ppermute | solution.py:14
  22.5 1.9 %collective-permute-start.2 = (f32[8,34,1]{2,0,1:T(8,128)S(1)}, f32[8,34,1]{2,0,1:T(8,128)S(1)}, u32[]{:S(2)}, u32[]{:S(2)}) collective-permute-start(f32[8,34,1]{2,0,1:T(8,128)S(1)} %pad_maximum_fusion.11), channel_id=1, source_target_pairs={{0,1},{1,2},{2,3},{3,4},{4,5},{5,6},{6,7},{7,8},{8,9},{9,10},{10,1... | collective-permute-start | bytes 3272 | tf_op jit(solution)/shard_map/ppermute | solution.py:14
  24.4 0.1 fusion.3
  24.5 0.2 subtract_divide_fusion.4
  24.8 0.1 subtract_divide_fusion.3
  25.0 0.1 subtract_divide_fusion.2
  25.5 0.8 multiply_subtract_fusion
  26.3 3.6 %collective-permute-done.5 = f32[8,34,1]{2,0,1:T(8,128)S(1)} collective-permute-done((f32[8,34,1]{2,0,1:T(8,128)S(1)}, f32[8,34,1]{2,0,1:T(8,128)S(1)}, u32[]{:S(2)}, u32[]{:S(2)}) %collective-permute-start.5) | collective-permute-done | bytes 1120 | tf_op jit(solution)/shard_map/ppermute | solution.py:14
  29.9 3.5 %collective-permute-done.2 = f32[8,34,1]{2,0,1:T(8,128)S(1)} collective-permute-done((f32[8,34,1]{2,0,1:T(8,128)S(1)}, f32[8,34,1]{2,0,1:T(8,128)S(1)}, u32[]{:S(2)}, u32[]{:S(2)}) %collective-permute-start.2) | collective-permute-done | bytes 1120 | tf_op jit(solution)/shard_map/ppermute | solution.py:14
  33.4 0.2 fusion
  33.6 0.4 copy-done.10
  34.0 0.1 copy-done.7
  34.2 0.1 subtract_divide_fusion.11
  34.4 0.2 fusion.103
  34.9 0.2 subtract_divide_fusion.10
  35.1 0.2 multiply_add_fusion.9
  35.3 0.2 fusion.102
  35.8 0.2 subtract_divide_fusion.9
  36.0 0.2 multiply_add_fusion.8
  36.2 0.2 fusion.101
  36.5 0.1 slice.1348
  36.8 0.2 subtract_divide_fusion.8
  37.0 0.2 multiply_add_fusion.7
  37.2 0.2 fusion.100
  37.7 0.2 subtract_divide_fusion.7
  37.9 0.2 multiply_add_fusion.6
  38.1 0.2 fusion.99
  38.4 0.1 slice.1364
  38.6 0.2 subtract_divide_fusion.6
  38.8 0.2 multiply_add_fusion.5
  39.0 0.2 fusion.98
  39.4 0.1 slice.1372
  39.6 0.2 subtract_divide_fusion.5
  39.8 0.2 multiply_add_fusion.4
  40.0 0.2 fusion.97
  40.4 0.1 fusion.150
  40.5 0.2 multiply_subtract_fusion.1
  40.7 0.2 add_divide_fusion.1
  41.0 0.2 slice_negate_fusion
  41.2 0.1 copy.860
  41.4 0.1 copy.862
  41.5 0.1 copy.863
  41.6 0.1 copy.864
  41.7 0.1 copy.865
  41.9 0.1 copy.866
  42.0 0.1 copy.867
  42.2 15.8 %all-gather = f32[112,8,32]{2,1,0:T(8,128)S(1)} all-gather(f32[7,8,32]{2,1,0:T(8,128)S(1)} %constant_dynamic-update-slice_fusion), channel_id=2, replica_groups=mesh['lat'=32,'lon'=16] {'lon'}, dimensions={0}, use_global_device_ids=true | all-gather | bytes 121856 | tf_op jit(solution)/shard_map/all_gather | solution.py:112
  59.0 0.2 add_select_fusion
  59.4 0.1 multiply_add_fusion.3
  60.1 0.8 copy-done.1
  61.3 39.2 %all-gather.1 = f32[224,8,128]{2,1,0:T(8,128)S(1)} all-gather(f32[7,8,128]{2,1,0:T(8,128)S(1)} %constant_dynamic-update-slice_fusion.7), channel_id=3, replica_groups=mesh['lat'=32,'lon'=16] {'lat'}, dimensions={0}, use_global_device_ids=true | all-gather | bytes 946176 | tf_op jit(solution)/shard_map/all_gather | solution.py:112
  100.7 0.1 fusion.12
  101.0 0.1 fusion.17
  102.0 0.7 copy-done.3
  102.7 0.2 add_multiply_fusion
  102.9 0.7 copy.887
  (201 shorter events, 5.6 us)
Async XLA Ops:
  0.0 4.0 %copy-start = (s32[8,32,128]{2,1,0:T(8,128)S(1)}, s32[8,32,128]{2,1,0:T(8,128)}, u32[]{:S(2)}) copy-start(s32[8,32,128]{2,1,0:T(8,128)} %param.7) | copy-start | bytes 393220
  0.9 7.0 %copy-start.4 = (bf16[8,32,128]{2,1,0:T(8,128)(2,1)S(1)}, bf16[8,32,128]{2,1,0:T(8,128)(2,1)}, u32[]{:S(2)}) copy-start(bf16[8,32,128]{2,1,0:T(8,128)(2,1)} %param.5) | copy-start | bytes 196612
  0.9 23.5 %collective-permute-start.7 = (f32[8,1,128]{2,0,1:T(8,128)S(1)}, f32[8,1,128]{2,0,1:T(8,128)S(1)}, u32[]{:S(2)}, u32[]{:S(2)}) collective-permute-start(f32[8,1,128]{2,0,1:T(8,128)S(1)} %slice.1460), channel_id=1, source_target_pairs={{0,16},{16,32},{32,48},{48,64},{64,80},{80,96},{96,112},{112,128},... | collective-permute-start | bytes 12296 | tf_op jit(solution)/shard_map/ppermute | solution.py:14
  4.0 9.2 %copy-start.6 = (f32[8,32,128]{2,1,0:T(8,128)S(1)}, f32[8,32,128]{2,1,0:T(8,128)}, u32[]{:S(2)}) copy-start(f32[8,32,128]{2,1,0:T(8,128)} %param.4) | copy-start | bytes 393220
  4.1 9.4 %collective-permute-start.3 = (f32[8,1,128]{2,0,1:T(8,128)S(1)}, f32[8,1,128]{2,0,1:T(8,128)S(1)}, u32[]{:S(2)}, u32[]{:S(2)}) collective-permute-start(f32[8,1,128]{2,0,1:T(8,128)S(1)} %get-tuple-element.306), channel_id=1, source_target_pairs={{0,16},{16,32},{32,48},{48,64},{64,80},{80,96},{96,112},{112,128},... | collective-permute-start | bytes 12296 | tf_op jit(solution)/shard_map/ppermute | solution.py:14
  4.1 9.3 %collective-permute-start.4 = (f32[8,1,128]{2,0,1:T(8,128)S(1)}, f32[8,1,128]{2,0,1:T(8,128)S(1)}, u32[]{:S(2)}, u32[]{:S(2)}) collective-permute-start(f32[8,1,128]{2,0,1:T(8,128)S(1)} %get-tuple-element.305), channel_id=1, source_target_pairs={{16,0},{32,16},{48,32},{64,48},{80,64},{96,80},{112,96},{128,112},... | collective-permute-start | bytes 12296 | tf_op jit(solution)/shard_map/ppermute | solution.py:15
  8.0 14.3 %collective-permute-start.1 = (f32[8,1,128]{2,0,1:T(8,128)S(1)}, f32[8,1,128]{2,0,1:T(8,128)S(1)}, u32[]{:S(2)}, u32[]{:S(2)}) collective-permute-start(f32[8,1,128]{2,0,1:T(8,128)S(1)} %get-tuple-element.304), channel_id=1, source_target_pairs={{16,0},{32,16},{48,32},{64,48},{80,64},{96,80},{112,96},{128,112},... | collective-permute-start | bytes 12296 | tf_op jit(solution)/shard_map/ppermute | solution.py:15
  11.6 10.8 %collective-permute-start = (f32[8,1,128]{2,0,1:T(8,128)S(1)}, f32[8,1,128]{2,0,1:T(8,128)S(1)}, u32[]{:S(2)}, u32[]{:S(2)}) collective-permute-start(f32[8,1,128]{2,0,1:T(8,128)S(1)} %get-tuple-element.303), channel_id=1, source_target_pairs={{0,16},{16,32},{32,48},{48,64},{64,80},{80,96},{96,112},{112,128},... | collective-permute-start | bytes 12296 | tf_op jit(solution)/shard_map/ppermute | solution.py:14
  13.6 12.7 %collective-permute-start.6 = (f32[8,34,1]{2,0,1:T(8,128)S(1)}, f32[8,34,1]{2,0,1:T(8,128)S(1)}, u32[]{:S(2)}, u32[]{:S(2)}) collective-permute-start(f32[8,34,1]{2,0,1:T(8,128)S(1)} %get-tuple-element.167), channel_id=1, source_target_pairs={{1,0},{2,1},{3,2},{4,3},{5,4},{6,5},{7,6},{8,7},{9,8},{10,9},{11,1... | collective-permute-start | bytes 3272 | tf_op jit(solution)/shard_map/ppermute | solution.py:15
  20.4 9.5 %collective-permute-start.5 = (f32[8,34,1]{2,0,1:T(8,128)S(1)}, f32[8,34,1]{2,0,1:T(8,128)S(1)}, u32[]{:S(2)}, u32[]{:S(2)}) collective-permute-start(f32[8,34,1]{2,0,1:T(8,128)S(1)} %get-tuple-element.166), channel_id=1, source_target_pairs={{0,1},{1,2},{2,3},{3,4},{4,5},{5,6},{6,7},{7,8},{8,9},{9,10},{10,1... | collective-permute-start | bytes 3272 | tf_op jit(solution)/shard_map/ppermute | solution.py:14
  22.5 10.9 %collective-permute-start.2 = (f32[8,34,1]{2,0,1:T(8,128)S(1)}, f32[8,34,1]{2,0,1:T(8,128)S(1)}, u32[]{:S(2)}, u32[]{:S(2)}) collective-permute-start(f32[8,34,1]{2,0,1:T(8,128)S(1)} %pad_maximum_fusion.11), channel_id=1, source_target_pairs={{0,1},{1,2},{2,3},{3,4},{4,5},{5,6},{6,7},{7,8},{8,9},{9,10},{10,1... | collective-permute-start | bytes 3272 | tf_op jit(solution)/shard_map/ppermute | solution.py:14
  33.4 0.7 copy-start.10
  33.4 0.7 copy-start.11
  33.6 0.6 copy-start.7
  33.6 0.6 copy-start.8
  33.6 0.6 copy-start.9
  60.0 0.9 copy-start.1
  60.0 1.0 copy-start.2
  101.9 0.8 copy-start.3
  101.9 0.9 copy-start.5

commit v2 on v1

v2 whole, which is shorter than its diff:
```python
import jax
import jax.numpy as jnp
from jax import lax
from jax.sharding import PartitionSpec as P


def earlier(values, stride, axis):
    length = values.shape[axis]
    padding = jnp.zeros_like(lax.slice_in_dim(values, 0, stride, axis=axis))
    return jnp.concatenate([padding, lax.slice_in_dim(values, 0, length - stride, axis=axis)], axis)


def following(values, stride, axis):
    length = values.shape[axis]
    padding = jnp.zeros_like(lax.slice_in_dim(values, 0, stride, axis=axis))
    return jnp.concatenate([lax.slice_in_dim(values, stride, length, axis=axis), padding], axis)


def local_solve(lower_band, upper_band, excess, sources, axis):
    length = lower_band.shape[axis]
    stride = 1
    while stride < length:
        inverse = 1.0 / (excess - lower_band - upper_band)
        left_weight = -lower_band * earlier(inverse, stride, axis)
        right_coefficient = -upper_band * following(inverse, stride, axis)
        new_lower = left_weight * earlier(lower_band, stride, axis)
        new_upper = right_coefficient * following(upper_band, stride, axis)
        excess = (
            excess
            + left_weight * earlier(excess, stride, axis)
            + right_coefficient * following(excess, stride, axis)
        )
        sources = (
            sources
            + left_weight * earlier(sources, stride, axis + 1)
            + right_coefficient * following(sources, stride, axis + 1)
        )
        lower_band, upper_band = (new_lower, new_upper)
        stride = stride * 2
    return sources / (excess - lower_band - upper_band)


def circular_solve(lower_band, upper_band, excess, sources):
    devices = lower_band.shape[0]
    stride = 1
    while stride < devices:
        inverse = 1.0 / (excess - lower_band - upper_band)
        left_weight = -lower_band * jnp.roll(inverse, stride, 0)
        right_coefficient = -upper_band * jnp.roll(inverse, -stride, 0)
        new_lower = left_weight * jnp.roll(lower_band, stride, 0)
        new_upper = right_coefficient * jnp.roll(upper_band, -stride, 0)
        excess = (
            excess
            + left_weight * jnp.roll(excess, stride, 0)
            + right_coefficient * jnp.roll(excess, -stride, 0)
        )
        sources = (
            sources
            + left_weight * jnp.roll(sources, stride, 0)
            + right_coefficient * jnp.roll(sources, -stride, 0)
        )
        lower_band, upper_band = (new_lower, new_upper)
        stride = stride * 2
    return sources / excess


def line_pass(values, faces, edge_kappa, edge_wet, axis, mesh_axis, periodic):
    length = values.shape[axis]
    position = lax.broadcasted_iota(jnp.int32, values.shape, axis)
    zero = jnp.zeros_like(lax.slice_in_dim(values, 0, 1, axis=axis))
    left_face = jnp.concatenate([zero, faces], axis)
    right_face = jnp.concatenate([faces, zero], axis)
    sources = jnp.stack(
        [
            values,
            jnp.where(position == 0, 1.0, 0.0),
            jnp.where(position == length - 1, 1.0, 0.0),
        ],
        0,
    )
    solved = local_solve(-left_face, -right_face, jnp.ones_like(values), sources, axis)
    particular, from_left, from_right = solved[0], solved[1], solved[2]

    def row_at(member, place):
        return lax.index_in_dim(member, place, axis, keepdims=False)

    terms = jnp.stack(
        [
            row_at(particular, 0),
            row_at(from_left, 0),
            row_at(from_right, 0),
            row_at(particular, length - 1),
            row_at(from_left, length - 1),
            row_at(from_right, length - 1),
            edge_kappa,
            edge_wet,
        ],
        0,
    )
    gathered = lax.all_gather(terms[None], mesh_axis, axis=0, tiled=True)
    head_p, head_u, head_w, tail_p, tail_u, tail_w, tail_kappa, head_wet = (
        gathered[:, k] for k in range(terms.shape[0])
    )
    devices = gathered.shape[0]

    def next_of(member):
        return jnp.roll(member, -1, 0)

    face = tail_kappa * next_of(head_wet)
    if not periodic:
        device = lax.broadcasted_iota(jnp.int32, face.shape, 0)
        face = jnp.where(device == devices - 1, 0.0, face)
    lower = -face * tail_u
    upper = -face * next_of(head_w)
    diagonal = 1.0 + face * (next_of(head_u) + tail_w)
    flux = circular_solve(lower, upper, diagonal + lower + upper, face * (next_of(head_p) - tail_p))
    index = lax.axis_index(mesh_axis)
    here = lax.dynamic_index_in_dim(flux, index, 0, keepdims=False)
    before = lax.dynamic_index_in_dim(flux, (index + devices - 1) % devices, 0, keepdims=False)
    return (
        particular
        - from_left * jnp.expand_dims(before, axis)
        + from_right * jnp.expand_dims(here, axis)
    )


def shards(source, kappa_lon, kappa_lat, sea_mask):
    wet_cells = sea_mask.astype(jnp.float32)
    lon_kappa = kappa_lon.astype(jnp.float32)
    lat_kappa = kappa_lat.astype(jnp.float32)
    lon_weight = lon_kappa * wet_cells
    lat_weight = lat_kappa * wet_cells
    lon_faces = lon_weight[:, :, :-1] * wet_cells[:, :, 1:]
    lon_pass = line_pass(
        source, lon_faces, lon_weight[:, :, -1], wet_cells[:, :, 0], 2, "lon", True
    )
    lat_faces = lat_weight[:, :-1, :] * wet_cells[:, 1:, :]
    lat_pass = line_pass(
        lon_pass, lat_faces, lat_weight[:, -1, :], wet_cells[:, 0, :], 1, "lat", False
    )
    return wet_cells * 4.0 * jnp.sqrt(jnp.sqrt(lon_kappa * lat_kappa)) * lat_pass


def solution(mesh):
    return jax.shard_map(
        shards,
        mesh=mesh,
        in_specs=(
            P(None, "lat", "lon"),
            P(None, "lat", "lon"),
            P(None, "lat", "lon"),
            P(None, "lat", "lon"),
        ),
        out_specs=P(None, "lat", "lon"),
        check_vma=False,
    )
```

time: 104 us -> 181 us (1.74)
  waiting for transfers between devices: 7.07 us -> 78.7 us
  blocking collectives: 54.9 us -> 20.1 us
  local copies, waits for them, and re-layouts: 8.92 us -> 43.2 us
  starting transfers between devices: 21.2 us -> 0.01 us
  between operations: 1.52 us -> 15 us
  other arithmetic: 9.97 us -> 23.2 us
    all_gather x0 -> x1, waiting for transfers between devices: none -> 78.7 us  [line_pass(): gathered = lax.all_gather(terms[None], mesh_axis, axis=0, tiled=True)]
    all_gather x2 -> x1, blocking collectives: 54.9 us -> 20.1 us  [line_pass(): gathered = lax.all_gather(terms[None], mesh_axis, axis=0, tiled=True)]
    slice x73 -> x92, local copies, waits for them, and re-layouts: 1.13 us -> 22.8 us  [the longest x9 12.1 us: row_at(): return lax.index_in_dim(member, place, axis, keepdims=False)]
    ppermute x8 -> x0, starting transfers between devices: 21.2 us -> none  [the longest x3 14.3 us: padded(): after = lax.ppermute(leading, axis, down)]
    ppermute x8 -> x0, waiting for transfers between devices: 7.07 us -> none  [the longest x5 7.06 us: padded(): before = lax.ppermute(last, axis, up)]
    unnamed x32 -> x99, local copies, waits for them, and re-layouts: 2.28 us -> 9.24 us
    div x12, other arithmetic: 1.86 us -> 6.03 us  [local_solve(): inverse = 1.0 / (excess - lower_band - upper_band)]
    mul x5, other arithmetic: 0.35 us -> 3.29 us  [the longest x1 1.24 us: shards(): lat_faces = lat_weight[:, :-1, :] * wet_cells[:, 1:, :]]
  transfers between devices with their start and end apart: 8 -> 1, of which waited for: 2 -> 1; matrix products, arithmetic and copies ran while one was open for 4% -> 0% of each run, Pallas kernels for 0% -> 0%
where the time goes in v2:
time: 181 us; the launch traced here: 180 us
  waiting for transfers between devices  78.7 us (43%)
  local copies, waits for them, and re-layouts  43.2 us (24%)
  other arithmetic  23.2 us (13%)
  blocking collectives  20.1 us (11%)
  between operations  15 us (8%)
    all_gather x1, waiting for transfers between devices, line_pass(): gathered = lax.all_gather(terms[None], mesh_axis, axis=0, tiled=True)  78.7 us
    all_gather x1, blocking collectives, line_pass(): gathered = lax.all_gather(terms[None], mesh_axis, axis=0, tiled=True)  20.1 us
    slice x9, local copies, waits for them, and re-layouts, row_at(): return lax.index_in_dim(member, place, axis, keepdims=False)  12.1 us
    unnamed x99, local copies, waits for them, and re-layouts  9.24 us
    div x12, other arithmetic, local_solve(): inverse = 1.0 / (excess - lower_band - upper_band)  6.03 us
    slice x26, local copies, waits for them, and re-layouts, earlier(): lax.slice_in_dim(values, 0, length - stride, axis=axis)  4.8 us
    add x10, other arithmetic, local_solve(): sources + left_weight * earlier(sources, stride, axis + 1)  4.04 us
  transfers between devices with their start and end apart: 1, of which 1 were waited for; matrix products, arithmetic and copies ran while one was open for 0% of the time, Pallas kernels for 0%

profile of v2, /device:TPU:1, one launch (start us, length us, event | category | flops | bytes accessed | tf_op | source)
XLA Modules:
  0.0 180.2 jit_solution(14112881031736275784)
XLA Ops:
  6.5 0.5 broadcast_select_fusion
  7.1 0.5 compare_select_fusion
  7.6 1.0 copy.506
  8.6 1.0 copy.505
  9.6 1.2 copy.504
  10.9 0.9 convert_multiply_fusion
  11.9 1.1 slice_negate_fusion.2
  13.0 0.9 subtract_divide_fusion.11
  13.9 0.8 pad_maximum_fusion.1
  14.7 1.5 copy.508
  16.5 0.8 copy-done.2
  17.4 0.9 copy-done.9
  25.7 0.7 constant_dynamic-update-slice_fusion.1
  26.4 20.1 %all-gather = f32[128,8,32]{2,1,0:T(8,128)S(1)} all-gather(f32[8,8,32]{2,1,0:T(8,128)S(1)} %constant_dynamic-update-slice_fusion), channel_id=2, replica_groups=mesh['lat'=32,'lon'=16] {'lon'}, dimensions={0}, use_global_device_ids=true | all-gather | bytes 139264 | tf_op jit(solution)/shard_map/all_gather | solution.py:100
  47.0 0.6 slice.1325
  47.6 0.6 slice.1320
  48.3 0.6 slice.1319
  48.9 0.6 fusion.139
  49.5 0.7 fusion.140
  50.1 0.6 fusion.137
  50.7 0.6 fusion.138
  51.5 0.7 fusion.130
  52.2 0.6 fusion.131
  52.8 1.2 slice_multiply_fusion
  54.2 1.3 slice_negate_fusion
  55.5 1.0 subtract_divide_fusion.4
  56.5 1.0 slice.1382
  57.7 0.7 fusion.136
  58.5 0.6 fusion.128
  59.1 1.1 add_divide_fusion.3
  60.5 0.5 fusion.68
  61.0 0.5 copy-done.1
  61.8 0.8 copy-done.7
  63.1 0.5 subtract_divide_fusion.3
  63.6 0.6 multiply_add_fusion.3
  64.1 0.5 fusion.67
  65.2 0.5 subtract_divide_fusion.2
  65.7 0.5 multiply_add_fusion.2
  66.3 0.5 fusion.66
  67.4 0.5 subtract_divide_fusion.1
  67.9 0.5 multiply_add_fusion.1
  68.5 0.5 fusion.65
  69.6 0.5 subtract_divide_fusion
  70.6 0.5 fusion.64
  71.7 0.5 multiply_subtract_fusion
  72.3 0.8 add_divide_fusion
  73.0 0.9 slice_bitcast_fusion
  73.9 1.1 fusion.78
  75.1 1.2 copy.517
  76.3 2.4 %fusion.77 = (f32[8,1,128]{1,0,2:T(8,128)}, f32[8,1,128]{1,0,2:T(8,128)}) fusion(f32[8,32,128]{1,0,2:T(8,128)} %get-tuple-element.112), kind=kLoop, calls=%fused_computation.294 | loop fusion | bytes 16384 | tf_op jit(solution)/shard_map/slice | solution.py:85
  78.7 1.2 copy.518
  79.9 1.1 fusion.76
  81.0 1.3 copy.519
  82.3 1.2 copy.520
  83.5 1.2 copy.521
  84.8 1.2 copy.522
  86.5 0.6 copy-done.38
  87.2 78.7 %all-gather.4.cloned.1.call-done = f32[256,8,128]{2,1,0:T(8,128)} async-done(((f32[8,8,128]{2,1,0:T(8,128)}), f32[256,8,128]{2,1,0:T(8,128)}) %all-gather.4.cloned.1.call-update) | async-done | bytes 1048592 | tf_op jit(solution)/shard_map/all_gather | solution.py:100
  165.9 0.7 slice_bitcast_fusion.22
  166.6 1.1 slice_bitcast_fusion.10
  167.7 1.1 fusion.11
  168.8 1.0 subtract_divide_fusion.16
  171.5 0.5 copy-done.4
  172.5 0.9 copy.532
  (254 shorter events, 14.2 us)
Async XLA Ops:
  6.5 159.3 %all-gather.4.cloned.1.call-start = ((), (), s32[]{:S(2)}) async-start(), calls=%async_computation | async-start | bytes 1081344 | tf_op jit(solution)/shard_map/all_gather | solution.py:100
  9.6 2.2 %copy-start.3 = (bf16[8,32,128]{1,0,2:T(8,128)(2,1)}, bf16[8,32,128]{1,0,2:T(8,128)(2,1)S(1)}, u32[]{:S(2)}) copy-start(bf16[8,32,128]{1,0,2:T(8,128)(2,1)S(1)} %copy.505) | copy-start | bytes 196612
  11.8 2.0 %copy-start.5 = (f32[8,32,128]{1,0,2:T(8,128)}, f32[8,32,128]{1,0,2:T(8,128)S(1)}, u32[]{:S(2)}) copy-start(f32[8,32,128]{1,0,2:T(8,128)S(1)} %get-tuple-element.176) | copy-start | bytes 393220
  11.9 2.0 %copy-start.31 = (f32[8,32,128]{2,1,0:T(8,128)S(1)}, f32[8,32,128]{2,1,0:T(8,128)}, u32[]{:S(2)}) copy-start(f32[8,32,128]{2,1,0:T(8,128)} %param.4) | copy-start | bytes 393220
  16.2 1.0 copy-start.2
  16.3 1.2 copy-start.19
  17.3 1.1 copy-start.9
  17.3 1.2 copy-start.10
  17.3 1.4 copy-start.18
  47.0 5.8 %copy-start.14 = (f32[16,8,32]{2,1,0:T(8,128)}, f32[16,8,32]{2,1,0:T(8,128)S(1)}, u32[]{:S(2)}) copy-start(f32[16,8,32]{2,1,0:T(8,128)S(1)} %get-tuple-element.61) | copy-start | bytes 49156
  47.0 5.8 %copy-start.16 = (f32[16,8,32]{2,1,0:T(8,128)}, f32[16,8,32]{2,1,0:T(8,128)S(1)}, u32[]{:S(2)}) copy-start(f32[16,8,32]{2,1,0:T(8,128)S(1)} %get-tuple-element.62) | copy-start | bytes 49156
  54.0 2.5 %copy-start = (f32[8,32,128]{1,0,2:T(8,128)S(1)}, f32[8,32,128]{1,0,2:T(8,128)}, u32[]{:S(2)}) copy-start(f32[8,32,128]{1,0,2:T(8,128)} %get-tuple-element.175) | copy-start | bytes 393220
  54.1 3.5 %copy-start.15 = (f32[16,8,32]{2,1,0:T(8,128)S(1)}, f32[16,8,32]{2,1,0:T(8,128)}, u32[]{:S(2)}) copy-start(f32[16,8,32]{2,1,0:T(8,128)} %copy-done.14) | copy-start | bytes 49156
  54.1 3.5 %copy-start.17 = (f32[16,8,32]{2,1,0:T(8,128)S(1)}, f32[16,8,32]{2,1,0:T(8,128)}, u32[]{:S(2)}) copy-start(f32[16,8,32]{2,1,0:T(8,128)} %copy-done.16) | copy-start | bytes 49156
  54.1 3.5 %copy-start.22 = (f32[12,8,32]{2,1,0:T(8,128)S(1)}, f32[12,8,32]{2,1,0:T(8,128)}, u32[]{:S(2)}) copy-start(f32[12,8,32]{2,1,0:T(8,128)} %slice.1325) | copy-start | bytes 36868
  54.1 3.5 %copy-start.23 = (f32[12,8,32]{2,1,0:T(8,128)S(1)}, f32[12,8,32]{2,1,0:T(8,128)}, u32[]{:S(2)}) copy-start(f32[12,8,32]{2,1,0:T(8,128)} %slice.1320) | copy-start | bytes 36868
  54.1 3.5 %copy-start.26 = (f32[12,8,32]{2,1,0:T(8,128)S(1)}, f32[12,8,32]{2,1,0:T(8,128)}, u32[]{:S(2)}) copy-start(f32[12,8,32]{2,1,0:T(8,128)} %get-tuple-element.295) | copy-start | bytes 36868
  54.1 3.5 %copy-start.27 = (f32[12,8,32]{2,1,0:T(8,128)S(1)}, f32[12,8,32]{2,1,0:T(8,128)}, u32[]{:S(2)}) copy-start(f32[12,8,32]{2,1,0:T(8,128)} %get-tuple-element.296) | copy-start | bytes 36868
  54.1 3.5 %copy-start.28 = (f32[12,8,32]{2,1,0:T(8,128)S(1)}, f32[12,8,32]{2,1,0:T(8,128)}, u32[]{:S(2)}) copy-start(f32[12,8,32]{2,1,0:T(8,128)} %get-tuple-element.291) | copy-start | bytes 36868
  54.1 3.5 %copy-start.29 = (f32[12,8,32]{2,1,0:T(8,128)S(1)}, f32[12,8,32]{2,1,0:T(8,128)}, u32[]{:S(2)}) copy-start(f32[12,8,32]{2,1,0:T(8,128)} %get-tuple-element.292) | copy-start | bytes 36868
  54.1 3.5 %copy-start.30 = (f32[4,8,32]{2,1,0:T(8,128)S(1)}, f32[4,8,32]{2,1,0:T(8,128)}, u32[]{:S(2)}) copy-start(f32[4,8,32]{2,1,0:T(8,128)} %slice.1319) | copy-start | bytes 12292
  54.1 3.5 %copy-start.34 = (f32[4,8,32]{2,1,0:T(8,128)S(1)}, f32[4,8,32]{2,1,0:T(8,128)}, u32[]{:S(2)}) copy-start(f32[4,8,32]{2,1,0:T(8,128)} %get-tuple-element.293) | copy-start | bytes 12292
  54.2 3.5 %copy-start.35 = (f32[4,8,32]{2,1,0:T(8,128)S(1)}, f32[4,8,32]{2,1,0:T(8,128)}, u32[]{:S(2)}) copy-start(f32[4,8,32]{2,1,0:T(8,128)} %get-tuple-element.294) | copy-start | bytes 12292
  54.2 3.5 %copy-start.36 = (f32[4,8,32]{2,1,0:T(8,128)S(1)}, f32[4,8,32]{2,1,0:T(8,128)}, u32[]{:S(2)}) copy-start(f32[4,8,32]{2,1,0:T(8,128)} %get-tuple-element.289) | copy-start | bytes 12292
  54.2 3.5 %copy-start.37 = (f32[4,8,32]{2,1,0:T(8,128)S(1)}, f32[4,8,32]{2,1,0:T(8,128)}, u32[]{:S(2)}) copy-start(f32[4,8,32]{2,1,0:T(8,128)} %get-tuple-element.290) | copy-start | bytes 12292
  55.5 2.9 %copy-start.24 = (f32[12,8,32]{2,1,0:T(8,128)S(1)}, f32[12,8,32]{2,1,0:T(8,128)}, u32[]{:S(2)}) copy-start(f32[12,8,32]{2,1,0:T(8,128)} %get-tuple-element.275) | copy-start | bytes 36868
  55.5 2.9 %copy-start.25 = (f32[12,8,32]{2,1,0:T(8,128)S(1)}, f32[12,8,32]{2,1,0:T(8,128)}, u32[]{:S(2)}) copy-start(f32[12,8,32]{2,1,0:T(8,128)} %get-tuple-element.276) | copy-start | bytes 36868
  55.5 2.9 %copy-start.32 = (f32[4,8,32]{2,1,0:T(8,128)S(1)}, f32[4,8,32]{2,1,0:T(8,128)}, u32[]{:S(2)}) copy-start(f32[4,8,32]{2,1,0:T(8,128)} %get-tuple-element.277) | copy-start | bytes 12292
  55.5 2.9 %copy-start.33 = (f32[4,8,32]{2,1,0:T(8,128)S(1)}, f32[4,8,32]{2,1,0:T(8,128)}, u32[]{:S(2)}) copy-start(f32[4,8,32]{2,1,0:T(8,128)} %get-tuple-element.278) | copy-start | bytes 12292
  57.7 0.7 copy-start.11
  57.7 0.7 copy-start.12
  57.7 0.7 copy-start.13
  59.1 1.2 copy-start.40
  59.1 1.2 copy-start.39
  60.5 1.0 copy-start.1
  61.5 1.0 copy-start.7
  61.5 1.2 copy-start.8
  61.5 1.4 copy-start.20
  61.5 1.5 copy-start.21
  81.0 5.0 %copy-start.6 = (f32[8,1,128]{1,0,2:T(8,128)S(1)}, f32[8,1,128]{1,0,2:T(8,128)}, u32[]{:S(2)}) copy-start(f32[8,1,128]{1,0,2:T(8,128)} %slice.1382) | copy-start | bytes 12292
  86.5 0.6 copy-start.38
  171.1 1.0 copy-start.4
Sparse Core Ops, SparseCore 0:
  87.3 78.5 all-gather.3

commit v3 on v2

v3 whole, which is shorter than its diff:
```python
import functools

import jax
import jax.numpy as jnp
from jax import lax
from jax.experimental import pallas as pl
from jax.experimental.pallas import tpu as pltpu
from jax.sharding import PartitionSpec as P

TERMS = 7


def shifted(values, shift, axis):
    length = values.shape[axis]
    return pltpu.roll(values, shift % length, axis)


def block_solve(lower_band, upper_band, excess, sources, axis):
    length = lower_band.shape[axis]
    stride = 1
    while stride < length:
        inverse = 1.0 / (excess - lower_band - upper_band)
        left_weight = -lower_band * shifted(inverse, stride, axis)
        right_coefficient = -upper_band * shifted(inverse, -stride, axis)
        new_lower = left_weight * shifted(lower_band, stride, axis)
        new_upper = right_coefficient * shifted(upper_band, -stride, axis)
        excess = (
            excess
            + left_weight * shifted(excess, stride, axis)
            + right_coefficient * shifted(excess, -stride, axis)
        )
        sources = [
            member
            + left_weight * shifted(member, stride, axis)
            + right_coefficient * shifted(member, -stride, axis)
            for member in sources
        ]
        lower_band, upper_band = (new_lower, new_upper)
        stride = stride * 2
    diagonal = excess - lower_band - upper_band
    return [member / diagonal for member in sources]


def pass_kernel(axis, corrected, *refs):
    if corrected:
        (p_ref, u_ref, w_ref, before_ref, here_ref, kappa_ref, mask_ref,
         p_out, u_out, w_out, edge_out) = refs
        values = (
            p_ref[...]
            - u_ref[...] * before_ref[...]
            + w_ref[...] * here_ref[...]
        )
    else:
        (source_ref, kappa_ref, mask_ref, p_out, u_out, w_out, edge_out) = refs
        values = source_ref[...]
    shape = values.shape
    length = shape[axis]
    wet = mask_ref[...].astype(jnp.float32)
    weight = kappa_ref[...].astype(jnp.float32) * wet
    position = lax.broadcasted_iota(jnp.int32, shape, axis)
    last = position == length - 1
    right_face = jnp.where(last, 0.0, weight * shifted(wet, -1, axis))
    left_face = shifted(right_face, 1, axis)
    first = position == 0
    particular, from_left, from_right = block_solve(
        -left_face,
        -right_face,
        jnp.ones(shape, jnp.float32),
        [values, jnp.where(first, 1.0, 0.0), jnp.where(last, 1.0, 0.0)],
        axis,
    )
    p_out[...] = particular
    u_out[...] = from_left
    w_out[...] = from_right
    tail_weight = shifted(weight, 4, axis)
    entries = [
        wet * particular,
        shifted(wet * from_left, 1, axis),
        shifted(wet * from_right, 2, axis),
        tail_weight,
        shifted(from_left, 4 + 1, axis),
        shifted(from_right, 4 + 2, axis),
        shifted(particular, 4 + 3, axis),
    ]
    edge = entries[0]
    for k in range(1, TERMS):
        edge = jnp.where(position == k, entries[k], edge)
    if axis == 2:
        edge_out[...] = edge
    else:
        edge_out[...] = lax.slice_in_dim(edge, 0, 8, axis=axis)


def local_pass(axis, inputs):
    shape = inputs[0].shape
    corrected = len(inputs) > 3
    edge_shape = shape if axis == 2 else shape[:axis] + (8,) + shape[axis + 1:]
    return pl.pallas_call(
        functools.partial(pass_kernel, axis, corrected),
        out_shape=(
            jax.ShapeDtypeStruct(shape, jnp.float32),
            jax.ShapeDtypeStruct(shape, jnp.float32),
            jax.ShapeDtypeStruct(shape, jnp.float32),
            jax.ShapeDtypeStruct(edge_shape, jnp.float32),
        ),
    )(*inputs)


def circular_solve(lower_band, upper_band, excess, sources):
    devices = lower_band.shape[0]
    stride = 1
    while stride < devices:
        inverse = 1.0 / (excess - lower_band - upper_band)
        left_weight = -lower_band * jnp.roll(inverse, stride, 0)
        right_coefficient = -upper_band * jnp.roll(inverse, -stride, 0)
        new_lower = left_weight * jnp.roll(lower_band, stride, 0)
        new_upper = right_coefficient * jnp.roll(upper_band, -stride, 0)
        excess = (
            excess
            + left_weight * jnp.roll(excess, stride, 0)
            + right_coefficient * jnp.roll(excess, -stride, 0)
        )
        sources = (
            sources
            + left_weight * jnp.roll(sources, stride, 0)
            + right_coefficient * jnp.roll(sources, -stride, 0)
        )
        lower_band, upper_band = (new_lower, new_upper)
        stride = stride * 2
    return sources / excess


def interface_flux(edge, axis, mesh_axis, periodic):
    terms = lax.slice_in_dim(edge, 0, TERMS, axis=axis)
    gathered = lax.all_gather(terms[None], mesh_axis, axis=0, tiled=True)
    devices = gathered.shape[0]
    (head_p, head_u, head_w, tail_kappa, tail_u, tail_w, tail_p) = (
        lax.index_in_dim(gathered, k, axis + 1, keepdims=False) for k in range(TERMS)
    )

    def next_of(member):
        return jnp.roll(member, -1, 0)

    next_wet = jnp.where(next_of(head_u) > 0.0, 1.0, 0.0)
    face = tail_kappa * next_wet
    if not periodic:
        device = lax.broadcasted_iota(jnp.int32, face.shape, 0)
        face = jnp.where(device == devices - 1, 0.0, face)
        tail_kappa = jnp.where(device == devices - 1, 0.0, tail_kappa)
    lower = -face * tail_u
    upper = -tail_kappa * next_of(head_w)
    diagonal = 1.0 + tail_kappa * next_of(head_u) + face * tail_w
    flux = circular_solve(
        lower, upper, diagonal + lower + upper, tail_kappa * next_of(head_p) - face * tail_p
    )
    index = lax.axis_index(mesh_axis)
    here = lax.dynamic_index_in_dim(flux, index, 0, keepdims=True)
    before = lax.dynamic_index_in_dim(flux, (index + devices - 1) % devices, 0, keepdims=True)
    return before[0], here[0]


def shards(source, kappa_lon, kappa_lat, sea_mask):
    p_lon, u_lon, w_lon, edge_lon = local_pass(2, (source, kappa_lon, sea_mask))
    before, here = interface_flux(edge_lon, 2, "lon", True)
    p_lat, u_lat, w_lat, edge_lat = local_pass(
        1, (p_lon, u_lon, w_lon, before[:, :, None], here[:, :, None], kappa_lat, sea_mask)
    )
    before, here = interface_flux(edge_lat, 1, "lat", False)
    lat_pass = p_lat - u_lat * before[:, None, :] + w_lat * here[:, None, :]
    wet_cells = sea_mask.astype(jnp.float32)
    lon_kappa = kappa_lon.astype(jnp.float32)
    lat_kappa = kappa_lat.astype(jnp.float32)
    return wet_cells * 4.0 * jnp.sqrt(jnp.sqrt(lon_kappa * lat_kappa)) * lat_pass


def solution(mesh):
    return jax.shard_map(
        shards,
        mesh=mesh,
        in_specs=(
            P(None, "lat", "lon"),
            P(None, "lat", "lon"),
            P(None, "lat", "lon"),
            P(None, "lat", "lon"),
        ),
        out_specs=P(None, "lat", "lon"),
        check_vma=False,
    )
```

time: 181 us -> 80.6 us (0.45)
  waiting for transfers between devices: 78.7 us -> 0 us
  blocking collectives: 20.1 us -> 64.9 us
  local copies, waits for them, and re-layouts: 43.2 us -> 4.97 us
  other arithmetic: 23.2 us -> 2.03 us
  between operations: 15 us -> 0.79 us
  Pallas kernels: 0 us -> 7.64 us
    all_gather x1 -> x0, waiting for transfers between devices: 78.7 us -> none  [line_pass(): gathered = lax.all_gather(terms[None], mesh_axis, axis=0, tiled=True)]
    all_gather x1 -> x2, blocking collectives: 20.1 us -> 64.9 us  [interface_flux(): gathered = lax.all_gather(terms[None], mesh_axis, axis=0, tiled=True)]
    slice x60 -> x2, local copies, waits for them, and re-layouts: 20.9 us -> 1.78 us  [interface_flux(): terms = lax.slice_in_dim(edge, 0, TERMS, axis=axis)]
    unnamed x99 -> x12, local copies, waits for them, and re-layouts: 9.24 us -> 0.98 us
    pallas_call x0 -> x2, Pallas kernels: none -> 7.64 us  [local_pass(): pl.pallas_call(functools.partial(pass_kernel, axis, corrected), out_shape...]
    div x14 -> x0, other arithmetic: 7.11 us -> none  [the longest x12 6.03 us: local_solve(): inverse = 1.0 / (excess - lower_band - upper_band)]
    add x11 -> x0, other arithmetic: 4.11 us -> none  [the longest x10 4.04 us: local_solve(): sources + left_weight * earlier(sources, stride, axis + 1)]
    mul x5 -> x0, other arithmetic: 3.29 us -> none  [the longest x1 1.24 us: shards(): lat_faces = lat_weight[:, :-1, :] * wet_cells[:, 1:, :]]
  transfers between devices with their start and end apart: 1 -> 0, of which waited for: 1 -> 0; matrix products, arithmetic and copies ran while one was open for 0% -> 0% of each run, Pallas kernels for 0% -> 0%
where the time goes in v3:
time: 80.6 us; the launch traced here: 80.3 us
  blocking collectives  64.9 us (81%)
  Pallas kernels  7.64 us (9%)
  local copies, waits for them, and re-layouts  4.97 us (6%)
  other arithmetic  2.03 us (3%)
    all_gather x2, blocking collectives, interface_flux(): gathered = lax.all_gather(terms[None], mesh_axis, axis=0, tiled=True)  64.9 us
    pallas_call x2, Pallas kernels, local_pass(): pl.pallas_call(functools.partial(pass_kernel, axis, corrected), out_shape...  7.64 us
    slice x2, local copies, waits for them, and re-layouts, interface_flux(): terms = lax.slice_in_dim(edge, 0, TERMS, axis=axis)  1.78 us

profile of v3, /device:TPU:1, one launch (start us, length us, event | category | flops | bytes accessed | tf_op | source)
XLA Modules:
  0.0 80.3 jit_solution(1088534547647619451)
XLA Ops:
  0.0 4.7 %shard_map.46 = (f32[8,32,128]{2,1,0:T(8,128)}, f32[8,32,128]{2,1,0:T(8,128)}, f32[8,32,128]{2,1,0:T(8,128)}, f32[8,32,128]{2,1,0:T(8,128)}) custom-call(f32[8,32,128]{2,1,0:T(8,128)} %refs_0_.1, bf16[8,32,128]{2,1,0:T(8,128)(2,1)} %refs_1_.1, s32[8,32,128]{2,1,0:T(8,128)} %refs_6_.1), custom_call_target="tpu_custom_call" | custom-call | tf_op jit(solution)/shard_map/pallas_call | solution.py:98
  4.7 1.0 %copy.43 = f32[8,32,7]{1,0,2:T(8,128)S(1)} copy(f32[8,32,7]{2,1,0:T(8,128)} %bitcast.128) | data formatting | bytes 14336 | tf_op jit(solution)/shard_map/slice | solution.py:134
  5.8 20.2 %all-gather = f32[128,32,7]{1,0,2:T(8,128)S(1)} all-gather(f32[8,32,7]{1,0,2:T(8,128)S(1)} %copy.43), channel_id=2, replica_groups=mesh['lat'=32,'lon'=16] {'lon'}, dimensions={0}, use_global_device_ids=true | all-gather | bytes 121856 | tf_op jit(solution)/shard_map/all_gather | solution.py:135
  26.0 0.1 subtract_divide_fusion.8
  26.2 0.1 subtract_divide_fusion.7
  26.5 0.1 subtract_divide_fusion.6
  26.7 0.1 subtract_divide_fusion.5
  26.8 0.1 add_divide_fusion.1
  26.9 0.8 copy.46.refs_3_
  27.7 0.8 copy.47.refs_4_
  28.4 2.9 %shard_map.47 = (f32[8,32,128]{2,1,0:T(8,128)}, f32[8,32,128]{2,1,0:T(8,128)}, f32[8,32,128]{2,1,0:T(8,128)}, f32[8,8,128]{2,1,0:T(8,128)}) custom-call(f32[8,32,128]{2,1,0:T(8,128)} %get-tuple-element.13.refs_0_, f32[8,32,128]{2,1,0:T(8,128)} %get-tuple-element.14.refs_1_, f32[8,32,128]{2,1,0:T(8,128)} %get-tuple-element.15.refs_2_, ...), custom_call_target="tpu_custom_call" | custom-call | tf_op jit(solution)/shard_map/pallas_call | solution.py:98
  31.4 0.8 copy.48
  32.1 44.7 %all-gather.1 = f32[256,7,128]{2,0,1:T(8,128)S(1)} all-gather(f32[8,7,128]{2,0,1:T(8,128)S(1)} %copy.48), channel_id=3, replica_groups=mesh['lat'=32,'lon'=16] {'lat'}, dimensions={0}, use_global_device_ids=true | all-gather | bytes 946176 | tf_op jit(solution)/shard_map/all_gather | solution.py:135
  76.9 0.2 subtract_divide_fusion.4
  77.1 0.1 fusion.8
  77.3 0.1 subtract_divide_fusion.3
  77.5 0.1 fusion.12
  77.7 0.1 subtract_divide_fusion.2
  77.8 0.1 fusion.16
  78.0 0.1 subtract_divide_fusion.1
  78.2 0.1 subtract_divide_fusion
  78.4 0.0 copy-start
  78.4 0.0 copy-start.2
  78.4 0.0 copy-start.3
  78.4 0.0 copy-start.4
  78.4 0.0 copy-start.5
  78.4 0.1 add_divide_fusion
  78.5 0.0 copy-start.1
  78.6 0.7 copy-done
  79.3 0.0 copy-done.2
  79.3 0.1 copy-done.3
  79.4 0.1 copy-done.4
  79.5 0.1 copy-done.5
  79.5 0.0 copy-done.1
  79.5 0.8 add_multiply_fusion
  (85 shorter events, 0.8 us)
Async XLA Ops:
  78.4 0.9 %copy-start = (s32[8,32,128]{2,1,0:T(8,128)S(1)}, s32[8,32,128]{2,1,0:T(8,128)}, u32[]{:S(2)}) copy-start(s32[8,32,128]{2,1,0:T(8,128)} %refs_6_.1) | copy-start | bytes 393220
  78.4 0.9 %copy-start.2 = (bf16[8,32,128]{2,1,0:T(8,128)(2,1)S(1)}, bf16[8,32,128]{2,1,0:T(8,128)(2,1)}, u32[]{:S(2)}) copy-start(bf16[8,32,128]{2,1,0:T(8,128)(2,1)} %refs_5_.1) | copy-start | bytes 196612
  78.4 1.0 %copy-start.3 = (f32[8,32,128]{2,1,0:T(8,128)S(1)}, f32[8,32,128]{2,1,0:T(8,128)}, u32[]{:S(2)}) copy-start(f32[8,32,128]{2,1,0:T(8,128)} %get-tuple-element.17) | copy-start | bytes 393220
  78.4 1.0 %copy-start.4 = (f32[8,32,128]{2,1,0:T(8,128)S(1)}, f32[8,32,128]{2,1,0:T(8,128)}, u32[]{:S(2)}) copy-start(f32[8,32,128]{2,1,0:T(8,128)} %get-tuple-element.18) | copy-start | bytes 393220
  78.4 1.1 %copy-start.5 = (f32[8,32,128]{2,1,0:T(8,128)S(1)}, f32[8,32,128]{2,1,0:T(8,128)}, u32[]{:S(2)}) copy-start(f32[8,32,128]{2,1,0:T(8,128)} %get-tuple-element.20) | copy-start | bytes 393220
  78.5 1.0 %copy-start.1 = (bf16[8,32,128]{2,1,0:T(8,128)(2,1)S(1)}, bf16[8,32,128]{2,1,0:T(8,128)(2,1)}, u32[]{:S(2)}) copy-start(bf16[8,32,128]{2,1,0:T(8,128)(2,1)} %refs_1_.1) | copy-start | bytes 196612

commit v4 on v3

--- a/solution.py
+++ b/solution.py
@@ -130,10 +130,14 @@
     return sources / excess
 
 
-def interface_flux(edge, axis, mesh_axis, periodic):
+def interface_flux(edge, axis, mesh_axis, periodic, exchange):
     terms = lax.slice_in_dim(edge, 0, TERMS, axis=axis)
-    gathered = lax.all_gather(terms[None], mesh_axis, axis=0, tiled=True)
-    devices = gathered.shape[0]
+    devices = lax.axis_size(mesh_axis)
+    if exchange == "all_to_all":
+        copies = jnp.broadcast_to(terms[None], (devices,) + terms.shape)
+        gathered = lax.all_to_all(copies, mesh_axis, 0, 0, tiled=True)
+    else:
+        gathered = lax.all_gather(terms[None], mesh_axis, axis=0, tiled=True)
     (head_p, head_u, head_w, tail_kappa, tail_u, tail_w, tail_p) = (
         lax.index_in_dim(gathered, k, axis + 1, keepdims=False) for k in range(TERMS)
     )
@@ -161,11 +165,11 @@
 
 def shards(source, kappa_lon, kappa_lat, sea_mask):
     p_lon, u_lon, w_lon, edge_lon = local_pass(2, (source, kappa_lon, sea_mask))
-    before, here = interface_flux(edge_lon, 2, "lon", True)
+    before, here = interface_flux(edge_lon, 2, "lon", True, "all_to_all")
     p_lat, u_lat, w_lat, edge_lat = local_pass(
         1, (p_lon, u_lon, w_lon, before[:, :, None], here[:, :, None], kappa_lat, sea_mask)
     )
-    before, here = interface_flux(edge_lat, 1, "lat", False)
+    before, here = interface_flux(edge_lat, 1, "lat", False, "all_gather")
     lat_pass = p_lat - u_lat * before[:, None, :] + w_lat * here[:, None, :]
     wet_cells = sea_mask.astype(jnp.float32)
     lon_kappa = kappa_lon.astype(jnp.float32)

time: 80.6 us -> 73.2 us (0.908)
  blocking collectives: 64.9 us -> 40.6 us
  starting transfers between devices: 0 us -> 7.57 us
  waiting for transfers between devices: 0 us -> 6.61 us
  local copies, waits for them, and re-layouts: 4.97 us -> 6.68 us
  other arithmetic: 2.03 us -> 2.92 us
    all_gather x2 -> x1, blocking collectives: 64.9 us -> 40.6 us  [interface_flux(): gathered = lax.all_gather(terms[None], mesh_axis, axis=0, tiled=True)]
    all_to_all x0 -> x1, starting transfers between devices: none -> 7.57 us  [interface_flux(): gathered = lax.all_to_all(copies, mesh_axis, 0, 0, tiled=True)]
    all_to_all x0 -> x1, waiting for transfers between devices: none -> 6.61 us  [interface_flux(): gathered = lax.all_to_all(copies, mesh_axis, 0, 0, tiled=True)]
    unnamed x12 -> x15, local copies, waits for them, and re-layouts: 0.98 us -> 2.1 us
    all_to_all x0 -> x1, other arithmetic: none -> 0.9 us  [interface_flux(): gathered = lax.all_to_all(copies, mesh_axis, 0, 0, tiled=True)]
  transfers between devices with their start and end apart: 0 -> 1, of which waited for: 0 -> 1; matrix products, arithmetic and copies ran while one was open for 0% -> 0% of each run, Pallas kernels for 0% -> 0%
where the time goes in v4:
time: 73.2 us; the launch traced here: 72.9 us
  blocking collectives  40.6 us (55%)
  Pallas kernels  7.64 us (10%)
  starting transfers between devices  7.57 us (10%)
  local copies, waits for them, and re-layouts  6.68 us (9%)
  waiting for transfers between devices  6.61 us (9%)
  other arithmetic  2.92 us (4%)
  between operations  0.82 us (1%)
    all_gather x1, blocking collectives, interface_flux(): gathered = lax.all_gather(terms[None], mesh_axis, axis=0, tiled=True)  40.6 us
    pallas_call x2, Pallas kernels, local_pass(): pl.pallas_call(functools.partial(pass_kernel, axis, corrected), out_shape...  7.64 us
    all_to_all x1, starting transfers between devices, interface_flux(): gathered = lax.all_to_all(copies, mesh_axis, 0, 0, tiled=True)  7.57 us
    all_to_all x1, waiting for transfers between devices, interface_flux(): gathered = lax.all_to_all(copies, mesh_axis, 0, 0, tiled=True)  6.61 us
    unnamed x15, local copies, waits for them, and re-layouts  2.1 us
    slice x2, local copies, waits for them, and re-layouts, interface_flux(): terms = lax.slice_in_dim(edge, 0, TERMS, axis=axis)  1.78 us
  transfers between devices with their start and end apart: 1, of which 1 were waited for; matrix products, arithmetic and copies ran while one was open for 0% of the time, Pallas kernels for 0%

profile of v4, /device:TPU:1, one launch (start us, length us, event | category | flops | bytes accessed | tf_op | source)
XLA Modules:
  0.0 72.9 jit_solution(5917866879583100503)
XLA Ops:
  0.0 4.7 %shard_map.46 = (f32[8,32,128]{2,1,0:T(8,128)}, f32[8,32,128]{2,1,0:T(8,128)}, f32[8,32,128]{2,1,0:T(8,128)}, f32[8,32,128]{2,1,0:T(8,128)}) custom-call(f32[8,32,128]{2,1,0:T(8,128)} %refs_0_.1, bf16[8,32,128]{2,1,0:T(8,128)(2,1)} %refs_1_.1, s32[8,32,128]{2,1,0:T(8,128)} %refs_6_.1), custom_call_target="tpu_custom_call" | custom-call | tf_op jit(solution)/shard_map/pallas_call | solution.py:98
  4.7 1.0 %copy.29 = f32[8,32,7]{1,0,2:T(8,128)S(1)} copy(f32[8,32,7]{2,1,0:T(8,128)} %bitcast.140) | data formatting | bytes 14336 | tf_op jit(solution)/shard_map/slice | solution.py:134
  5.8 0.9 %reshape.16 = f32[16,1,1792]{2,1,0:T(1,128)} reshape(f32[16,7,8,32]{3,2,1,0:T(8,128)S(1)} %broadcast_bitcast_fusion) | data formatting | bytes 229376
  6.7 7.6 %all-to-all-start = ((f32[16,1,1792]{2,1,0:T(1,128)}), f32[16,1,1792]{2,1,0:T(1,128)S(1)}, u32[]{:S(2)}, u32[]{:S(2)}) async-start(f32[16,1,1792]{2,1,0:T(1,128)} %reshape.16), calls=%async_computation | async-start | bytes 229376 | tf_op jit(solution)/shard_map/all_to_all | solution.py:138
  14.3 6.6 %all-to-all-done = f32[16,1,1792]{2,1,0:T(1,128)S(1)} async-done(((f32[16,1,1792]{2,1,0:T(1,128)}), f32[16,1,1792]{2,1,0:T(1,128)S(1)}, u32[]{:S(2)}, u32[]{:S(2)}) %all-to-all-start) | async-done | bytes 114720 | tf_op jit(solution)/shard_map/all_to_all | solution.py:138
  20.9 0.6 broadcast.12
  21.5 0.9 %reduce = f32[16,1792]{1,0:T(8,128)S(1)} reduce(f32[16,1,1792]{2,1,0:T(1,128)S(1)} %all-to-all-done, f32[]{:T(128)} %broadcast.12), dimensions={1}, to_apply=%all_to_all.3.reduce_sub_computation | reduce | bytes 229380 | tf_op jit(solution)/shard_map/all_to_all | solution.py:138
  22.4 0.2 reshape.17
  22.6 0.1 subtract_divide_fusion.8
  22.9 0.1 subtract_divide_fusion.7
  23.1 0.1 subtract_divide_fusion.6
  23.3 0.1 subtract_divide_fusion.5
  23.4 0.1 add_divide_fusion.1
  23.5 0.8 %copy.37.refs_3_ = f32[8,32,1]{2,1,0:T(8,128)} copy(f32[8,32,1]{1,0,2:T(8,128)S(1)} %get-tuple-element.128) | data formatting | bytes 2048 | tf_op jit(solution)/shard_map/broadcast_in_dim;squeeze | solution.py:170
  24.3 0.8 %copy.38.refs_4_ = f32[8,32,1]{2,1,0:T(8,128)} copy(f32[8,32,1]{1,0,2:T(8,128)S(1)} %get-tuple-element.127) | data formatting | bytes 2048 | tf_op jit(solution)/shard_map/broadcast_in_dim;squeeze | solution.py:170
  25.1 2.9 %shard_map.47 = (f32[8,32,128]{2,1,0:T(8,128)}, f32[8,32,128]{2,1,0:T(8,128)}, f32[8,32,128]{2,1,0:T(8,128)}, f32[8,8,128]{2,1,0:T(8,128)}) custom-call(f32[8,32,128]{2,1,0:T(8,128)} %get-tuple-element.13.refs_0_, f32[8,32,128]{2,1,0:T(8,128)} %get-tuple-element.14.refs_1_, f32[8,32,128]{2,1,0:T(8,128)} %get-tuple-element.15.refs_2_, ...), custom_call_target="tpu_custom_call" | custom-call | tf_op jit(solution)/shard_map/pallas_call | solution.py:98
  28.0 0.8 %copy.39 = f32[8,7,128]{2,0,1:T(8,128)S(1)} copy(f32[8,7,128]{2,1,0:T(8,128)} %bitcast.141) | data formatting | bytes 57344 | tf_op jit(solution)/shard_map/slice | solution.py:134
  28.7 40.6 %all-gather = f32[256,7,128]{2,0,1:T(8,128)S(1)} all-gather(f32[8,7,128]{2,0,1:T(8,128)S(1)} %copy.39), channel_id=2, replica_groups=mesh['lat'=32,'lon'=16] {'lat'}, dimensions={0}, use_global_device_ids=true | all-gather | bytes 946176 | tf_op jit(solution)/shard_map/all_gather | solution.py:140
  69.4 0.2 subtract_divide_fusion.4
  69.7 0.1 fusion.8
  69.9 0.1 subtract_divide_fusion.3
  70.0 0.1 fusion.12
  70.2 0.1 subtract_divide_fusion.2
  70.4 0.1 fusion.16
  70.6 0.1 subtract_divide_fusion.1
  70.8 0.1 subtract_divide_fusion
  70.9 0.0 copy-start
  71.0 0.0 copy-start.1
  71.0 0.0 copy-start.2
  71.0 0.0 copy-start.3
  71.0 0.0 copy-start.4
  71.0 0.0 copy-start.5
  71.0 0.1 add_divide_fusion
  71.1 0.7 %copy-done = s32[8,32,128]{2,1,0:T(8,128)S(1)} copy-done((s32[8,32,128]{2,1,0:T(8,128)S(1)}, s32[8,32,128]{2,1,0:T(8,128)}, u32[]{:S(2)}) %copy-start) | copy-done | bytes 131096
  71.9 0.0 copy-done.1
  71.9 0.0 copy-done.2
  71.9 0.1 copy-done.3
  72.0 0.1 copy-done.4
  72.1 0.1 copy-done.5
  72.1 0.8 %add_multiply_fusion = f32[8,32,128]{2,1,0:T(8,128)} fusion(f32[8,32,128]{2,1,0:T(8,128)S(1)} %copy-done.5, f32[8,32,128]{2,1,0:T(8,128)S(1)} %copy-done.3, f32[8,32,128]{2,1,0:T(8,128)S(1)} %copy-done.4, bf16[8,32,128]{2,1,0:T(8,128)(2,1)S(1)} %copy-done.2, bf16[8,32,128]{2,1,0:T(8,128)(2,1)S(1)} %copy-done.1, s32[8,32,128]{2,1,0:T(8,128)S(1)} %copy-done, ...), kind=kLoop, calls=%fused_computation.65 | loop fusion | flops 360448 | bytes 794624 | tf_op jit(solution)/shard_map/mul | solution.py:177
  (86 shorter events, 0.9 us)
Async XLA Ops:
  6.7 14.2 %all-to-all-start = ((f32[16,1,1792]{2,1,0:T(1,128)}), f32[16,1,1792]{2,1,0:T(1,128)S(1)}, u32[]{:S(2)}, u32[]{:S(2)}) async-start(f32[16,1,1792]{2,1,0:T(1,128)} %reshape.16), calls=%async_computation | async-start | bytes 229376 | tf_op jit(solution)/shard_map/all_to_all | solution.py:138
  70.9 0.9 %copy-start = (s32[8,32,128]{2,1,0:T(8,128)S(1)}, s32[8,32,128]{2,1,0:T(8,128)}, u32[]{:S(2)}) copy-start(s32[8,32,128]{2,1,0:T(8,128)} %refs_6_.1) | copy-start | bytes 393220
  71.0 0.9 %copy-start.1 = (bf16[8,32,128]{2,1,0:T(8,128)(2,1)S(1)}, bf16[8,32,128]{2,1,0:T(8,128)(2,1)}, u32[]{:S(2)}) copy-start(bf16[8,32,128]{2,1,0:T(8,128)(2,1)} %refs_1_.1) | copy-start | bytes 196612
  71.0 0.9 %copy-start.2 = (bf16[8,32,128]{2,1,0:T(8,128)(2,1)S(1)}, bf16[8,32,128]{2,1,0:T(8,128)(2,1)}, u32[]{:S(2)}) copy-start(bf16[8,32,128]{2,1,0:T(8,128)(2,1)} %refs_5_.1) | copy-start | bytes 196612
  71.0 1.0 %copy-start.3 = (f32[8,32,128]{2,1,0:T(8,128)S(1)}, f32[8,32,128]{2,1,0:T(8,128)}, u32[]{:S(2)}) copy-start(f32[8,32,128]{2,1,0:T(8,128)} %get-tuple-element.17) | copy-start | bytes 393220
  71.0 1.1 %copy-start.4 = (f32[8,32,128]{2,1,0:T(8,128)S(1)}, f32[8,32,128]{2,1,0:T(8,128)}, u32[]{:S(2)}) copy-start(f32[8,32,128]{2,1,0:T(8,128)} %get-tuple-element.18) | copy-start | bytes 393220
  71.0 1.1 %copy-start.5 = (f32[8,32,128]{2,1,0:T(8,128)S(1)}, f32[8,32,128]{2,1,0:T(8,128)}, u32[]{:S(2)}) copy-start(f32[8,32,128]{2,1,0:T(8,128)} %get-tuple-element.20) | copy-start | bytes 393220

commit v5 on v4

--- a/solution.py
+++ b/solution.py
@@ -15,13 +15,15 @@
     return pltpu.roll(values, shift % length, axis)
 
 
-def block_solve(lower_band, upper_band, excess, sources, axis):
+def block_solve(lower_band, upper_band, excess, sources, axis, weights=None):
     length = lower_band.shape[axis]
     stride = 1
     while stride < length:
         inverse = 1.0 / (excess - lower_band - upper_band)
         left_weight = -lower_band * shifted(inverse, stride, axis)
         right_coefficient = -upper_band * shifted(inverse, -stride, axis)
+        if weights is not None:
+            weights.append((left_weight, right_coefficient))
         new_lower = left_weight * shifted(lower_band, stride, axis)
         new_upper = right_coefficient * shifted(upper_band, -stride, axis)
         excess = (
@@ -38,6 +40,8 @@
         lower_band, upper_band = (new_lower, new_upper)
         stride = stride * 2
     diagonal = excess - lower_band - upper_band
+    if weights is not None:
+        weights.append(diagonal)
     return [member / diagonal for member in sources]
 
 
@@ -106,6 +110,96 @@
     )(*inputs)
 
 
+def lat_matrix_kernel(kappa_ref, mask_ref, lon_kappa_ref, u_out, w_out, left_out, right_out,
+                      diagonal_out, edge_out, scale_out):
+    axis = 1
+    wet = mask_ref[...].astype(jnp.float32)
+    lat_kappa = kappa_ref[...].astype(jnp.float32)
+    scale_out[...] = wet * 4.0 * jnp.sqrt(jnp.sqrt(lon_kappa_ref[...].astype(jnp.float32) * lat_kappa))
+    weight = lat_kappa * wet
+    shape = wet.shape
+    length = shape[axis]
+    position = lax.broadcasted_iota(jnp.int32, shape, axis)
+    last = position == length - 1
+    right_face = jnp.where(last, 0.0, weight * shifted(wet, -1, axis))
+    left_face = shifted(right_face, 1, axis)
+    weights = []
+    from_left, from_right = block_solve(
+        -left_face,
+        -right_face,
+        jnp.ones(shape, jnp.float32),
+        [jnp.where(position == 0, 1.0, 0.0), jnp.where(last, 1.0, 0.0)],
+        axis,
+        weights,
+    )
+    u_out[...] = from_left
+    w_out[...] = from_right
+    for step, (left_weight, right_coefficient) in enumerate(weights[:-1]):
+        left_out[step] = left_weight
+        right_out[step] = right_coefficient
+    diagonal_out[...] = weights[-1]
+    entries = [
+        None,
+        shifted(wet * from_left, 1, axis),
+        shifted(wet * from_right, 2, axis),
+        shifted(weight, 4, axis),
+        shifted(from_left, 4 + 1, axis),
+        shifted(from_right, 4 + 2, axis),
+    ]
+    edge = entries[1]
+    for k in range(2, 6):
+        edge = jnp.where(position == k, entries[k], edge)
+    edge_out[...] = lax.slice_in_dim(edge, 0, 8, axis=axis)
+
+
+def lat_rhs_kernel(p_ref, u_ref, w_ref, before_ref, here_ref, mask_ref, left_ref, right_ref,
+                   diagonal_ref, matrix_edge_ref, p_out, edge_out):
+    axis = 1
+    values = p_ref[...] - u_ref[...] * before_ref[...] + w_ref[...] * here_ref[...]
+    length = values.shape[axis]
+    stride = 1
+    step = 0
+    while stride < length:
+        values = (
+            values
+            + left_ref[step] * shifted(values, stride, axis)
+            + right_ref[step] * shifted(values, -stride, axis)
+        )
+        stride = stride * 2
+        step = step + 1
+    particular = values / diagonal_ref[...]
+    p_out[...] = particular
+    wet = mask_ref[...].astype(jnp.float32)
+    position = lax.broadcasted_iota(jnp.int32, values.shape, axis)
+    edge = jnp.where(position == 0, wet * particular, shifted(particular, 4 + 3, axis))
+    edge = lax.slice_in_dim(edge, 0, 8, axis=axis)
+    row = lax.broadcasted_iota(jnp.int32, edge.shape, axis)
+    edge_out[...] = jnp.where((row == 0) | (row == 6), edge, matrix_edge_ref[...])
+
+
+def lat_matrix(kappa_lat, sea_mask, kappa_lon):
+    shape = kappa_lat.shape
+    steps = (shape[1] - 1).bit_length()
+    full = jax.ShapeDtypeStruct(shape, jnp.float32)
+    stacked = jax.ShapeDtypeStruct((steps,) + shape, jnp.float32)
+    edge = jax.ShapeDtypeStruct((shape[0], 8, shape[2]), jnp.float32)
+    return pl.pallas_call(
+        lat_matrix_kernel,
+        out_shape=(full, full, stacked, stacked, full, edge, full),
+    )(kappa_lat, sea_mask, kappa_lon)
+
+
+def lat_rhs(*inputs):
+    shape = inputs[0].shape
+    return pl.pallas_call(
+        lat_rhs_kernel,
+        out_shape=(
+            jax.ShapeDtypeStruct(shape, jnp.float32),
+            jax.ShapeDtypeStruct((shape[0], 8, shape[2]), jnp.float32),
+        ),
+    )(*inputs)
+
+
 def circular_solve(lower_band, upper_band, excess, sources):
     devices = lower_band.shape[0]
     stride = 1
@@ -165,16 +259,14 @@
 
 def shards(source, kappa_lon, kappa_lat, sea_mask):
     p_lon, u_lon, w_lon, edge_lon = local_pass(2, (source, kappa_lon, sea_mask))
+    u_lat, w_lat, left, right, diagonal, matrix_edge, scale = lat_matrix(kappa_lat, sea_mask, kappa_lon)
     before, here = interface_flux(edge_lon, 2, "lon", True, "all_to_all")
-    p_lat, u_lat, w_lat, edge_lat = local_pass(
-        1, (p_lon, u_lon, w_lon, before[:, :, None], here[:, :, None], kappa_lat, sea_mask)
+    p_lat, edge_lat = lat_rhs(
+        p_lon, u_lon, w_lon, before[:, :, None], here[:, :, None], sea_mask,
+        left, right, diagonal, matrix_edge,
     )
     before, here = interface_flux(edge_lat, 1, "lat", False, "all_gather")
-    lat_pass = p_lat - u_lat * before[:, None, :] + w_lat * here[:, None, :]
-    wet_cells = sea_mask.astype(jnp.float32)
-    lon_kappa = kappa_lon.astype(jnp.float32)
-    lat_kappa = kappa_lat.astype(jnp.float32)
-    return wet_cells * 4.0 * jnp.sqrt(jnp.sqrt(lon_kappa * lat_kappa)) * lat_pass
+    return scale * (p_lat - u_lat * before[:, None, :] + w_lat * here[:, None, :])
 
 
 def solution(mesh):

time: 73.2 us -> 72.5 us (level)
  waiting for transfers between devices: 6.61 us -> 3.85 us
  Pallas kernels: 7.64 us -> 10 us
    pallas_call x0 -> x2, Pallas kernels: none -> 5.3 us  [the longest x1 2.77 us: lat_matrix(): pl.pallas_call(lat_matrix_kernel, out_shape=(full, full, stacked, stacked...]
    pallas_call x2 -> x1, Pallas kernels: 7.64 us -> 4.74 us  [local_pass(): pl.pallas_call(functools.partial(pass_kernel, axis, corrected), out_shape...]
    all_to_all x1, waiting for transfers between devices: 6.61 us -> 3.85 us  [interface_flux(): gathered = lax.all_to_all(copies, mesh_axis, 0, 0, tiled=True)]
    unnamed x15 -> x11, local copies, waits for them, and re-layouts: 2.1 us -> 2.03 us
  transfers between devices with their start and end apart: 1 -> 1, of which waited for: 1 -> 1; matrix products, arithmetic and copies ran while one was open for 0% -> 0% of each run, Pallas kernels for 0% -> 4%
where the time goes in v5:
time: 72.5 us; the launch traced here: 72.2 us
  blocking collectives  40.6 us (56%)
  Pallas kernels  10 us (14%)
  starting transfers between devices  7.57 us (10%)
  local copies, waits for them, and re-layouts  6.5 us (9%)
  waiting for transfers between devices  3.85 us (5%)
  other arithmetic  2.76 us (4%)
  between operations  0.8 us (1%)
    all_gather x1, blocking collectives, interface_flux(): gathered = lax.all_gather(terms[None], mesh_axis, axis=0, tiled=True)  40.6 us
    all_to_all x1, starting transfers between devices, interface_flux(): gathered = lax.all_to_all(copies, mesh_axis, 0, 0, tiled=True)  7.57 us
    pallas_call x1, Pallas kernels, local_pass(): pl.pallas_call(functools.partial(pass_kernel, axis, corrected), out_shape...  4.74 us
    all_to_all x1, waiting for transfers between devices, interface_flux(): gathered = lax.all_to_all(copies, mesh_axis, 0, 0, tiled=True)  3.85 us
    pallas_call x1, Pallas kernels, lat_matrix(): pl.pallas_call(lat_matrix_kernel, out_shape=(full, full, stacked, stacked...  2.77 us
    pallas_call x1, Pallas kernels, lat_rhs(): pl.pallas_call(lat_rhs_kernel, out_shape=(jax.ShapeDtypeStruct(shape, jnp...  2.53 us
    unnamed x11, local copies, waits for them, and re-layouts  2.03 us
    slice x2, local copies, waits for them, and re-layouts, interface_flux(): terms = lax.slice_in_dim(edge, 0, TERMS, axis=axis)  1.78 us
  transfers between devices with their start and end apart: 1, of which 1 were waited for; matrix products, arithmetic and copies ran while one was open for 0% of the time, Pallas kernels for 4%

profile of v5, /device:TPU:1, one launch (start us, length us, event | category | flops | bytes accessed | tf_op | source)
XLA Modules:
  0.0 72.2 jit_solution(7472988124246272000)
XLA Ops:
  0.0 4.7 %shard_map.47 = (f32[8,32,128]{2,1,0:T(8,128)}, f32[8,32,128]{2,1,0:T(8,128)}, f32[8,32,128]{2,1,0:T(8,128)}, f32[8,32,128]{2,1,0:T(8,128)}) custom-call(f32[8,32,128]{2,1,0:T(8,128)} %refs_0_.1, bf16[8,32,128]{2,1,0:T(8,128)(2,1)} %refs_1_.1, s32[8,32,128]{2,1,0:T(8,128)} %mask_ref.3), custom_call_target="tpu_custom_call" | custom-call | tf_op jit(solution)/shard_map/pallas_call | solution.py:102
  4.7 1.0 %copy.29 = f32[8,32,7]{1,0,2:T(8,128)S(1)} copy(f32[8,32,7]{2,1,0:T(8,128)} %bitcast.140) | data formatting | bytes 14336 | tf_op jit(solution)/shard_map/slice | solution.py:228
  5.8 0.9 %reshape.16 = f32[16,1,1792]{2,1,0:T(1,128)} reshape(f32[16,7,8,32]{3,2,1,0:T(8,128)S(1)} %broadcast_bitcast_fusion) | data formatting | bytes 229376
  6.7 7.6 %all-to-all-start = ((f32[16,1,1792]{2,1,0:T(1,128)}), f32[16,1,1792]{2,1,0:T(1,128)S(1)}, u32[]{:S(2)}, u32[]{:S(2)}) async-start(f32[16,1,1792]{2,1,0:T(1,128)} %reshape.16), calls=%async_computation | async-start | bytes 229376 | tf_op jit(solution)/shard_map/all_to_all | solution.py:232
  14.3 2.8 %shard_map.46 = (f32[8,32,128]{2,1,0:T(8,128)}, f32[8,32,128]{2,1,0:T(8,128)}, f32[5,8,32,128]{3,2,1,0:T(8,128)}, f32[5,8,32,128]{3,2,1,0:T(8,128)}, f32[8,32,12...) custom-call(bf16[8,32,128]{2,1,0:T(8,128)(2,1)} %kappa_ref.1, s32[8,32,128]{2,1,0:T(8,128)} %mask_ref.3, ...), custom_call_target="tpu_custom_call" | custom-call | tf_op jit(solution)/shard_map/pallas_call | solution.py:186
  17.1 3.9 %all-to-all-done = f32[16,1,1792]{2,1,0:T(1,128)S(1)} async-done(((f32[16,1,1792]{2,1,0:T(1,128)}), f32[16,1,1792]{2,1,0:T(1,128)S(1)}, u32[]{:S(2)}, u32[]{:S(2)}) %all-to-all-start) | async-done | bytes 114720 | tf_op jit(solution)/shard_map/all_to_all | solution.py:232
  20.9 0.5 broadcast.12
  21.4 0.8 %reduce = f32[16,1792]{1,0:T(8,128)S(1)} reduce(f32[16,1,1792]{2,1,0:T(1,128)S(1)} %all-to-all-done, f32[]{:T(128)} %broadcast.12), dimensions={1}, to_apply=%all_to_all.3.reduce_sub_computation | reduce | bytes 229380 | tf_op jit(solution)/shard_map/all_to_all | solution.py:232
  22.2 0.2 reshape.17
  22.4 0.1 subtract_divide_fusion.8
  22.7 0.1 subtract_divide_fusion.7
  22.9 0.1 subtract_divide_fusion.6
  23.1 0.1 subtract_divide_fusion.5
  23.2 0.1 add_divide_fusion.1
  23.3 0.8 %copy.37.before_ref = f32[8,32,1]{2,1,0:T(8,128)} copy(f32[8,32,1]{1,0,2:T(8,128)S(1)} %get-tuple-element.138) | data formatting | bytes 2048 | tf_op jit(solution)/shard_map/broadcast_in_dim;squeeze | solution.py:265
  24.1 0.8 %copy.38.here_ref = f32[8,32,1]{2,1,0:T(8,128)} copy(f32[8,32,1]{1,0,2:T(8,128)S(1)} %get-tuple-element.137) | data formatting | bytes 2048 | tf_op jit(solution)/shard_map/broadcast_in_dim;squeeze | solution.py:265
  24.9 2.5 %shard_map.48 = (f32[8,32,128]{2,1,0:T(8,128)}, f32[8,8,128]{2,1,0:T(8,128)}) custom-call(f32[8,32,128]{2,1,0:T(8,128)} %get-tuple-element.19.p_ref, f32[8,32,128]{2,1,0:T(8,128)} %get-tuple-element.20.u_ref, f32[8,32,128]{2,1,0:T(8,128)} %get-tuple-element.21.w_ref, f32[8,32,1]{2,1,0:T(8,128)} %copy.37.before_ref, f32[8,32,1]{2,1,0:T(8,128)} %copy.38.here_ref, ...), custom_call_target="tpu_custom_call" | custom-call | tf_op jit(solution)/shard_map/pallas_call | solution.py:194
  27.4 0.8 %copy.39 = f32[8,7,128]{2,0,1:T(8,128)S(1)} copy(f32[8,7,128]{2,1,0:T(8,128)} %bitcast.141) | data formatting | bytes 57344 | tf_op jit(solution)/shard_map/slice | solution.py:228
  28.2 40.6 %all-gather = f32[256,7,128]{2,0,1:T(8,128)S(1)} all-gather(f32[8,7,128]{2,0,1:T(8,128)S(1)} %copy.39), channel_id=2, replica_groups=mesh['lat'=32,'lon'=16] {'lat'}, dimensions={0}, use_global_device_ids=true | all-gather | bytes 946176 | tf_op jit(solution)/shard_map/all_gather | solution.py:234
  68.9 0.2 subtract_divide_fusion.4
  69.1 0.1 fusion.8
  69.3 0.1 subtract_divide_fusion.3
  69.5 0.1 fusion.12
  69.6 0.1 subtract_divide_fusion.2
  69.8 0.1 fusion.16
  70.0 0.1 subtract_divide_fusion.1
  70.2 0.1 subtract_divide_fusion
  70.4 0.0 copy-start
  70.4 0.0 copy-start.1
  70.4 0.0 copy-start.2
  70.4 0.0 copy-start.3
  70.4 0.1 add_divide_fusion
  70.5 0.8 %copy-done = f32[8,32,128]{2,1,0:T(8,128)S(1)} copy-done((f32[8,32,128]{2,1,0:T(8,128)S(1)}, f32[8,32,128]{2,1,0:T(8,128)}, u32[]{:S(2)}) %copy-start) | copy-done | bytes 131096
  71.3 0.1 copy-done.1
  71.4 0.1 copy-done.2
  71.4 0.1 copy-done.3
  71.5 0.7 add_multiply_fusion
  (86 shorter events, 0.8 us)
Async XLA Ops:
  6.7 14.2 %all-to-all-start = ((f32[16,1,1792]{2,1,0:T(1,128)}), f32[16,1,1792]{2,1,0:T(1,128)S(1)}, u32[]{:S(2)}, u32[]{:S(2)}) async-start(f32[16,1,1792]{2,1,0:T(1,128)} %reshape.16), calls=%async_computation | async-start | bytes 229376 | tf_op jit(solution)/shard_map/all_to_all | solution.py:232
  70.4 0.9 %copy-start = (f32[8,32,128]{2,1,0:T(8,128)S(1)}, f32[8,32,128]{2,1,0:T(8,128)}, u32[]{:S(2)}) copy-start(f32[8,32,128]{2,1,0:T(8,128)} %get-tuple-element.28) | copy-start | bytes 393220
  70.4 1.0 %copy-start.1 = (f32[8,32,128]{2,1,0:T(8,128)S(1)}, f32[8,32,128]{2,1,0:T(8,128)}, u32[]{:S(2)}) copy-start(f32[8,32,128]{2,1,0:T(8,128)} %get-tuple-element.30) | copy-start | bytes 393220
  70.4 1.0 %copy-start.2 = (f32[8,32,128]{2,1,0:T(8,128)S(1)}, f32[8,32,128]{2,1,0:T(8,128)}, u32[]{:S(2)}) copy-start(f32[8,32,128]{2,1,0:T(8,128)} %get-tuple-element.18) | copy-start | bytes 393220
  70.4 1.1 %copy-start.3 = (f32[8,32,128]{2,1,0:T(8,128)S(1)}, f32[8,32,128]{2,1,0:T(8,128)}, u32[]{:S(2)}) copy-start(f32[8,32,128]{2,1,0:T(8,128)} %get-tuple-element.27) | copy-start | bytes 393220

commit v6 on v5

--- a/solution.py
+++ b/solution.py
@@ -111,7 +111,7 @@
 
 
 def lat_matrix_kernel(kappa_ref, mask_ref, lon_kappa_ref, u_out, w_out, left_out, right_out,
-                      diagonal_out, edge_out, scale_out):
+                      diagonal_out, edge_out, scale_out, weight_scratch):
     axis = 1
     wet = mask_ref[...].astype(jnp.float32)
     lat_kappa = kappa_ref[...].astype(jnp.float32)
@@ -138,24 +138,19 @@
         left_out[step] = left_weight
         right_out[step] = right_coefficient
     diagonal_out[...] = weights[-1]
-    entries = [
-        None,
-        shifted(wet * from_left, 1, axis),
-        shifted(wet * from_right, 2, axis),
-        shifted(weight, 4, axis),
-        shifted(from_left, 4 + 1, axis),
-        shifted(from_right, 4 + 2, axis),
-    ]
-    edge = entries[1]
-    for k in range(2, 6):
-        edge = jnp.where(position == k, entries[k], edge)
-    edge_out[...] = lax.slice_in_dim(edge, 0, 8, axis=axis)
-
-
-def lat_rhs_kernel(p_ref, u_ref, w_ref, before_ref, here_ref, mask_ref, left_ref, right_ref,
+    weight_scratch[...] = weight
+    head_wet = mask_ref[:, 0, :].astype(jnp.float32)
+    edge_out[0] = head_wet * u_out[:, 0, :]
+    edge_out[1] = head_wet * w_out[:, 0, :]
+    edge_out[2] = weight_scratch[:, length - 1, :]
+    edge_out[3] = u_out[:, length - 1, :]
+    edge_out[4] = w_out[:, length - 1, :]
+
+
+def lat_rhs_kernel(p_ref, u_ref, w_ref, flux_ref, mask_ref, left_ref, right_ref,
                    diagonal_ref, matrix_edge_ref, p_out, edge_out):
     axis = 1
-    values = p_ref[...] - u_ref[...] * before_ref[...] + w_ref[...] * here_ref[...]
+    values = p_ref[...] - u_ref[...] * flux_ref[0] + w_ref[...] * flux_ref[1]
     length = values.shape[axis]
     stride = 1
     step = 0
@@ -167,14 +162,10 @@
         )
         stride = stride * 2
         step = step + 1
-    particular = values / diagonal_ref[...]
-    p_out[...] = particular
-    wet = mask_ref[...].astype(jnp.float32)
-    position = lax.broadcasted_iota(jnp.int32, values.shape, axis)
-    edge = jnp.where(position == 0, wet * particular, shifted(particular, 4 + 3, axis))
-    edge = lax.slice_in_dim(edge, 0, 8, axis=axis)
-    row = lax.broadcasted_iota(jnp.int32, edge.shape, axis)
-    edge_out[...] = jnp.where((row == 0) | (row == 6), edge, matrix_edge_ref[...])
+    p_out[...] = values / diagonal_ref[...]
+    edge_out[0] = mask_ref[:, 0, :].astype(jnp.float32) * p_out[:, 0, :]
+    edge_out[1:TERMS - 1] = matrix_edge_ref[...]
+    edge_out[TERMS - 1] = p_out[:, length - 1, :]
 
 
 def lat_matrix(kappa_lat, sea_mask, kappa_lon):
@@ -182,10 +173,11 @@
     steps = (shape[1] - 1).bit_length()
     full = jax.ShapeDtypeStruct(shape, jnp.float32)
     stacked = jax.ShapeDtypeStruct((steps,) + shape, jnp.float32)
-    edge = jax.ShapeDtypeStruct((shape[0], 8, shape[2]), jnp.float32)
+    edge = jax.ShapeDtypeStruct((TERMS - 2, shape[0], shape[2]), jnp.float32)
     return pl.pallas_call(
         lat_matrix_kernel,
         out_shape=(full, full, stacked, stacked, full, edge, full),
+        scratch_shapes=[pltpu.VMEM(shape, jnp.float32)],
     )(kappa_lat, sea_mask, kappa_lon)
 
 
@@ -195,7 +187,7 @@
         lat_rhs_kernel,
         out_shape=(
             jax.ShapeDtypeStruct(shape, jnp.float32),
-            jax.ShapeDtypeStruct((shape[0], 8, shape[2]), jnp.float32),
+            jax.ShapeDtypeStruct((TERMS, shape[0], shape[2]), jnp.float32),
         ),
     )(*inputs)
 
@@ -225,7 +217,7 @@
 
 
 def interface_flux(edge, axis, mesh_axis, periodic, exchange):
-    terms = lax.slice_in_dim(edge, 0, TERMS, axis=axis)
+    terms = lax.slice_in_dim(edge, 0, TERMS, axis=axis) if edge.shape[axis] > TERMS else edge
     devices = lax.axis_size(mesh_axis)
     if exchange == "all_to_all":
         copies = jnp.broadcast_to(terms[None], (devices,) + terms.shape)
@@ -262,10 +254,10 @@
     u_lat, w_lat, left, right, diagonal, matrix_edge, scale = lat_matrix(kappa_lat, sea_mask, kappa_lon)
     before, here = interface_flux(edge_lon, 2, "lon", True, "all_to_all")
     p_lat, edge_lat = lat_rhs(
-        p_lon, u_lon, w_lon, before[:, :, None], here[:, :, None], sea_mask,
+        p_lon, u_lon, w_lon, jnp.stack([before, here], 0)[..., None], sea_mask,
         left, right, diagonal, matrix_edge,
     )
-    before, here = interface_flux(edge_lat, 1, "lat", False, "all_gather")
+    before, here = interface_flux(edge_lat, 0, "lat", False, "all_gather")
     return scale * (p_lat - u_lat * before[:, None, :] + w_lat * here[:, None, :])
 
 

time: 72.5 us -> 71.3 us (0.983)
  local copies, waits for them, and re-layouts: 6.5 us -> 5.09 us
    another operation x3 -> x0, local copies, waits for them, and re-layouts: 1.56 us -> none  [the longest x2 0.79 us: shards(): here[:, :, None]]
    broadcast_in_dim x0 -> x1, local copies, waits for them, and re-layouts: none -> 0.87 us  [shards(): jnp.stack([before, here], 0)[..., None]]
    slice x2 -> x1, local copies, waits for them, and re-layouts: 1.78 us -> 1.02 us  [interface_flux(): lax.slice_in_dim(edge, 0, TERMS, axis=axis)]
where the time goes in v6:
time: 71.3 us; the launch traced here: 71 us
  blocking collectives  40.9 us (57%)
  Pallas kernels  10.1 us (14%)
  starting transfers between devices  7.57 us (11%)
  local copies, waits for them, and re-layouts  5.09 us (7%)
  waiting for transfers between devices  3.76 us (5%)
  other arithmetic  2.78 us (4%)
  between operations  0.81 us (1%)
    all_gather x1, blocking collectives, interface_flux(): gathered = lax.all_gather(terms[None], mesh_axis, axis=0, tiled=True)  40.9 us
    all_to_all x1, starting transfers between devices, interface_flux(): gathered = lax.all_to_all(copies, mesh_axis, 0, 0, tiled=True)  7.57 us
    pallas_call x1, Pallas kernels, local_pass(): pl.pallas_call(functools.partial(pass_kernel, axis, corrected), out_shape...  4.74 us
    all_to_all x1, waiting for transfers between devices, interface_flux(): gathered = lax.all_to_all(copies, mesh_axis, 0, 0, tiled=True)  3.76 us
    pallas_call x1, Pallas kernels, lat_matrix(): pl.pallas_call(lat_matrix_kernel, out_shape=(full, full, stacked, stacked...  2.86 us
    pallas_call x1, Pallas kernels, lat_rhs(): pl.pallas_call(lat_rhs_kernel, out_shape=(jax.ShapeDtypeStruct(shape, jnp...  2.51 us
    unnamed x11, local copies, waits for them, and re-layouts  2.03 us
  transfers between devices with their start and end apart: 1, of which 1 were waited for; matrix products, arithmetic and copies ran while one was open for 0% of the time, Pallas kernels for 4%

profile of v6, /device:TPU:1, one launch (start us, length us, event | category | flops | bytes accessed | tf_op | source)
XLA Modules:
  0.0 71.0 jit_solution(13630363049246704204)
XLA Ops:
  0.0 4.7 %shard_map.47 = (f32[8,32,128]{2,1,0:T(8,128)}, f32[8,32,128]{2,1,0:T(8,128)}, f32[8,32,128]{2,1,0:T(8,128)}, f32[8,32,128]{2,1,0:T(8,128)}) custom-call(f32[8,32,128]{2,1,0:T(8,128)} %refs_0_.1, bf16[8,32,128]{2,1,0:T(8,128)(2,1)} %refs_1_.1, s32[8,32,128]{2,1,0:T(8,128)} %mask_ref.3), custom_call_target="tpu_custom_call" | custom-call | tf_op jit(solution)/shard_map/pallas_call | solution.py:102
  4.7 1.0 %copy.24 = f32[8,32,7]{1,0,2:T(8,128)S(1)} copy(f32[8,32,7]{2,1,0:T(8,128)} %bitcast.145) | data formatting | bytes 14336 | tf_op jit(solution)/shard_map/slice | solution.py:220
  5.8 0.9 %reshape.16 = f32[16,1,1792]{2,1,0:T(1,128)} reshape(f32[16,7,8,32]{3,2,1,0:T(8,128)S(1)} %broadcast_bitcast_fusion) | data formatting | bytes 229376
  6.7 7.6 %all-to-all-start = ((f32[16,1,1792]{2,1,0:T(1,128)}), f32[16,1,1792]{2,1,0:T(1,128)S(1)}, u32[]{:S(2)}, u32[]{:S(2)}) async-start(f32[16,1,1792]{2,1,0:T(1,128)} %reshape.16), calls=%async_computation | async-start | bytes 229376 | tf_op jit(solution)/shard_map/all_to_all | solution.py:224
  14.3 2.9 %shard_map.46 = (f32[8,32,128]{2,1,0:T(8,128)}, f32[8,32,128]{2,1,0:T(8,128)}, f32[5,8,32,128]{3,2,1,0:T(8,128)}, f32[5,8,32,128]{3,2,1,0:T(8,128)}, f32[8,32,12...) custom-call(bf16[8,32,128]{2,1,0:T(8,128)(2,1)} %kappa_ref.1, s32[8,32,128]{2,1,0:T(8,128)} %mask_ref.3, ...), custom_call_target="tpu_custom_call" | custom-call | tf_op jit(solution)/shard_map/pallas_call | solution.py:177
  17.2 3.8 %all-to-all-done = f32[16,1,1792]{2,1,0:T(1,128)S(1)} async-done(((f32[16,1,1792]{2,1,0:T(1,128)}), f32[16,1,1792]{2,1,0:T(1,128)S(1)}, u32[]{:S(2)}, u32[]{:S(2)}) %all-to-all-start) | async-done | bytes 114720 | tf_op jit(solution)/shard_map/all_to_all | solution.py:224
  20.9 0.5 broadcast.12
  21.4 0.8 %reduce = f32[16,1792]{1,0:T(8,128)S(1)} reduce(f32[16,1,1792]{2,1,0:T(1,128)S(1)} %all-to-all-done, f32[]{:T(128)} %broadcast.12), dimensions={1}, to_apply=%all_to_all.3.reduce_sub_computation | reduce | bytes 229380 | tf_op jit(solution)/shard_map/all_to_all | solution.py:224
  22.3 0.2 reshape.17
  22.5 0.1 subtract_divide_fusion.8
  22.7 0.1 subtract_divide_fusion.7
  23.0 0.1 subtract_divide_fusion.6
  23.1 0.1 subtract_divide_fusion.5
  23.3 0.1 add_divide_fusion.1
  23.4 0.9 %copy.32.flux_ref = f32[2,8,32,1]{3,2,1,0:T(8,128)} copy(f32[2,8,32,1]{2,1,0,3:T(8,128)S(1)} %maximum_bitcast_fusion) | data formatting | bytes 4096 | tf_op jit(solution)/shard_map/broadcast_in_dim | solution.py:257
  24.3 2.5 %shard_map.48 = (f32[8,32,128]{2,1,0:T(8,128)}, f32[7,8,128]{2,1,0:T(8,128)}) custom-call(f32[8,32,128]{2,1,0:T(8,128)} %get-tuple-element.19.p_ref, f32[8,32,128]{2,1,0:T(8,128)} %get-tuple-element.20.u_ref, f32[8,32,128]{2,1,0:T(8,128)} %get-tuple-element.21.w_ref, f32[2,8,32,1]{3,2,1,0:T(8,128)} %copy.32.flux_ref, s32[8,32,128]{2,1,0:T(8,128)} %mask_ref.3, ...), custom_call_target="tpu_custom_call" | custom-call | tf_op jit(solution)/shard_map/pallas_call | solution.py:186
  26.8 40.9 %all-gather = f32[224,8,128]{2,1,0:T(8,128)S(1)} all-gather(f32[7,8,128]{2,1,0:T(8,128)} %get-tuple-element.29), channel_id=2, replica_groups=mesh['lat'=32,'lon'=16] {'lat'}, dimensions={0}, use_global_device_ids=true | all-gather | bytes 946176 | tf_op jit(solution)/shard_map/all_gather | solution.py:226
  67.7 0.2 subtract_divide_fusion.4
  68.0 0.1 fusion.8
  68.2 0.1 subtract_divide_fusion.3
  68.3 0.1 fusion.12
  68.5 0.1 subtract_divide_fusion.2
  68.6 0.1 fusion.16
  68.8 0.1 subtract_divide_fusion.1
  69.0 0.1 subtract_divide_fusion
  69.2 0.0 copy-start
  69.2 0.0 copy-start.1
  69.2 0.0 copy-start.2
  69.3 0.0 copy-start.3
  69.3 0.1 add_divide_fusion
  69.4 0.8 %copy-done = f32[8,32,128]{2,1,0:T(8,128)S(1)} copy-done((f32[8,32,128]{2,1,0:T(8,128)S(1)}, f32[8,32,128]{2,1,0:T(8,128)}, u32[]{:S(2)}) %copy-start) | copy-done | bytes 131096
  70.1 0.1 copy-done.1
  70.2 0.1 copy-done.2
  70.3 0.1 copy-done.3
  70.3 0.7 add_multiply_fusion
  (87 shorter events, 0.9 us)
Async XLA Ops:
  6.7 14.2 %all-to-all-start = ((f32[16,1,1792]{2,1,0:T(1,128)}), f32[16,1,1792]{2,1,0:T(1,128)S(1)}, u32[]{:S(2)}, u32[]{:S(2)}) async-start(f32[16,1,1792]{2,1,0:T(1,128)} %reshape.16), calls=%async_computation | async-start | bytes 229376 | tf_op jit(solution)/shard_map/all_to_all | solution.py:224
  69.2 0.9 %copy-start = (f32[8,32,128]{2,1,0:T(8,128)S(1)}, f32[8,32,128]{2,1,0:T(8,128)}, u32[]{:S(2)}) copy-start(f32[8,32,128]{2,1,0:T(8,128)} %get-tuple-element.28) | copy-start | bytes 393220
  69.2 1.0 %copy-start.1 = (f32[8,32,128]{2,1,0:T(8,128)S(1)}, f32[8,32,128]{2,1,0:T(8,128)}, u32[]{:S(2)}) copy-start(f32[8,32,128]{2,1,0:T(8,128)} %get-tuple-element.30) | copy-start | bytes 393220
  69.2 1.0 %copy-start.2 = (f32[8,32,128]{2,1,0:T(8,128)S(1)}, f32[8,32,128]{2,1,0:T(8,128)}, u32[]{:S(2)}) copy-start(f32[8,32,128]{2,1,0:T(8,128)} %get-tuple-element.18) | copy-start | bytes 393220
  69.3 1.1 %copy-start.3 = (f32[8,32,128]{2,1,0:T(8,128)S(1)}, f32[8,32,128]{2,1,0:T(8,128)}, u32[]{:S(2)}) copy-start(f32[8,32,128]{2,1,0:T(8,128)} %get-tuple-element.27) | copy-start | bytes 393220

commit v7 on v6

--- a/solution.py
+++ b/solution.py
@@ -192,44 +192,50 @@
     )(*inputs)
 
 
-def circular_solve(lower_band, upper_band, excess, sources):
+def circular_solve(lower_band, upper_band, excess, sources, roll=jnp.roll):
     devices = lower_band.shape[0]
     stride = 1
     while stride < devices:
         inverse = 1.0 / (excess - lower_band - upper_band)
-        left_weight = -lower_band * jnp.roll(inverse, stride, 0)
-        right_coefficient = -upper_band * jnp.roll(inverse, -stride, 0)
-        new_lower = left_weight * jnp.roll(lower_band, stride, 0)
-        new_upper = right_coefficient * jnp.roll(upper_band, -stride, 0)
+        left_weight = -lower_band * roll(inverse, stride, 0)
+        right_coefficient = -upper_band * roll(inverse, -stride, 0)
+        new_lower = left_weight * roll(lower_band, stride, 0)
+        new_upper = right_coefficient * roll(upper_band, -stride, 0)
         excess = (
             excess
-            + left_weight * jnp.roll(excess, stride, 0)
-            + right_coefficient * jnp.roll(excess, -stride, 0)
+            + left_weight * roll(excess, stride, 0)
+            + right_coefficient * roll(excess, -stride, 0)
         )
         sources = (
             sources
-            + left_weight * jnp.roll(sources, stride, 0)
-            + right_coefficient * jnp.roll(sources, -stride, 0)
+            + left_weight * roll(sources, stride, 0)
+            + right_coefficient * roll(sources, -stride, 0)
         )
         lower_band, upper_band = (new_lower, new_upper)
         stride = stride * 2
     return sources / excess
 
 
-def interface_flux(edge, axis, mesh_axis, periodic, exchange):
-    terms = lax.slice_in_dim(edge, 0, TERMS, axis=axis) if edge.shape[axis] > TERMS else edge
-    devices = lax.axis_size(mesh_axis)
-    if exchange == "all_to_all":
-        copies = jnp.broadcast_to(terms[None], (devices,) + terms.shape)
-        gathered = lax.all_to_all(copies, mesh_axis, 0, 0, tiled=True)
-    else:
-        gathered = lax.all_gather(terms[None], mesh_axis, axis=0, tiled=True)
-    (head_p, head_u, head_w, tail_kappa, tail_u, tail_w, tail_p) = (
-        lax.index_in_dim(gathered, k, axis + 1, keepdims=False) for k in range(TERMS)
-    )
+def leading_roll(values, shift, axis):
+    shift = shift % values.shape[axis]
+    if shift == 0:
+        return values
+    length = values.shape[axis]
+    return jnp.concatenate(
+        [
+            lax.slice_in_dim(values, length - shift, length, axis=axis),
+            lax.slice_in_dim(values, 0, length - shift, axis=axis),
+        ],
+        axis,
+    )
+
+
+def flux_system(terms, periodic, roll):
+    head_p, head_u, head_w, tail_kappa, tail_u, tail_w, tail_p = terms
+    devices = head_p.shape[0]
 
     def next_of(member):
-        return jnp.roll(member, -1, 0)
+        return roll(member, -1, 0)
 
     next_wet = jnp.where(next_of(head_u) > 0.0, 1.0, 0.0)
     face = tail_kappa * next_wet
@@ -240,9 +246,46 @@
     lower = -face * tail_u
     upper = -tail_kappa * next_of(head_w)
     diagonal = 1.0 + tail_kappa * next_of(head_u) + face * tail_w
-    flux = circular_solve(
-        lower, upper, diagonal + lower + upper, tail_kappa * next_of(head_p) - face * tail_p
-    )
+    return circular_solve(
+        lower, upper, diagonal + lower + upper, tail_kappa * next_of(head_p) - face * tail_p, roll
+    )
+
+
+def final_kernel(index_ref, gathered_ref, scale_ref, p_ref, u_ref, w_ref, out_ref, flux_scratch):
+    terms = [gathered_ref[:, k] for k in range(TERMS)]
+    flux_scratch[...] = flux_system(terms, False, leading_roll)
+    devices = flux_scratch.shape[0]
+    index = index_ref[0]
+    here = flux_scratch[index]
+    before = flux_scratch[(index + devices - 1) % devices]
+    out_ref[...] = scale_ref[...] * (
+        p_ref[...] - u_ref[...] * before[:, None, :] + w_ref[...] * here[:, None, :]
+    )
+
+
+def lat_final(edge, scale, p_lat, u_lat, w_lat):
+    gathered = lax.all_gather(edge[None], "lat", axis=0, tiled=True)
+    index = jnp.full((1,), lax.axis_index("lat"), jnp.int32)
+    vmem = pl.BlockSpec(memory_space=pltpu.VMEM)
+    return pl.pallas_call(
+        final_kernel,
+        out_shape=jax.ShapeDtypeStruct(p_lat.shape, jnp.float32),
+        in_specs=[pl.BlockSpec(memory_space=pltpu.SMEM)] + [vmem] * 5,
+        out_specs=vmem,
+        scratch_shapes=[pltpu.VMEM((gathered.shape[0],) + edge.shape[1:], jnp.float32)],
+    )(index, gathered, scale, p_lat, u_lat, w_lat)
+
+
+def interface_flux(edge, axis, mesh_axis, periodic, exchange):
+    terms = lax.slice_in_dim(edge, 0, TERMS, axis=axis) if edge.shape[axis] > TERMS else edge
+    devices = lax.axis_size(mesh_axis)
+    if exchange == "all_to_all":
+        copies = jnp.broadcast_to(terms[None], (devices,) + terms.shape)
+        gathered = lax.all_to_all(copies, mesh_axis, 0, 0, tiled=True)
+    else:
+        gathered = lax.all_gather(terms[None], mesh_axis, axis=0, tiled=True)
+    terms = [lax.index_in_dim(gathered, k, axis + 1, keepdims=False) for k in range(TERMS)]
+    flux = flux_system(terms, periodic, jnp.roll)
     index = lax.axis_index(mesh_axis)
     here = lax.dynamic_index_in_dim(flux, index, 0, keepdims=True)
     before = lax.dynamic_index_in_dim(flux, (index + devices - 1) % devices, 0, keepdims=True)
@@ -257,8 +300,7 @@
         p_lon, u_lon, w_lon, jnp.stack([before, here], 0)[..., None], sea_mask,
         left, right, diagonal, matrix_edge,
     )
-    before, here = interface_flux(edge_lat, 0, "lat", False, "all_gather")
-    return scale * (p_lat - u_lat * before[:, None, :] + w_lat * here[:, None, :])
+    return lat_final(edge_lat, scale, p_lat, u_lat, w_lat)
 
 
 def solution(mesh):

time: 71.3 us -> 73.4 us (1.029)
  Pallas kernels: 10.1 us -> 12.9 us
  blocking collectives: 40.9 us -> 43.6 us
  other arithmetic: 2.78 us -> 1.27 us
  local copies, waits for them, and re-layouts: 5.09 us -> 3.7 us
    pallas_call x0 -> x1, Pallas kernels: none -> 2.73 us  [lat_final(): pl.pallas_call(final_kernel, out_shape=jax.ShapeDtypeStruct(p_lat.shape,...]
    all_gather x1, blocking collectives: 40.9 us -> 43.6 us  [lat_final(): gathered = lax.all_gather(edge[None], 'lat', axis=0, tiled=True)]
    unnamed x11 -> x3, local copies, waits for them, and re-layouts: 2.03 us -> 1.08 us
where the time goes in v7:
time: 73.4 us; the launch traced here: 73.1 us
  blocking collectives  43.6 us (59%)
  Pallas kernels  12.9 us (18%)
  starting transfers between devices  7.57 us (10%)
  waiting for transfers between devices  3.73 us (5%)
  local copies, waits for them, and re-layouts  3.7 us (5%)
  other arithmetic  1.27 us (2%)
    all_gather x1, blocking collectives, lat_final(): gathered = lax.all_gather(edge[None], 'lat', axis=0, tiled=True)  43.6 us
    all_to_all x1, starting transfers between devices, interface_flux(): gathered = lax.all_to_all(copies, mesh_axis, 0, 0, tiled=True)  7.57 us
    pallas_call x1, Pallas kernels, local_pass(): pl.pallas_call(functools.partial(pass_kernel, axis, corrected), out_shape...  4.75 us
    all_to_all x1, waiting for transfers between devices, interface_flux(): gathered = lax.all_to_all(copies, mesh_axis, 0, 0, tiled=True)  3.73 us
    pallas_call x1, Pallas kernels, lat_matrix(): pl.pallas_call(lat_matrix_kernel, out_shape=(full, full, stacked, stacked...  2.91 us
    pallas_call x1, Pallas kernels, lat_final(): pl.pallas_call(final_kernel, out_shape=jax.ShapeDtypeStruct(p_lat.shape,...  2.73 us
    pallas_call x1, Pallas kernels, lat_rhs(): pl.pallas_call(lat_rhs_kernel, out_shape=(jax.ShapeDtypeStruct(shape, jnp...  2.52 us
  transfers between devices with their start and end apart: 1, of which 1 were waited for; matrix products, arithmetic and copies ran while one was open for 0% of the time, Pallas kernels for 4%

profile of v7, /device:TPU:1, one launch (start us, length us, event | category | flops | bytes accessed | tf_op | source)
XLA Modules:
  0.0 73.1 jit_solution(16797222668755935278)
XLA Ops:
  0.0 4.8 %shard_map.46 = (f32[8,32,128]{2,1,0:T(8,128)}, f32[8,32,128]{2,1,0:T(8,128)}, f32[8,32,128]{2,1,0:T(8,128)}, f32[8,32,128]{2,1,0:T(8,128)}) custom-call(f32[8,32,128]{2,1,0:T(8,128)} %refs_0_.1, bf16[8,32,128]{2,1,0:T(8,128)(2,1)} %lon_kappa_ref.1, s32[8,32,128]{2,1,0:T(8,128)} %mask_ref.3), custom_call_target="tpu_custom_call" | custom-call | tf_op jit(solution)/shard_map/pallas_call | solution.py:102
  4.8 1.0 %copy.12 = f32[8,32,7]{1,0,2:T(8,128)S(1)} copy(f32[8,32,7]{2,1,0:T(8,128)} %bitcast.73) | data formatting | bytes 14336 | tf_op jit(solution)/shard_map/slice | solution.py:280
  5.8 0.9 %reshape.8 = f32[16,1,1792]{2,1,0:T(1,128)} reshape(f32[16,7,8,32]{3,2,1,0:T(8,128)S(1)} %broadcast_bitcast_fusion) | data formatting | bytes 229376
  6.7 7.6 %all-to-all-start = ((f32[16,1,1792]{2,1,0:T(1,128)}), f32[16,1,1792]{2,1,0:T(1,128)S(1)}, u32[]{:S(2)}, u32[]{:S(2)}) async-start(f32[16,1,1792]{2,1,0:T(1,128)} %reshape.8), calls=%async_computation | async-start | bytes 229376 | tf_op jit(solution)/shard_map/all_to_all | solution.py:284
  14.3 2.9 %shard_map.47 = (f32[8,32,128]{2,1,0:T(8,128)}, f32[8,32,128]{2,1,0:T(8,128)}, f32[5,8,32,128]{3,2,1,0:T(8,128)}, f32[5,8,32,128]{3,2,1,0:T(8,128)}, f32[8,32,12...) custom-call(bf16[8,32,128]{2,1,0:T(8,128)(2,1)} %kappa_ref.1, s32[8,32,128]{2,1,0:T(8,128)} %mask_ref.3, ...), custom_call_target="tpu_custom_call" | custom-call | tf_op jit(solution)/shard_map/pallas_call | solution.py:177
  17.2 3.7 %all-to-all-done = f32[16,1,1792]{2,1,0:T(1,128)S(1)} async-done(((f32[16,1,1792]{2,1,0:T(1,128)}), f32[16,1,1792]{2,1,0:T(1,128)S(1)}, u32[]{:S(2)}, u32[]{:S(2)}) %all-to-all-start) | async-done | bytes 114720 | tf_op jit(solution)/shard_map/all_to_all | solution.py:284
  20.9 0.5 broadcast.3
  21.4 0.8 %reduce = f32[16,1792]{1,0:T(8,128)S(1)} reduce(f32[16,1,1792]{2,1,0:T(1,128)S(1)} %all-to-all-done, f32[]{:T(128)} %broadcast.3), dimensions={1}, to_apply=%all_to_all.3.reduce_sub_computation | reduce | bytes 229380 | tf_op jit(solution)/shard_map/all_to_all | solution.py:284
  22.3 0.2 reshape.9
  22.5 0.1 subtract_divide_fusion.3
  22.7 0.1 subtract_divide_fusion.2
  22.8 0.1 subtract_divide_fusion.1
  23.2 0.1 subtract_divide_fusion
  23.3 0.1 add_divide_fusion
  23.4 0.9 %copy.20.flux_ref = f32[2,8,32,1]{3,2,1,0:T(8,128)} copy(f32[2,8,32,1]{2,1,0,3:T(8,128)S(1)} %maximum_bitcast_fusion) | data formatting | bytes 4096 | tf_op jit(solution)/shard_map/broadcast_in_dim | solution.py:300
  24.3 2.5 %shard_map.48 = (f32[8,32,128]{2,1,0:T(8,128)}, f32[7,8,128]{2,1,0:T(8,128)}) custom-call(f32[8,32,128]{2,1,0:T(8,128)} %get-tuple-element.18.p_ref, f32[8,32,128]{2,1,0:T(8,128)} %get-tuple-element.19.u_ref, f32[8,32,128]{2,1,0:T(8,128)} %get-tuple-element.20.w_ref, f32[2,8,32,1]{3,2,1,0:T(8,128)} %copy.20.flux_ref, s32[8,32,128]{2,1,0:T(8,128)} %mask_ref.3, ...), custom_call_target="tpu_custom_call" | custom-call | tf_op jit(solution)/shard_map/pallas_call | solution.py:186
  26.8 43.6 %all-gather = f32[224,8,128]{2,1,0:T(8,128)} all-gather(f32[7,8,128]{2,1,0:T(8,128)} %get-tuple-element.26), channel_id=2, replica_groups=mesh['lat'=32,'lon'=16] {'lat'}, dimensions={0}, use_global_device_ids=true | all-gather | bytes 946176 | tf_op jit(solution)/shard_map/all_gather | solution.py:267
  70.4 2.7 %shard_map.49 = f32[8,32,128]{2,1,0:T(8,128)} custom-call(s32[1]{0:T(128)} %bitcast.index_ref, f32[32,7,8,128]{3,2,1,0:T(8,128)} %bitcast.69, f32[8,32,128]{2,1,0:T(8,128)} %get-tuple-element.27.scale_ref, f32[8,32,128]{2,1,0:T(8,128)} %get-tuple-element.28.p_ref, f32[8,32,128]{2,1,0:T(8,128)} %get-tuple-element.29.u_ref, f32[8,32,128]{2,1,0:T(8,128)} %get-tuple-element.30.w_ref), custom_call_target="tpu_custom_call" | custom-call | tf_op jit(solution)/shard_map/pallas_call | solution.py:270
  (39 shorter events, 0.4 us)
Async XLA Ops:
  6.7 14.2 %all-to-all-start = ((f32[16,1,1792]{2,1,0:T(1,128)}), f32[16,1,1792]{2,1,0:T(1,128)S(1)}, u32[]{:S(2)}, u32[]{:S(2)}) async-start(f32[16,1,1792]{2,1,0:T(1,128)} %reshape.8), calls=%async_computation | async-start | bytes 229376 | tf_op jit(solution)/shard_map/all_to_all | solution.py:284

commit v8 on v6

--- a/solution.py
+++ b/solution.py
@@ -108,6 +108,54 @@
             jax.ShapeDtypeStruct(edge_shape, jnp.float32),
         ),
     )(*inputs)
+
+
+def lon_kernel(source_ref, kappa_ref, mask_ref, p_out, u_out, w_out, edge_out):
+    levels, rows, length = source_ref.shape
+    lines = levels * rows
+
+    def across(values):
+        return jnp.transpose(values.astype(jnp.float32).reshape(lines, length))
+
+    def back(values):
+        return jnp.transpose(values).reshape(levels, rows, length)
+
+    wet = across(mask_ref[...])
+    weight = across(kappa_ref[...]) * wet
+    values = across(source_ref[...])
+    axis = 0
+    shape = values.shape
+    position = lax.broadcasted_iota(jnp.int32, shape, axis)
+    last = position == length - 1
+    right_face = jnp.where(last, 0.0, weight * shifted(wet, -1, axis))
+    left_face = shifted(right_face, 1, axis)
+    particular, from_left, from_right = block_solve(
+        -left_face,
+        -right_face,
+        jnp.ones(shape, jnp.float32),
+        [values, jnp.where(position == 0, 1.0, 0.0), jnp.where(last, 1.0, 0.0)],
+        axis,
+    )
+    p_out[...] = back(particular)
+    u_out[...] = back(from_left)
+    w_out[...] = back(from_right)
+    head_wet = wet[0:1, :]
+    edge_out[0:1, :] = head_wet * particular[0:1, :]
+    edge_out[1:2, :] = head_wet * from_left[0:1, :]
+    edge_out[2:3, :] = head_wet * from_right[0:1, :]
+    edge_out[3:4, :] = weight[length - 1:length, :]
+    edge_out[4:5, :] = from_left[length - 1:length, :]
+    edge_out[5:6, :] = from_right[length - 1:length, :]
+    edge_out[6:7, :] = particular[length - 1:length, :]
+
+
+def lon_pass(source, kappa_lon, sea_mask):
+    shape = source.shape
+    full = jax.ShapeDtypeStruct(shape, jnp.float32)
+    return pl.pallas_call(
+        lon_kernel,
+        out_shape=(full, full, full, jax.ShapeDtypeStruct((TERMS, shape[0] * shape[1]), jnp.float32)),
+    )(source, kappa_lon, sea_mask)
 
 
 def lat_matrix_kernel(kappa_ref, mask_ref, lon_kappa_ref, u_out, w_out, left_out, right_out,
@@ -216,17 +264,9 @@
     return sources / excess
 
 
-def interface_flux(edge, axis, mesh_axis, periodic, exchange):
-    terms = lax.slice_in_dim(edge, 0, TERMS, axis=axis) if edge.shape[axis] > TERMS else edge
-    devices = lax.axis_size(mesh_axis)
-    if exchange == "all_to_all":
-        copies = jnp.broadcast_to(terms[None], (devices,) + terms.shape)
-        gathered = lax.all_to_all(copies, mesh_axis, 0, 0, tiled=True)
-    else:
-        gathered = lax.all_gather(terms[None], mesh_axis, axis=0, tiled=True)
-    (head_p, head_u, head_w, tail_kappa, tail_u, tail_w, tail_p) = (
-        lax.index_in_dim(gathered, k, axis + 1, keepdims=False) for k in range(TERMS)
-    )
+def flux_system(terms, periodic):
+    head_p, head_u, head_w, tail_kappa, tail_u, tail_w, tail_p = terms
+    devices = head_p.shape[0]
 
     def next_of(member):
         return jnp.roll(member, -1, 0)
@@ -240,22 +280,47 @@
     lower = -face * tail_u
     upper = -tail_kappa * next_of(head_w)
     diagonal = 1.0 + tail_kappa * next_of(head_u) + face * tail_w
-    flux = circular_solve(
+    return circular_solve(
         lower, upper, diagonal + lower + upper, tail_kappa * next_of(head_p) - face * tail_p
     )
+
+
+def interface_flux(edge, axis, mesh_axis, periodic, exchange):
+    terms = lax.slice_in_dim(edge, 0, TERMS, axis=axis) if edge.shape[axis] > TERMS else edge
+    devices = lax.axis_size(mesh_axis)
+    if exchange == "all_to_all":
+        copies = jnp.broadcast_to(terms[None], (devices,) + terms.shape)
+        gathered = lax.all_to_all(copies, mesh_axis, 0, 0, tiled=True)
+    else:
+        gathered = lax.all_gather(terms[None], mesh_axis, axis=0, tiled=True)
+    terms = [lax.index_in_dim(gathered, k, axis + 1, keepdims=False) for k in range(TERMS)]
+    flux = flux_system(terms, periodic)
     index = lax.axis_index(mesh_axis)
     here = lax.dynamic_index_in_dim(flux, index, 0, keepdims=True)
     before = lax.dynamic_index_in_dim(flux, (index + devices - 1) % devices, 0, keepdims=True)
     return before[0], here[0]
 
 
+def lon_flux(edge):
+    devices = lax.axis_size("lon")
+    copies = jnp.broadcast_to(edge[None], (devices,) + edge.shape)
+    gathered = lax.all_to_all(copies, "lon", 0, 0, tiled=True)
+    terms = [gathered[:, k] for k in range(TERMS)]
+    flux = flux_system(terms, True)
+    index = lax.axis_index("lon")
+    here = lax.dynamic_index_in_dim(flux, index, 0, keepdims=False)
+    before = lax.dynamic_index_in_dim(flux, (index + devices - 1) % devices, 0, keepdims=False)
+    return before, here
+
+
 def shards(source, kappa_lon, kappa_lat, sea_mask):
-    p_lon, u_lon, w_lon, edge_lon = local_pass(2, (source, kappa_lon, sea_mask))
+    p_lon, u_lon, w_lon, edge_lon = lon_pass(source, kappa_lon, sea_mask)
     u_lat, w_lat, left, right, diagonal, matrix_edge, scale = lat_matrix(kappa_lat, sea_mask, kappa_lon)
-    before, here = interface_flux(edge_lon, 2, "lon", True, "all_to_all")
+    before, here = lon_flux(edge_lon)
+    lines = source.shape[:2] + (1,)
+    flux = jnp.stack([before.reshape(lines), here.reshape(lines)], 0)
     p_lat, edge_lat = lat_rhs(
-        p_lon, u_lon, w_lon, jnp.stack([before, here], 0)[..., None], sea_mask,
-        left, right, diagonal, matrix_edge,
+        p_lon, u_lon, w_lon, flux, sea_mask, left, right, diagonal, matrix_edge,
     )
     before, here = interface_flux(edge_lat, 0, "lat", False, "all_gather")
     return scale * (p_lat - u_lat * before[:, None, :] + w_lat * here[:, None, :])

time: 71.3 us -> 67.5 us (0.947)
  Pallas kernels: 10.1 us -> 8.29 us
  local copies, waits for them, and re-layouts: 5.09 us -> 4.06 us
  other arithmetic: 2.78 us -> 1.75 us
    pallas_call x1, Pallas kernels: 4.74 us -> 2.91 us  [lon_pass(): pl.pallas_call(lon_kernel, out_shape=(full, full, full, jax.ShapeDtypeStr...]
    unnamed x11 -> x9, local copies, waits for them, and re-layouts: 2.03 us -> 0.96 us
    another operation x0 -> x3, local copies, waits for them, and re-layouts: none -> 1.04 us  [shards(): flux = jnp.stack([before.reshape(lines), here.reshape(lines)], 0)]
    slice x1, local copies, waits for them, and re-layouts: 1.02 us -> 0.05 us  [lon_flux(): terms = [gathered[:, k] for k in range(TERMS)]]
    all_to_all x1 -> x0, other arithmetic: 0.82 us -> none  [interface_flux(): gathered = lax.all_to_all(copies, mesh_axis, 0, 0, tiled=True)]
where the time goes in v8:
time: 67.5 us; the launch traced here: 67.2 us
  blocking collectives  40.9 us (61%)
  Pallas kernels  8.29 us (12%)
  starting transfers between devices  7.57 us (11%)
  local copies, waits for them, and re-layouts  4.06 us (6%)
  waiting for transfers between devices  3.79 us (6%)
  other arithmetic  1.75 us (3%)
  between operations  0.8 us (1%)
    all_gather x1, blocking collectives, interface_flux(): gathered = lax.all_gather(terms[None], mesh_axis, axis=0, tiled=True)  40.9 us
    all_to_all x1, starting transfers between devices, lon_flux(): gathered = lax.all_to_all(copies, 'lon', 0, 0, tiled=True)  7.57 us
    all_to_all x1, waiting for transfers between devices, lon_flux(): gathered = lax.all_to_all(copies, 'lon', 0, 0, tiled=True)  3.79 us
    pallas_call x1, Pallas kernels, lon_pass(): pl.pallas_call(lon_kernel, out_shape=(full, full, full, jax.ShapeDtypeStr...  2.91 us
    pallas_call x1, Pallas kernels, lat_matrix(): pl.pallas_call(lat_matrix_kernel, out_shape=(full, full, stacked, stacked...  2.87 us
    pallas_call x1, Pallas kernels, lat_rhs(): pl.pallas_call(lat_rhs_kernel, out_shape=(jax.ShapeDtypeStruct(shape, jnp...  2.51 us
    broadcast_in_dim x1, local copies, waits for them, and re-layouts, lon_flux(): copies = jnp.broadcast_to(edge[None], (devices,) + edge.shape)  1.36 us
  transfers between devices with their start and end apart: 1, of which 1 were waited for; matrix products, arithmetic and copies ran while one was open for 0% of the time, Pallas kernels for 4%

profile of v8, /device:TPU:1, one launch (start us, length us, event | category | flops | bytes accessed | tf_op | source)
XLA Modules:
  0.0 67.2 jit_solution(11645824552219939674)
XLA Ops:
  0.0 2.9 %shard_map.47 = (f32[8,32,128]{2,1,0:T(8,128)}, f32[8,32,128]{2,1,0:T(8,128)}, f32[8,32,128]{2,1,0:T(8,128)}, f32[7,256]{1,0:T(8,128)}) custom-call(f32[8,32,128]{2,1,0:T(8,128)} %source_ref.1, bf16[8,32,128]{2,1,0:T(8,128)(2,1)} %kappa_ref.3, s32[8,32,128]{2,1,0:T(8,128)} %mask_ref.5), custom_call_target="tpu_custom_call" | custom-call | tf_op jit(solution)/shard_map/pallas_call | solution.py:155
  2.9 1.4 %broadcast_in_dim.26 = f32[16,7,256]{2,1,0:T(8,128)} broadcast(f32[7,256]{1,0:T(8,128)} %get-tuple-element.22), dimensions={1,2} | broadcast | bytes 121856 | tf_op jit(solution)/shard_map/broadcast_in_dim | solution.py:306
  4.3 7.6 %all-to-all-start = ((f32[16,7,256]{2,1,0:T(8,128)}), f32[16,7,256]{2,1,0:T(8,128)S(1)}, u32[]{:S(2)}, u32[]{:S(2)}) async-start(f32[16,7,256]{2,1,0:T(8,128)} %broadcast_in_dim.26), calls=%async_computation | async-start | bytes 262144 | tf_op jit(solution)/shard_map/all_to_all | solution.py:307
  11.9 2.9 %shard_map.46 = (f32[8,32,128]{2,1,0:T(8,128)}, f32[8,32,128]{2,1,0:T(8,128)}, f32[5,8,32,128]{3,2,1,0:T(8,128)}, f32[5,8,32,128]{3,2,1,0:T(8,128)}, f32[8,32,12...) custom-call(bf16[8,32,128]{2,1,0:T(8,128)(2,1)} %kappa_ref.2, s32[8,32,128]{2,1,0:T(8,128)} %mask_ref.5, ...), custom_call_target="tpu_custom_call" | custom-call | tf_op jit(solution)/shard_map/pallas_call | solution.py:225
  14.8 3.8 %all-to-all-done = f32[16,7,256]{2,1,0:T(8,128)S(1)} async-done(((f32[16,7,256]{2,1,0:T(8,128)}), f32[16,7,256]{2,1,0:T(8,128)S(1)}, u32[]{:S(2)}, u32[]{:S(2)}) %all-to-all-start) | async-done | bytes 114720 | tf_op jit(solution)/shard_map/all_to_all | solution.py:307
  18.6 0.1 fusion.84
  19.4 0.1 stack_reshape.6
  19.4 0.1 stack_reshape.7
  19.5 0.9 %copy.25.flux_ref = f32[2,8,32,1]{3,2,1,0:T(8,128)} copy(f32[2,8,32,1]{2,1,3,0:T(8,128)S(1)} %pad_maximum_fusion.8) | data formatting | bytes 4096 | tf_op jit(solution)/shard_map/stack | solution.py:321
  20.4 2.5 %shard_map.48 = (f32[8,32,128]{2,1,0:T(8,128)}, f32[7,8,128]{2,1,0:T(8,128)}) custom-call(f32[8,32,128]{2,1,0:T(8,128)} %get-tuple-element.19.p_ref, f32[8,32,128]{2,1,0:T(8,128)} %get-tuple-element.20.u_ref, f32[8,32,128]{2,1,0:T(8,128)} %get-tuple-element.21.w_ref, f32[2,8,32,1]{3,2,1,0:T(8,128)} %copy.25.flux_ref, s32[8,32,128]{2,1,0:T(8,128)} %mask_ref.5, ...), custom_call_target="tpu_custom_call" | custom-call | tf_op jit(solution)/shard_map/pallas_call | solution.py:234
  22.9 40.9 %all-gather = f32[224,8,128]{2,1,0:T(8,128)S(1)} all-gather(f32[7,8,128]{2,1,0:T(8,128)} %get-tuple-element.29), channel_id=2, replica_groups=mesh['lat'=32,'lon'=16] {'lat'}, dimensions={0}, use_global_device_ids=true | all-gather | bytes 946176 | tf_op jit(solution)/shard_map/all_gather | solution.py:295
  63.8 0.2 subtract_divide_fusion.4
  64.1 0.1 fusion.8
  64.3 0.1 subtract_divide_fusion.3
  64.4 0.1 fusion.12
  64.6 0.1 subtract_divide_fusion.2
  64.8 0.1 fusion.16
  65.0 0.1 subtract_divide_fusion.1
  65.2 0.1 subtract_divide_fusion
  65.4 0.0 copy-start
  65.4 0.0 copy-start.1
  65.4 0.0 copy-start.2
  65.4 0.0 copy-start.3
  65.4 0.1 add_divide_fusion
  65.5 0.8 %copy-done = f32[8,32,128]{2,1,0:T(8,128)S(1)} copy-done((f32[8,32,128]{2,1,0:T(8,128)S(1)}, f32[8,32,128]{2,1,0:T(8,128)}, u32[]{:S(2)}) %copy-start) | copy-done | bytes 131096
  66.3 0.1 copy-done.1
  66.3 0.1 copy-done.2
  66.4 0.1 copy-done.3
  66.5 0.7 %add_multiply_fusion = f32[8,32,128]{2,1,0:T(8,128)} fusion(f32[8,32,128]{2,1,0:T(8,128)S(1)} %copy-done.2, f32[8,32,128]{2,1,0:T(8,128)S(1)} %copy-done.1, f32[8,32,128]{2,1,0:T(8,128)S(1)} %copy-done.3, f32[8,32,128]{2,1,0:T(8,128)S(1)} %copy-done, f32[8,128]{1,0:T(8,128)S(1)} %get-tuple-element.85, f32[8,128]{1,0:T(8,128)S(1)} %get-tuple-element.84), kind=kLoop, calls=%fused_computation.65 | loop fusion | flops 163840 | bytes 663552 | tf_op jit(solution)/shard_map/mul | solution.py:326
  (93 shorter events, 0.9 us)
Async XLA Ops:
  4.3 14.3 %all-to-all-start = ((f32[16,7,256]{2,1,0:T(8,128)}), f32[16,7,256]{2,1,0:T(8,128)S(1)}, u32[]{:S(2)}, u32[]{:S(2)}) async-start(f32[16,7,256]{2,1,0:T(8,128)} %broadcast_in_dim.26), calls=%async_computation | async-start | bytes 262144 | tf_op jit(solution)/shard_map/all_to_all | solution.py:307
  65.4 0.9 %copy-start = (f32[8,32,128]{2,1,0:T(8,128)S(1)}, f32[8,32,128]{2,1,0:T(8,128)}, u32[]{:S(2)}) copy-start(f32[8,32,128]{2,1,0:T(8,128)} %get-tuple-element.28) | copy-start | bytes 393220
  65.4 1.0 %copy-start.1 = (f32[8,32,128]{2,1,0:T(8,128)S(1)}, f32[8,32,128]{2,1,0:T(8,128)}, u32[]{:S(2)}) copy-start(f32[8,32,128]{2,1,0:T(8,128)} %get-tuple-element.30) | copy-start | bytes 393220
  65.4 1.0 %copy-start.2 = (f32[8,32,128]{2,1,0:T(8,128)S(1)}, f32[8,32,128]{2,1,0:T(8,128)}, u32[]{:S(2)}) copy-start(f32[8,32,128]{2,1,0:T(8,128)} %get-tuple-element.18) | copy-start | bytes 393220
  65.4 1.1 %copy-start.3 = (f32[8,32,128]{2,1,0:T(8,128)S(1)}, f32[8,32,128]{2,1,0:T(8,128)}, u32[]{:S(2)}) copy-start(f32[8,32,128]{2,1,0:T(8,128)} %get-tuple-element.27) | copy-start | bytes 393220

commit v9 on v8

--- a/solution.py
+++ b/solution.py
@@ -140,22 +140,25 @@
     u_out[...] = back(from_left)
     w_out[...] = back(from_right)
     head_wet = wet[0:1, :]
-    edge_out[0:1, :] = head_wet * particular[0:1, :]
-    edge_out[1:2, :] = head_wet * from_left[0:1, :]
-    edge_out[2:3, :] = head_wet * from_right[0:1, :]
-    edge_out[3:4, :] = weight[length - 1:length, :]
-    edge_out[4:5, :] = from_left[length - 1:length, :]
-    edge_out[5:6, :] = from_right[length - 1:length, :]
-    edge_out[6:7, :] = particular[length - 1:length, :]
-
-
-def lon_pass(source, kappa_lon, sea_mask):
+    rows = [
+        head_wet * particular[0:1, :],
+        head_wet * from_left[0:1, :],
+        head_wet * from_right[0:1, :],
+        weight[length - 1:length, :],
+        from_left[length - 1:length, :],
+        from_right[length - 1:length, :],
+        particular[length - 1:length, :],
+    ]
+    for copy in range(edge_out.shape[0]):
+        for k, row in enumerate(rows):
+            edge_out[copy, k:k + 1, :] = row
+
+
+def lon_pass(source, kappa_lon, sea_mask, devices):
     shape = source.shape
     full = jax.ShapeDtypeStruct(shape, jnp.float32)
-    return pl.pallas_call(
-        lon_kernel,
-        out_shape=(full, full, full, jax.ShapeDtypeStruct((TERMS, shape[0] * shape[1]), jnp.float32)),
-    )(source, kappa_lon, sea_mask)
+    edge = jax.ShapeDtypeStruct((devices, TERMS, shape[0] * shape[1]), jnp.float32)
+    return pl.pallas_call(lon_kernel, out_shape=(full, full, full, edge))(source, kappa_lon, sea_mask)
 
 
 def lat_matrix_kernel(kappa_ref, mask_ref, lon_kappa_ref, u_out, w_out, left_out, right_out,
@@ -301,9 +304,8 @@
     return before[0], here[0]
 
 
-def lon_flux(edge):
-    devices = lax.axis_size("lon")
-    copies = jnp.broadcast_to(edge[None], (devices,) + edge.shape)
+def lon_flux(copies):
+    devices = copies.shape[0]
     gathered = lax.all_to_all(copies, "lon", 0, 0, tiled=True)
     terms = [gathered[:, k] for k in range(TERMS)]
     flux = flux_system(terms, True)
@@ -314,7 +316,7 @@
 
 
 def shards(source, kappa_lon, kappa_lat, sea_mask):
-    p_lon, u_lon, w_lon, edge_lon = lon_pass(source, kappa_lon, sea_mask)
+    p_lon, u_lon, w_lon, edge_lon = lon_pass(source, kappa_lon, sea_mask, lax.axis_size("lon"))
     u_lat, w_lat, left, right, diagonal, matrix_edge, scale = lat_matrix(kappa_lat, sea_mask, kappa_lon)
     before, here = lon_flux(edge_lon)
     lines = source.shape[:2] + (1,)

time: 67.5 us -> 66.1 us (0.979)
  local copies, waits for them, and re-layouts: 4.06 us -> 2.71 us
    broadcast_in_dim x1 -> x0, local copies, waits for them, and re-layouts: 1.36 us -> none  [lon_flux(): copies = jnp.broadcast_to(edge[None], (devices,) + edge.shape)]
where the time goes in v9:
time: 66.1 us; the launch traced here: 65.8 us
  blocking collectives  40.9 us (62%)
  Pallas kernels  8.34 us (13%)
  starting transfers between devices  7.57 us (11%)
  waiting for transfers between devices  3.77 us (6%)
  local copies, waits for them, and re-layouts  2.71 us (4%)
  other arithmetic  1.74 us (3%)
  between operations  0.81 us (1%)
    all_gather x1, blocking collectives, interface_flux(): gathered = lax.all_gather(terms[None], mesh_axis, axis=0, tiled=True)  40.9 us
    all_to_all x1, starting transfers between devices, lon_flux(): gathered = lax.all_to_all(copies, 'lon', 0, 0, tiled=True)  7.57 us
    all_to_all x1, waiting for transfers between devices, lon_flux(): gathered = lax.all_to_all(copies, 'lon', 0, 0, tiled=True)  3.77 us
    pallas_call x1, Pallas kernels, lon_pass(): pl.pallas_call(lon_kernel, out_shape=(full, full, full, edge))  2.95 us
    pallas_call x1, Pallas kernels, lat_matrix(): pl.pallas_call(lat_matrix_kernel, out_shape=(full, full, stacked, stacked...  2.89 us
    pallas_call x1, Pallas kernels, lat_rhs(): pl.pallas_call(lat_rhs_kernel, out_shape=(jax.ShapeDtypeStruct(shape, jnp...  2.51 us
  transfers between devices with their start and end apart: 1, of which 1 were waited for; matrix products, arithmetic and copies ran while one was open for 0% of the time, Pallas kernels for 4%

profile of v9, /device:TPU:1, one launch (start us, length us, event | category | flops | bytes accessed | tf_op | source)
XLA Modules:
  0.0 65.8 jit_solution(13091791686585674656)
XLA Ops:
  0.0 2.9 %shard_map.47 = (f32[8,32,128]{2,1,0:T(8,128)}, f32[8,32,128]{2,1,0:T(8,128)}, f32[8,32,128]{2,1,0:T(8,128)}, f32[16,7,256]{2,1,0:T(8,128)}) custom-call(f32[8,32,128]{2,1,0:T(8,128)} %source_ref.1, bf16[8,32,128]{2,1,0:T(8,128)(2,1)} %kappa_ref.3, s32[8,32,128]{2,1,0:T(8,128)} %mask_ref.5), custom_call_target="tpu_custom_call" | custom-call | tf_op jit(solution)/shard_map/pallas_call | solution.py:161
  2.9 7.6 %all-to-all-start = ((f32[16,7,256]{2,1,0:T(8,128)}), f32[16,7,256]{2,1,0:T(8,128)S(1)}, u32[]{:S(2)}, u32[]{:S(2)}) async-start(f32[16,7,256]{2,1,0:T(8,128)} %get-tuple-element.22), calls=%async_computation | async-start | bytes 262144 | tf_op jit(solution)/shard_map/all_to_all | solution.py:309
  10.6 2.9 %shard_map.46 = (f32[8,32,128]{2,1,0:T(8,128)}, f32[8,32,128]{2,1,0:T(8,128)}, f32[5,8,32,128]{3,2,1,0:T(8,128)}, f32[5,8,32,128]{3,2,1,0:T(8,128)}, f32[8,32,12...) custom-call(bf16[8,32,128]{2,1,0:T(8,128)(2,1)} %kappa_ref.2, s32[8,32,128]{2,1,0:T(8,128)} %mask_ref.5, ...), custom_call_target="tpu_custom_call" | custom-call | tf_op jit(solution)/shard_map/pallas_call | solution.py:228
  13.5 3.8 %all-to-all-done = f32[16,7,256]{2,1,0:T(8,128)S(1)} async-done(((f32[16,7,256]{2,1,0:T(8,128)}), f32[16,7,256]{2,1,0:T(8,128)S(1)}, u32[]{:S(2)}, u32[]{:S(2)}) %all-to-all-start) | async-done | bytes 114720 | tf_op jit(solution)/shard_map/all_to_all | solution.py:309
  17.3 0.1 fusion.84
  18.0 0.1 stack_reshape.6
  18.1 0.1 stack_reshape.7
  18.2 0.9 %copy.37.flux_ref = f32[2,8,32,1]{3,2,1,0:T(8,128)} copy(f32[2,8,32,1]{2,1,3,0:T(8,128)S(1)} %pad_maximum_fusion.8) | data formatting | bytes 4096 | tf_op jit(solution)/shard_map/stack | solution.py:323
  19.1 2.5 %shard_map.48 = (f32[8,32,128]{2,1,0:T(8,128)}, f32[7,8,128]{2,1,0:T(8,128)}) custom-call(f32[8,32,128]{2,1,0:T(8,128)} %get-tuple-element.19.p_ref, f32[8,32,128]{2,1,0:T(8,128)} %get-tuple-element.20.u_ref, f32[8,32,128]{2,1,0:T(8,128)} %get-tuple-element.21.w_ref, f32[2,8,32,1]{3,2,1,0:T(8,128)} %copy.37.flux_ref, s32[8,32,128]{2,1,0:T(8,128)} %mask_ref.5, ...), custom_call_target="tpu_custom_call" | custom-call | tf_op jit(solution)/shard_map/pallas_call | solution.py:237
  21.6 40.9 %all-gather = f32[224,8,128]{2,1,0:T(8,128)S(1)} all-gather(f32[7,8,128]{2,1,0:T(8,128)} %get-tuple-element.29), channel_id=2, replica_groups=mesh['lat'=32,'lon'=16] {'lat'}, dimensions={0}, use_global_device_ids=true | all-gather | bytes 946176 | tf_op jit(solution)/shard_map/all_gather | solution.py:298
  62.5 0.2 subtract_divide_fusion.4
  62.8 0.1 fusion.8
  63.0 0.1 subtract_divide_fusion.3
  63.3 0.1 subtract_divide_fusion.2
  63.5 0.1 fusion.16
  63.6 0.1 subtract_divide_fusion.1
  63.9 0.1 subtract_divide_fusion
  64.0 0.0 copy-start
  64.0 0.0 copy-start.1
  64.1 0.0 copy-start.2
  64.1 0.0 copy-start.3
  64.1 0.1 add_divide_fusion
  64.2 0.8 %copy-done = f32[8,32,128]{2,1,0:T(8,128)S(1)} copy-done((f32[8,32,128]{2,1,0:T(8,128)S(1)}, f32[8,32,128]{2,1,0:T(8,128)}, u32[]{:S(2)}) %copy-start) | copy-done | bytes 131096
  64.9 0.1 copy-done.1
  65.0 0.1 copy-done.2
  65.1 0.1 copy-done.3
  65.1 0.7 %add_multiply_fusion = f32[8,32,128]{2,1,0:T(8,128)} fusion(f32[8,32,128]{2,1,0:T(8,128)S(1)} %copy-done.2, f32[8,32,128]{2,1,0:T(8,128)S(1)} %copy-done.1, f32[8,32,128]{2,1,0:T(8,128)S(1)} %copy-done.3, f32[8,32,128]{2,1,0:T(8,128)S(1)} %copy-done, f32[8,128]{1,0:T(8,128)S(1)} %get-tuple-element.85, f32[8,128]{1,0:T(8,128)S(1)} %get-tuple-element.84), kind=kLoop, calls=%fused_computation.65 | loop fusion | flops 163840 | bytes 663552 | tf_op jit(solution)/shard_map/mul | solution.py:328
  (94 shorter events, 1.0 us)
Async XLA Ops:
  2.9 14.3 %all-to-all-start = ((f32[16,7,256]{2,1,0:T(8,128)}), f32[16,7,256]{2,1,0:T(8,128)S(1)}, u32[]{:S(2)}, u32[]{:S(2)}) async-start(f32[16,7,256]{2,1,0:T(8,128)} %get-tuple-element.22), calls=%async_computation | async-start | bytes 262144 | tf_op jit(solution)/shard_map/all_to_all | solution.py:309
  64.0 0.9 %copy-start = (f32[8,32,128]{2,1,0:T(8,128)S(1)}, f32[8,32,128]{2,1,0:T(8,128)}, u32[]{:S(2)}) copy-start(f32[8,32,128]{2,1,0:T(8,128)} %get-tuple-element.28) | copy-start | bytes 393220
  64.0 1.0 %copy-start.1 = (f32[8,32,128]{2,1,0:T(8,128)S(1)}, f32[8,32,128]{2,1,0:T(8,128)}, u32[]{:S(2)}) copy-start(f32[8,32,128]{2,1,0:T(8,128)} %get-tuple-element.30) | copy-start | bytes 393220
  64.1 1.0 %copy-start.2 = (f32[8,32,128]{2,1,0:T(8,128)S(1)}, f32[8,32,128]{2,1,0:T(8,128)}, u32[]{:S(2)}) copy-start(f32[8,32,128]{2,1,0:T(8,128)} %get-tuple-element.18) | copy-start | bytes 393220
  64.1 1.1 %copy-start.3 = (f32[8,32,128]{2,1,0:T(8,128)S(1)}, f32[8,32,128]{2,1,0:T(8,128)}, u32[]{:S(2)}) copy-start(f32[8,32,128]{2,1,0:T(8,128)} %get-tuple-element.27) | copy-start | bytes 393220

commit v10 on v9

--- a/solution.py
+++ b/solution.py
@@ -201,7 +201,15 @@
 def lat_rhs_kernel(p_ref, u_ref, w_ref, flux_ref, mask_ref, left_ref, right_ref,
                    diagonal_ref, matrix_edge_ref, p_out, edge_out):
     axis = 1
-    values = p_ref[...] - u_ref[...] * flux_ref[0] + w_ref[...] * flux_ref[1]
+    levels, rows, width = p_ref.shape
+    lines = flux_ref.shape[1]
+    padded = jnp.concatenate(
+        [flux_ref[...], jnp.zeros((width - flux_ref.shape[0], lines), jnp.float32)], 0
+    )
+    columns = jnp.transpose(padded)
+    before = columns[:, 0:1].reshape(levels, rows, 1)
+    here = columns[:, 1:2].reshape(levels, rows, 1)
+    values = p_ref[...] - u_ref[...] * before + w_ref[...] * here
     length = values.shape[axis]
     stride = 1
     step = 0
@@ -319,8 +327,7 @@
     p_lon, u_lon, w_lon, edge_lon = lon_pass(source, kappa_lon, sea_mask, lax.axis_size("lon"))
     u_lat, w_lat, left, right, diagonal, matrix_edge, scale = lat_matrix(kappa_lat, sea_mask, kappa_lon)
     before, here = lon_flux(edge_lon)
-    lines = source.shape[:2] + (1,)
-    flux = jnp.stack([before.reshape(lines), here.reshape(lines)], 0)
+    flux = jnp.concatenate([before[None], here[None], jnp.zeros((6,) + before.shape, jnp.float32)], 0)
     p_lat, edge_lat = lat_rhs(
         p_lon, u_lon, w_lon, flux, sea_mask, left, right, diagonal, matrix_edge,
     )

time: 66.1 us -> 65.8 us (level)
  local copies, waits for them, and re-layouts: 2.71 us -> 1.73 us
    another operation x3 -> x0, local copies, waits for them, and re-layouts: 1.04 us -> none  [shards(): flux = jnp.stack([before.reshape(lines), here.reshape(lines)], 0)]
    concatenate x0 -> x1, other arithmetic: none -> 0.66 us  [shards(): jnp.concatenate([before[None], here[None], jnp.zeros((6,) + before.shape,...]
where the time goes in v10:
time: 65.8 us; the launch traced here: 65.6 us
  blocking collectives  40.9 us (62%)
  Pallas kernels  8.44 us (13%)
  starting transfers between devices  7.57 us (12%)
  waiting for transfers between devices  3.72 us (6%)
  other arithmetic  2.39 us (4%)
  local copies, waits for them, and re-layouts  1.73 us (3%)
  between operations  0.82 us (1%)
    all_gather x1, blocking collectives, interface_flux(): gathered = lax.all_gather(terms[None], mesh_axis, axis=0, tiled=True)  40.9 us
    all_to_all x1, starting transfers between devices, lon_flux(): gathered = lax.all_to_all(copies, 'lon', 0, 0, tiled=True)  7.57 us
    all_to_all x1, waiting for transfers between devices, lon_flux(): gathered = lax.all_to_all(copies, 'lon', 0, 0, tiled=True)  3.72 us
    pallas_call x1, Pallas kernels, lon_pass(): pl.pallas_call(lon_kernel, out_shape=(full, full, full, edge))  2.96 us
    pallas_call x1, Pallas kernels, lat_matrix(): pl.pallas_call(lat_matrix_kernel, out_shape=(full, full, stacked, stacked...  2.86 us
    pallas_call x1, Pallas kernels, lat_rhs(): pl.pallas_call(lat_rhs_kernel, out_shape=(jax.ShapeDtypeStruct(shape, jnp...  2.61 us
  transfers between devices with their start and end apart: 1, of which 1 were waited for; matrix products, arithmetic and copies ran while one was open for 0% of the time, Pallas kernels for 4%

profile of v10, /device:TPU:1, one launch (start us, length us, event | category | flops | bytes accessed | tf_op | source)
XLA Modules:
  0.0 65.6 jit_solution(2862315909462134114)
XLA Ops:
  0.0 3.0 %shard_map.47 = (f32[8,32,128]{2,1,0:T(8,128)}, f32[8,32,128]{2,1,0:T(8,128)}, f32[8,32,128]{2,1,0:T(8,128)}, f32[16,7,256]{2,1,0:T(8,128)}) custom-call(f32[8,32,128]{2,1,0:T(8,128)} %source_ref.1, bf16[8,32,128]{2,1,0:T(8,128)(2,1)} %kappa_ref.3, s32[8,32,128]{2,1,0:T(8,128)} %mask_ref.5), custom_call_target="tpu_custom_call" | custom-call | tf_op jit(solution)/shard_map/pallas_call | solution.py:161
  3.0 7.6 %all-to-all-start = ((f32[16,7,256]{2,1,0:T(8,128)}), f32[16,7,256]{2,1,0:T(8,128)S(1)}, u32[]{:S(2)}, u32[]{:S(2)}) async-start(f32[16,7,256]{2,1,0:T(8,128)} %get-tuple-element.22), calls=%async_computation | async-start | bytes 262144 | tf_op jit(solution)/shard_map/all_to_all | solution.py:317
  10.6 2.9 %shard_map.46 = (f32[8,32,128]{2,1,0:T(8,128)}, f32[8,32,128]{2,1,0:T(8,128)}, f32[5,8,32,128]{3,2,1,0:T(8,128)}, f32[5,8,32,128]{3,2,1,0:T(8,128)}, f32[8,32,12...) custom-call(bf16[8,32,128]{2,1,0:T(8,128)(2,1)} %kappa_ref.2, s32[8,32,128]{2,1,0:T(8,128)} %mask_ref.5, ...), custom_call_target="tpu_custom_call" | custom-call | tf_op jit(solution)/shard_map/pallas_call | solution.py:236
  13.4 0.1 pad.78.clone
  13.5 3.7 %all-to-all-done = f32[16,7,256]{2,1,0:T(8,128)S(1)} async-done(((f32[16,7,256]{2,1,0:T(8,128)}), f32[16,7,256]{2,1,0:T(8,128)S(1)}, u32[]{:S(2)}, u32[]{:S(2)}) %all-to-all-start) | async-done | bytes 114720 | tf_op jit(solution)/shard_map/all_to_all | solution.py:317
  17.3 0.1 fusion.84
  18.0 0.7 %maximum_maximum_fusion.flux_ref = f32[8,256]{1,0:T(8,128)} fusion(f32[1,256]{1,0:T(1,128)S(1)} %get-tuple-element.149, f32[1,256]{1,0:T(1,128)S(1)} %get-tuple-element.148, f32[8]{0:T(128)S(1)} %pad.78.clone), kind=kLoop, calls=%fused_computation.140 | loop fusion | flops 4096 | bytes 10272 | tf_op jit(solution)/shard_map/concatenate | solution.py:330
  18.7 2.6 %shard_map.48 = (f32[8,32,128]{2,1,0:T(8,128)}, f32[7,8,128]{2,1,0:T(8,128)}) custom-call(f32[8,32,128]{2,1,0:T(8,128)} %get-tuple-element.19.p_ref, f32[8,32,128]{2,1,0:T(8,128)} %get-tuple-element.20.u_ref, f32[8,32,128]{2,1,0:T(8,128)} %get-tuple-element.21.w_ref, f32[8,256]{1,0:T(8,128)} %maximum_maximum_fusion.flux_ref, s32[8,32,128]{2,1,0:T(8,128)} %mask_ref.5, ...), custom_call_target="tpu_custom_call" | custom-call | tf_op jit(solution)/shard_map/pallas_call | solution.py:245
  21.3 40.9 %all-gather = f32[224,8,128]{2,1,0:T(8,128)S(1)} all-gather(f32[7,8,128]{2,1,0:T(8,128)} %get-tuple-element.29), channel_id=2, replica_groups=mesh['lat'=32,'lon'=16] {'lat'}, dimensions={0}, use_global_device_ids=true | all-gather | bytes 946176 | tf_op jit(solution)/shard_map/all_gather | solution.py:306
  62.2 0.2 subtract_divide_fusion.4
  62.5 0.1 fusion.8
  62.7 0.1 subtract_divide_fusion.3
  63.0 0.1 subtract_divide_fusion.2
  63.2 0.1 fusion.16
  63.4 0.1 subtract_divide_fusion.1
  63.6 0.1 subtract_divide_fusion
  63.8 0.0 copy-start
  63.8 0.0 copy-start.1
  63.8 0.0 copy-start.2
  63.8 0.0 copy-start.3
  63.8 0.1 add_divide_fusion
  63.9 0.8 %copy-done = f32[8,32,128]{2,1,0:T(8,128)S(1)} copy-done((f32[8,32,128]{2,1,0:T(8,128)S(1)}, f32[8,32,128]{2,1,0:T(8,128)}, u32[]{:S(2)}) %copy-start) | copy-done | bytes 131096
  64.7 0.1 copy-done.1
  64.7 0.1 copy-done.2
  64.8 0.1 copy-done.3
  64.9 0.7 %add_multiply_fusion = f32[8,32,128]{2,1,0:T(8,128)} fusion(f32[8,32,128]{2,1,0:T(8,128)S(1)} %copy-done.2, f32[8,32,128]{2,1,0:T(8,128)S(1)} %copy-done.1, f32[8,32,128]{2,1,0:T(8,128)S(1)} %copy-done.3, f32[8,32,128]{2,1,0:T(8,128)S(1)} %copy-done, f32[8,128]{1,0:T(8,128)S(1)} %get-tuple-element.83, f32[8,128]{1,0:T(8,128)S(1)} %get-tuple-element.82), kind=kLoop, calls=%fused_computation.65 | loop fusion | flops 163840 | bytes 663552 | tf_op jit(solution)/shard_map/mul | solution.py:335
  (94 shorter events, 0.9 us)
Async XLA Ops:
  3.0 14.3 %all-to-all-start = ((f32[16,7,256]{2,1,0:T(8,128)}), f32[16,7,256]{2,1,0:T(8,128)S(1)}, u32[]{:S(2)}, u32[]{:S(2)}) async-start(f32[16,7,256]{2,1,0:T(8,128)} %get-tuple-element.22), calls=%async_computation | async-start | bytes 262144 | tf_op jit(solution)/shard_map/all_to_all | solution.py:317
  63.8 0.9 %copy-start = (f32[8,32,128]{2,1,0:T(8,128)S(1)}, f32[8,32,128]{2,1,0:T(8,128)}, u32[]{:S(2)}) copy-start(f32[8,32,128]{2,1,0:T(8,128)} %get-tuple-element.28) | copy-start | bytes 393220
  63.8 1.0 %copy-start.1 = (f32[8,32,128]{2,1,0:T(8,128)S(1)}, f32[8,32,128]{2,1,0:T(8,128)}, u32[]{:S(2)}) copy-start(f32[8,32,128]{2,1,0:T(8,128)} %get-tuple-element.30) | copy-start | bytes 393220
  63.8 1.0 %copy-start.2 = (f32[8,32,128]{2,1,0:T(8,128)S(1)}, f32[8,32,128]{2,1,0:T(8,128)}, u32[]{:S(2)}) copy-start(f32[8,32,128]{2,1,0:T(8,128)} %get-tuple-element.18) | copy-start | bytes 393220
  63.8 1.1 %copy-start.3 = (f32[8,32,128]{2,1,0:T(8,128)S(1)}, f32[8,32,128]{2,1,0:T(8,128)}, u32[]{:S(2)}) copy-start(f32[8,32,128]{2,1,0:T(8,128)} %get-tuple-element.27) | copy-start | bytes 393220

commit v11 on v10

--- a/solution.py
+++ b/solution.py
@@ -161,34 +161,23 @@
     return pl.pallas_call(lon_kernel, out_shape=(full, full, full, edge))(source, kappa_lon, sea_mask)
 
 
-def lat_matrix_kernel(kappa_ref, mask_ref, lon_kappa_ref, u_out, w_out, left_out, right_out,
-                      diagonal_out, edge_out, scale_out, weight_scratch):
+def lat_matrix_kernel(kappa_ref, mask_ref, lon_kappa_ref, u_out, w_out, edge_out, scale_out,
+                      weight_scratch):
     axis = 1
-    wet = mask_ref[...].astype(jnp.float32)
+    wet, weight, position, left_face, right_face = lat_faces(kappa_ref, mask_ref, axis)
     lat_kappa = kappa_ref[...].astype(jnp.float32)
     scale_out[...] = wet * 4.0 * jnp.sqrt(jnp.sqrt(lon_kappa_ref[...].astype(jnp.float32) * lat_kappa))
-    weight = lat_kappa * wet
     shape = wet.shape
     length = shape[axis]
-    position = lax.broadcasted_iota(jnp.int32, shape, axis)
-    last = position == length - 1
-    right_face = jnp.where(last, 0.0, weight * shifted(wet, -1, axis))
-    left_face = shifted(right_face, 1, axis)
-    weights = []
     from_left, from_right = block_solve(
         -left_face,
         -right_face,
         jnp.ones(shape, jnp.float32),
-        [jnp.where(position == 0, 1.0, 0.0), jnp.where(last, 1.0, 0.0)],
+        [jnp.where(position == 0, 1.0, 0.0), jnp.where(position == length - 1, 1.0, 0.0)],
         axis,
-        weights,
     )
     u_out[...] = from_left
     w_out[...] = from_right
-    for step, (left_weight, right_coefficient) in enumerate(weights[:-1]):
-        left_out[step] = left_weight
-        right_out[step] = right_coefficient
-    diagonal_out[...] = weights[-1]
     weight_scratch[...] = weight
     head_wet = mask_ref[:, 0, :].astype(jnp.float32)
     edge_out[0] = head_wet * u_out[:, 0, :]
@@ -198,8 +187,18 @@
     edge_out[4] = w_out[:, length - 1, :]
 
 
-def lat_rhs_kernel(p_ref, u_ref, w_ref, flux_ref, mask_ref, left_ref, right_ref,
-                   diagonal_ref, matrix_edge_ref, p_out, edge_out):
+def lat_faces(kappa_ref, mask_ref, axis):
+    wet = mask_ref[...].astype(jnp.float32)
+    weight = kappa_ref[...].astype(jnp.float32) * wet
+    position = lax.broadcasted_iota(jnp.int32, wet.shape, axis)
+    last = position == wet.shape[axis] - 1
+    right_face = jnp.where(last, 0.0, weight * shifted(wet, -1, axis))
+    left_face = shifted(right_face, 1, axis)
+    return wet, weight, position, left_face, right_face
+
+
+def lat_rhs_kernel(p_ref, u_ref, w_ref, flux_ref, kappa_ref, mask_ref, matrix_edge_ref,
+                   p_out, edge_out):
     axis = 1
     levels, rows, width = p_ref.shape
     lines = flux_ref.shape[1]
@@ -210,18 +209,12 @@
     before = columns[:, 0:1].reshape(levels, rows, 1)
     here = columns[:, 1:2].reshape(levels, rows, 1)
     values = p_ref[...] - u_ref[...] * before + w_ref[...] * here
+    wet, weight, position, left_face, right_face = lat_faces(kappa_ref, mask_ref, axis)
+    (particular,) = block_solve(
+        -left_face, -right_face, jnp.ones(values.shape, jnp.float32), [values], axis
+    )
+    p_out[...] = particular
     length = values.shape[axis]
-    stride = 1
-    step = 0
-    while stride < length:
-        values = (
-            values
-            + left_ref[step] * shifted(values, stride, axis)
-            + right_ref[step] * shifted(values, -stride, axis)
-        )
-        stride = stride * 2
-        step = step + 1
-    p_out[...] = values / diagonal_ref[...]
     edge_out[0] = mask_ref[:, 0, :].astype(jnp.float32) * p_out[:, 0, :]
     edge_out[1:TERMS - 1] = matrix_edge_ref[...]
     edge_out[TERMS - 1] = p_out[:, length - 1, :]
@@ -229,13 +222,11 @@
 
 def lat_matrix(kappa_lat, sea_mask, kappa_lon):
     shape = kappa_lat.shape
-    steps = (shape[1] - 1).bit_length()
     full = jax.ShapeDtypeStruct(shape, jnp.float32)
-    stacked = jax.ShapeDtypeStruct((steps,) + shape, jnp.float32)
     edge = jax.ShapeDtypeStruct((TERMS - 2, shape[0], shape[2]), jnp.float32)
     return pl.pallas_call(
         lat_matrix_kernel,
-        out_shape=(full, full, stacked, stacked, full, edge, full),
+        out_shape=(full, full, edge, full),
         scratch_shapes=[pltpu.VMEM(shape, jnp.float32)],
     )(kappa_lat, sea_mask, kappa_lon)
 
@@ -325,11 +316,11 @@
 
 def shards(source, kappa_lon, kappa_lat, sea_mask):
     p_lon, u_lon, w_lon, edge_lon = lon_pass(source, kappa_lon, sea_mask, lax.axis_size("lon"))
-    u_lat, w_lat, left, right, diagonal, matrix_edge, scale = lat_matrix(kappa_lat, sea_mask, kappa_lon)
+    u_lat, w_lat, matrix_edge, scale = lat_matrix(kappa_lat, sea_mask, kappa_lon)
     before, here = lon_flux(edge_lon)
     flux = jnp.concatenate([before[None], here[None], jnp.zeros((6,) + before.shape, jnp.float32)], 0)
     p_lat, edge_lat = lat_rhs(
-        p_lon, u_lon, w_lon, flux, sea_mask, left, right, diagonal, matrix_edge,
+        p_lon, u_lon, w_lon, flux, kappa_lat, sea_mask, matrix_edge,
     )
     before, here = interface_flux(edge_lat, 0, "lat", False, "all_gather")
     return scale * (p_lat - u_lat * before[:, None, :] + w_lat * here[:, None, :])

time: 65.8 us -> 65.8 us (level)
  no operation moved by 1% of the time
where the time goes in v11:
time: 65.8 us; the launch traced here: 65.5 us
  blocking collectives  40.9 us (62%)
  Pallas kernels  8.12 us (12%)
  starting transfers between devices  7.57 us (12%)
  waiting for transfers between devices  3.95 us (6%)
  other arithmetic  2.44 us (4%)
  local copies, waits for them, and re-layouts  1.73 us (3%)
  between operations  0.8 us (1%)
    all_gather x1, blocking collectives, interface_flux(): gathered = lax.all_gather(terms[None], mesh_axis, axis=0, tiled=True)  40.9 us
    all_to_all x1, starting transfers between devices, lon_flux(): gathered = lax.all_to_all(copies, 'lon', 0, 0, tiled=True)  7.57 us
    all_to_all x1, waiting for transfers between devices, lon_flux(): gathered = lax.all_to_all(copies, 'lon', 0, 0, tiled=True)  3.95 us
    pallas_call x1, Pallas kernels, lon_pass(): pl.pallas_call(lon_kernel, out_shape=(full, full, full, edge))  2.95 us
    pallas_call x1, Pallas kernels, lat_matrix(): pl.pallas_call(lat_matrix_kernel, out_shape=(full, full, edge, full), scr...  2.63 us
    pallas_call x1, Pallas kernels, lat_rhs(): pl.pallas_call(lat_rhs_kernel, out_shape=(jax.ShapeDtypeStruct(shape, jnp...  2.55 us
  transfers between devices with their start and end apart: 1, of which 1 were waited for; matrix products, arithmetic and copies ran while one was open for 0% of the time, Pallas kernels for 4%

profile of v11, /device:TPU:1, one launch (start us, length us, event | category | flops | bytes accessed | tf_op | source)
XLA Modules:
  0.0 65.5 jit_solution(12365261466655563895)
XLA Ops:
  0.0 3.0 %shard_map.47 = (f32[8,32,128]{2,1,0:T(8,128)}, f32[8,32,128]{2,1,0:T(8,128)}, f32[8,32,128]{2,1,0:T(8,128)}, f32[16,7,256]{2,1,0:T(8,128)}) custom-call(f32[8,32,128]{2,1,0:T(8,128)} %source_ref.1, bf16[8,32,128]{2,1,0:T(8,128)(2,1)} %kappa_ref.4, s32[8,32,128]{2,1,0:T(8,128)} %mask_ref.5), custom_call_target="tpu_custom_call" | custom-call | tf_op jit(solution)/shard_map/pallas_call | solution.py:161
  3.0 7.6 %all-to-all-start = ((f32[16,7,256]{2,1,0:T(8,128)}), f32[16,7,256]{2,1,0:T(8,128)S(1)}, u32[]{:S(2)}, u32[]{:S(2)}) async-start(f32[16,7,256]{2,1,0:T(8,128)} %get-tuple-element.19), calls=%async_computation | async-start | bytes 262144 | tf_op jit(solution)/shard_map/all_to_all | solution.py:308
  10.6 2.6 %shard_map.46 = (f32[8,32,128]{2,1,0:T(8,128)}, f32[8,32,128]{2,1,0:T(8,128)}, f32[5,8,128]{2,1,0:T(8,128)}, f32[8,32,128]{2,1,0:T(8,128)}) custom-call(bf16[8,32,128]{2,1,0:T(8,128)(2,1)} %kappa_ref.5, s32[8,32,128]{2,1,0:T(8,128)} %mask_ref.5, bf16[8,32,128]{2,1,0:T(8,128)(2,1)} %kappa_ref.4), custom_call_target="tpu_custom_call" | custom-call | tf_op jit(solution)/shard_map/pallas_call | solution.py:227
  13.2 0.1 pad.78.clone
  13.3 4.0 %all-to-all-done = f32[16,7,256]{2,1,0:T(8,128)S(1)} async-done(((f32[16,7,256]{2,1,0:T(8,128)}), f32[16,7,256]{2,1,0:T(8,128)S(1)}, u32[]{:S(2)}, u32[]{:S(2)}) %all-to-all-start) | async-done | bytes 114720 | tf_op jit(solution)/shard_map/all_to_all | solution.py:308
  17.3 0.1 fusion.84
  18.0 0.7 %maximum_maximum_fusion.flux_ref = f32[8,256]{1,0:T(8,128)} fusion(f32[1,256]{1,0:T(1,128)S(1)} %get-tuple-element.143, f32[1,256]{1,0:T(1,128)S(1)} %get-tuple-element.142, f32[8]{0:T(128)S(1)} %pad.78.clone), kind=kLoop, calls=%fused_computation.140 | loop fusion | flops 4096 | bytes 10272 | tf_op jit(solution)/shard_map/concatenate | solution.py:321
  18.7 2.5 %shard_map.48 = (f32[8,32,128]{2,1,0:T(8,128)}, f32[7,8,128]{2,1,0:T(8,128)}) custom-call(f32[8,32,128]{2,1,0:T(8,128)} %get-tuple-element.16.p_ref, f32[8,32,128]{2,1,0:T(8,128)} %get-tuple-element.17.u_ref, f32[8,32,128]{2,1,0:T(8,128)} %get-tuple-element.18.w_ref, f32[8,256]{1,0:T(8,128)} %maximum_maximum_fusion.flux_ref, bf16[8,32,128]{2,1,0:T(8,128)(2,1)} %kappa_ref.5, ...), custom_call_target="tpu_custom_call" | custom-call | tf_op jit(solution)/shard_map/pallas_call | solution.py:236
  21.2 40.9 %all-gather = f32[224,8,128]{2,1,0:T(8,128)S(1)} all-gather(f32[7,8,128]{2,1,0:T(8,128)} %get-tuple-element.23), channel_id=2, replica_groups=mesh['lat'=32,'lon'=16] {'lat'}, dimensions={0}, use_global_device_ids=true | all-gather | bytes 946176 | tf_op jit(solution)/shard_map/all_gather | solution.py:297
  62.2 0.2 subtract_divide_fusion.4
  62.4 0.1 fusion.8
  62.6 0.1 subtract_divide_fusion.3
  62.8 0.1 fusion.12
  63.0 0.1 subtract_divide_fusion.2
  63.1 0.1 fusion.16
  63.3 0.1 subtract_divide_fusion.1
  63.5 0.1 subtract_divide_fusion
  63.7 0.0 copy-start
  63.7 0.0 copy-start.1
  63.7 0.0 copy-start.2
  63.8 0.0 copy-start.3
  63.8 0.1 add_divide_fusion
  63.9 0.8 %copy-done = f32[8,32,128]{2,1,0:T(8,128)S(1)} copy-done((f32[8,32,128]{2,1,0:T(8,128)S(1)}, f32[8,32,128]{2,1,0:T(8,128)}, u32[]{:S(2)}) %copy-start) | copy-done | bytes 131096
  64.6 0.1 copy-done.1
  64.7 0.1 copy-done.2
  64.8 0.1 copy-done.3
  64.8 0.7 %add_multiply_fusion = f32[8,32,128]{2,1,0:T(8,128)} fusion(f32[8,32,128]{2,1,0:T(8,128)S(1)} %copy-done.2, f32[8,32,128]{2,1,0:T(8,128)S(1)} %copy-done.1, f32[8,32,128]{2,1,0:T(8,128)S(1)} %copy-done.3, f32[8,32,128]{2,1,0:T(8,128)S(1)} %copy-done, f32[8,128]{1,0:T(8,128)S(1)} %get-tuple-element.77, f32[8,128]{1,0:T(8,128)S(1)} %get-tuple-element.76), kind=kLoop, calls=%fused_computation.65 | loop fusion | flops 163840 | bytes 663552 | tf_op jit(solution)/shard_map/mul | solution.py:326
  (93 shorter events, 0.9 us)
Async XLA Ops:
  3.0 14.3 %all-to-all-start = ((f32[16,7,256]{2,1,0:T(8,128)}), f32[16,7,256]{2,1,0:T(8,128)S(1)}, u32[]{:S(2)}, u32[]{:S(2)}) async-start(f32[16,7,256]{2,1,0:T(8,128)} %get-tuple-element.19), calls=%async_computation | async-start | bytes 262144 | tf_op jit(solution)/shard_map/all_to_all | solution.py:308
  63.7 0.9 %copy-start = (f32[8,32,128]{2,1,0:T(8,128)S(1)}, f32[8,32,128]{2,1,0:T(8,128)}, u32[]{:S(2)}) copy-start(f32[8,32,128]{2,1,0:T(8,128)} %get-tuple-element.22) | copy-start | bytes 393220
  63.7 1.0 %copy-start.1 = (f32[8,32,128]{2,1,0:T(8,128)S(1)}, f32[8,32,128]{2,1,0:T(8,128)}, u32[]{:S(2)}) copy-start(f32[8,32,128]{2,1,0:T(8,128)} %get-tuple-element.24) | copy-start | bytes 393220
  63.7 1.0 %copy-start.2 = (f32[8,32,128]{2,1,0:T(8,128)S(1)}, f32[8,32,128]{2,1,0:T(8,128)}, u32[]{:S(2)}) copy-start(f32[8,32,128]{2,1,0:T(8,128)} %get-tuple-element.15) | copy-start | bytes 393220
  63.8 1.1 %copy-start.3 = (f32[8,32,128]{2,1,0:T(8,128)S(1)}, f32[8,32,128]{2,1,0:T(8,128)}, u32[]{:S(2)}) copy-start(f32[8,32,128]{2,1,0:T(8,128)} %get-tuple-element.21) | copy-start | bytes 393220

commit v12 on v11

--- a/solution.py
+++ b/solution.py
@@ -197,13 +197,26 @@
     return wet, weight, position, left_face, right_face
 
 
-def lat_rhs_kernel(p_ref, u_ref, w_ref, flux_ref, kappa_ref, mask_ref, matrix_edge_ref,
-                   p_out, edge_out):
+def lat_rhs_kernel(index_ref, gathered_ref, p_ref, u_ref, w_ref, kappa_ref, mask_ref,
+                   matrix_edge_ref, p_out, edge_out):
     axis = 1
+    terms = [gathered_ref[:, k, :] for k in range(TERMS)]
+    flux = flux_system(terms, True, lambda values, shift, along: shifted(values, shift, along))
+    devices, lines = flux.shape
+    device = lax.broadcasted_iota(jnp.int32, flux.shape, 0)
+    index = index_ref[0]
+
+    def pick(place):
+        return jnp.sum(jnp.where(device == place, flux, 0.0), axis=0, keepdims=True)
+
     levels, rows, width = p_ref.shape
-    lines = flux_ref.shape[1]
     padded = jnp.concatenate(
-        [flux_ref[...], jnp.zeros((width - flux_ref.shape[0], lines), jnp.float32)], 0
+        [
+            pick((index + devices - 1) % devices),
+            pick(index),
+            jnp.zeros((width - 2, lines), jnp.float32),
+        ],
+        0,
     )
     columns = jnp.transpose(padded)
     before = columns[:, 0:1].reshape(levels, rows, 1)
@@ -231,47 +244,51 @@
     )(kappa_lat, sea_mask, kappa_lon)
 
 
-def lat_rhs(*inputs):
+def lat_rhs(gathered, *inputs):
     shape = inputs[0].shape
+    index = jnp.full((1,), lax.axis_index("lon"), jnp.int32)
+    vmem = pl.BlockSpec(memory_space=pltpu.VMEM)
     return pl.pallas_call(
         lat_rhs_kernel,
         out_shape=(
             jax.ShapeDtypeStruct(shape, jnp.float32),
             jax.ShapeDtypeStruct((TERMS, shape[0], shape[2]), jnp.float32),
         ),
-    )(*inputs)
-
-
-def circular_solve(lower_band, upper_band, excess, sources):
+        in_specs=[pl.BlockSpec(memory_space=pltpu.SMEM)] + [vmem] * (1 + len(inputs)),
+        out_specs=(vmem, vmem),
+    )(index, gathered, *inputs)
+
+
+def circular_solve(lower_band, upper_band, excess, sources, roll=jnp.roll):
     devices = lower_band.shape[0]
     stride = 1
     while stride < devices:
         inverse = 1.0 / (excess - lower_band - upper_band)
-        left_weight = -lower_band * jnp.roll(inverse, stride, 0)
-        right_coefficient = -upper_band * jnp.roll(inverse, -stride, 0)
-        new_lower = left_weight * jnp.roll(lower_band, stride, 0)
-        new_upper = right_coefficient * jnp.roll(upper_band, -stride, 0)
+        left_weight = -lower_band * roll(inverse, stride, 0)
+        right_coefficient = -upper_band * roll(inverse, -stride, 0)
+        new_lower = left_weight * roll(lower_band, stride, 0)
+        new_upper = right_coefficient * roll(upper_band, -stride, 0)
         excess = (
             excess
-            + left_weight * jnp.roll(excess, stride, 0)
-            + right_coefficient * jnp.roll(excess, -stride, 0)
+            + left_weight * roll(excess, stride, 0)
+            + right_coefficient * roll(excess, -stride, 0)
         )
         sources = (
             sources
-            + left_weight * jnp.roll(sources, stride, 0)
-            + right_coefficient * jnp.roll(sources, -stride, 0)
+            + left_weight * roll(sources, stride, 0)
+            + right_coefficient * roll(sources, -stride, 0)
         )
         lower_band, upper_band = (new_lower, new_upper)
         stride = stride * 2
     return sources / excess
 
 
-def flux_system(terms, periodic):
+def flux_system(terms, periodic, roll=jnp.roll):
     head_p, head_u, head_w, tail_kappa, tail_u, tail_w, tail_p = terms
     devices = head_p.shape[0]
 
     def next_of(member):
-        return jnp.roll(member, -1, 0)
+        return roll(member, -1, 0)
 
     next_wet = jnp.where(next_of(head_u) > 0.0, 1.0, 0.0)
     face = tail_kappa * next_wet
@@ -283,7 +300,7 @@
     upper = -tail_kappa * next_of(head_w)
     diagonal = 1.0 + tail_kappa * next_of(head_u) + face * tail_w
     return circular_solve(
-        lower, upper, diagonal + lower + upper, tail_kappa * next_of(head_p) - face * tail_p
+        lower, upper, diagonal + lower + upper, tail_kappa * next_of(head_p) - face * tail_p, roll
     )
 
 
@@ -317,10 +334,9 @@
 def shards(source, kappa_lon, kappa_lat, sea_mask):
     p_lon, u_lon, w_lon, edge_lon = lon_pass(source, kappa_lon, sea_mask, lax.axis_size("lon"))
     u_lat, w_lat, matrix_edge, scale = lat_matrix(kappa_lat, sea_mask, kappa_lon)
-    before, here = lon_flux(edge_lon)
-    flux = jnp.concatenate([before[None], here[None], jnp.zeros((6,) + before.shape, jnp.float32)], 0)
+    gathered = lax.all_to_all(edge_lon, "lon", 0, 0, tiled=True)
     p_lat, edge_lat = lat_rhs(
-        p_lon, u_lon, w_lon, flux, kappa_lat, sea_mask, matrix_edge,
+        gathered, p_lon, u_lon, w_lon, kappa_lat, sea_mask, matrix_edge,
     )
     before, here = interface_flux(edge_lat, 0, "lat", False, "all_gather")
     return scale * (p_lat - u_lat * before[:, None, :] + w_lat * here[:, None, :])

time: 65.8 us -> 65 us (0.988)
  other arithmetic: 2.44 us -> 1.51 us
    concatenate x1 -> x0, other arithmetic: 0.66 us -> none  [shards(): jnp.concatenate([before[None], here[None], jnp.zeros((6,) + before.shape,...]
    unnamed x9 -> x10, local copies, waits for them, and re-layouts: 0.96 us -> 1.6 us
where the time goes in v12:
time: 65 us; the launch traced here: 64.8 us
  blocking collectives  40.9 us (63%)
  Pallas kernels  8.28 us (13%)
  starting transfers between devices  7.57 us (12%)
  waiting for transfers between devices  4.04 us (6%)
  local copies, waits for them, and re-layouts  2.03 us (3%)
  other arithmetic  1.51 us (2%)
    all_gather x1, blocking collectives, interface_flux(): gathered = lax.all_gather(terms[None], mesh_axis, axis=0, tiled=True)  40.9 us
    all_to_all x1, starting transfers between devices, shards(): gathered = lax.all_to_all(edge_lon, 'lon', 0, 0, tiled=True)  7.57 us
    all_to_all x1, waiting for transfers between devices, shards(): gathered = lax.all_to_all(edge_lon, 'lon', 0, 0, tiled=True)  4.04 us
    pallas_call x1, Pallas kernels, lon_pass(): pl.pallas_call(lon_kernel, out_shape=(full, full, full, edge))  2.97 us
    pallas_call x1, Pallas kernels, lat_rhs(): pl.pallas_call(lat_rhs_kernel, out_shape=(jax.ShapeDtypeStruct(shape, jnp...  2.69 us
    pallas_call x1, Pallas kernels, lat_matrix(): pl.pallas_call(lat_matrix_kernel, out_shape=(full, full, edge, full), scr...  2.63 us
    unnamed x10, local copies, waits for them, and re-layouts  1.6 us
  transfers between devices with their start and end apart: 1, of which 1 were waited for; matrix products, arithmetic and copies ran while one was open for 0% of the time, Pallas kernels for 4%

profile of v12, /device:TPU:1, one launch (start us, length us, event | category | flops | bytes accessed | tf_op | source)
XLA Modules:
  0.0 64.8 jit_solution(8673969464840107894)
XLA Ops:
  0.0 3.0 %shard_map.47 = (f32[8,32,128]{2,1,0:T(8,128)}, f32[8,32,128]{2,1,0:T(8,128)}, f32[8,32,128]{2,1,0:T(8,128)}, f32[16,7,256]{2,1,0:T(8,128)}) custom-call(f32[8,32,128]{2,1,0:T(8,128)} %source_ref.1, bf16[8,32,128]{2,1,0:T(8,128)(2,1)} %kappa_ref.4, s32[8,32,128]{2,1,0:T(8,128)} %mask_ref.5), custom_call_target="tpu_custom_call" | custom-call | tf_op jit(solution)/shard_map/pallas_call | solution.py:161
  3.0 7.6 %all-to-all-start = ((f32[16,7,256]{2,1,0:T(8,128)}), f32[16,7,256]{2,1,0:T(8,128)S(1)}, u32[]{:S(2)}, u32[]{:S(2)}) async-start(f32[16,7,256]{2,1,0:T(8,128)} %get-tuple-element.16), calls=%async_computation | async-start | bytes 262144 | tf_op jit(solution)/shard_map/all_to_all | solution.py:337
  10.6 2.6 %shard_map.46 = (f32[8,32,128]{2,1,0:T(8,128)}, f32[8,32,128]{2,1,0:T(8,128)}, f32[5,8,128]{2,1,0:T(8,128)}, f32[8,32,128]{2,1,0:T(8,128)}) custom-call(bf16[8,32,128]{2,1,0:T(8,128)(2,1)} %kappa_ref.5, s32[8,32,128]{2,1,0:T(8,128)} %mask_ref.5, bf16[8,32,128]{2,1,0:T(8,128)(2,1)} %kappa_ref.4), custom_call_target="tpu_custom_call" | custom-call | tf_op jit(solution)/shard_map/pallas_call | solution.py:240
  13.2 4.0 %all-to-all-done.gathered_ref = f32[16,7,256]{2,1,0:T(8,128)S(1)} async-done(((f32[16,7,256]{2,1,0:T(8,128)}), f32[16,7,256]{2,1,0:T(8,128)S(1)}, u32[]{:S(2)}, u32[]{:S(2)}) %all-to-all-start) | async-done | bytes 114720 | tf_op jit(solution)/shard_map/all_to_all | solution.py:337
  17.2 0.0 copy-start
  17.2 0.6 copy-done
  17.9 2.7 %shard_map.48 = (f32[8,32,128]{2,1,0:T(8,128)}, f32[7,8,128]{2,1,0:T(8,128)}) custom-call(s32[1]{0:T(128)} %bitcast.index_ref, f32[16,7,256]{2,1,0:T(8,128)} %copy-done, f32[8,32,128]{2,1,0:T(8,128)} %get-tuple-element.17.p_ref, f32[8,32,128]{2,1,0:T(8,128)} %get-tuple-element.18.u_ref, f32[8,32,128]{2,1,0:T(8,128)} %get-tuple-element.19.w_ref, ...), custom_call_target="tpu_custom_call" | custom-call | tf_op jit(solution)/shard_map/pallas_call | solution.py:251
  20.6 40.9 %all-gather = f32[224,8,128]{2,1,0:T(8,128)S(1)} all-gather(f32[7,8,128]{2,1,0:T(8,128)} %get-tuple-element.23), channel_id=2, replica_groups=mesh['lat'=32,'lon'=16] {'lat'}, dimensions={0}, use_global_device_ids=true | all-gather | bytes 946176 | tf_op jit(solution)/shard_map/all_gather | solution.py:314
  61.5 0.2 subtract_divide_fusion.4
  61.8 0.1 fusion.8
  62.0 0.1 subtract_divide_fusion.3
  62.1 0.1 fusion.12
  62.3 0.1 subtract_divide_fusion.2
  62.4 0.1 fusion.16
  62.6 0.1 subtract_divide_fusion.1
  62.8 0.1 subtract_divide_fusion
  63.0 0.0 copy-start.1
  63.0 0.0 copy-start.2
  63.0 0.0 copy-start.3
  63.0 0.0 copy-start.4
  63.0 0.1 add_divide_fusion
  63.1 0.8 %copy-done.1 = f32[8,32,128]{2,1,0:T(8,128)S(1)} copy-done((f32[8,32,128]{2,1,0:T(8,128)S(1)}, f32[8,32,128]{2,1,0:T(8,128)}, u32[]{:S(2)}) %copy-start.1) | copy-done | bytes 131096
  63.9 0.1 copy-done.2
  64.0 0.1 copy-done.3
  64.0 0.1 copy-done.4
  64.1 0.7 %add_multiply_fusion = f32[8,32,128]{2,1,0:T(8,128)} fusion(f32[8,32,128]{2,1,0:T(8,128)S(1)} %copy-done.3, f32[8,32,128]{2,1,0:T(8,128)S(1)} %copy-done.2, f32[8,32,128]{2,1,0:T(8,128)S(1)} %copy-done.4, f32[8,32,128]{2,1,0:T(8,128)S(1)} %copy-done.1, f32[8,128]{1,0:T(8,128)S(1)} %get-tuple-element.53, f32[8,128]{1,0:T(8,128)S(1)} %get-tuple-element.52), kind=kLoop, calls=%fused_computation.65 | loop fusion | flops 163840 | bytes 663552 | tf_op jit(solution)/shard_map/mul | solution.py:342
  (46 shorter events, 0.5 us)
Async XLA Ops:
  3.0 14.3 %all-to-all-start = ((f32[16,7,256]{2,1,0:T(8,128)}), f32[16,7,256]{2,1,0:T(8,128)S(1)}, u32[]{:S(2)}, u32[]{:S(2)}) async-start(f32[16,7,256]{2,1,0:T(8,128)} %get-tuple-element.16), calls=%async_computation | async-start | bytes 262144 | tf_op jit(solution)/shard_map/all_to_all | solution.py:337
  17.2 0.6 copy-start
  63.0 0.9 %copy-start.1 = (f32[8,32,128]{2,1,0:T(8,128)S(1)}, f32[8,32,128]{2,1,0:T(8,128)}, u32[]{:S(2)}) copy-start(f32[8,32,128]{2,1,0:T(8,128)} %get-tuple-element.22) | copy-start | bytes 393220
  63.0 1.0 %copy-start.2 = (f32[8,32,128]{2,1,0:T(8,128)S(1)}, f32[8,32,128]{2,1,0:T(8,128)}, u32[]{:S(2)}) copy-start(f32[8,32,128]{2,1,0:T(8,128)} %get-tuple-element.24) | copy-start | bytes 393220
  63.0 1.0 %copy-start.3 = (f32[8,32,128]{2,1,0:T(8,128)S(1)}, f32[8,32,128]{2,1,0:T(8,128)}, u32[]{:S(2)}) copy-start(f32[8,32,128]{2,1,0:T(8,128)} %get-tuple-element.15) | copy-start | bytes 393220
  63.0 1.1 %copy-start.4 = (f32[8,32,128]{2,1,0:T(8,128)S(1)}, f32[8,32,128]{2,1,0:T(8,128)}, u32[]{:S(2)}) copy-start(f32[8,32,128]{2,1,0:T(8,128)} %get-tuple-element.21) | copy-start | bytes 393220

commit v13 on v12

--- a/solution.py
+++ b/solution.py
@@ -185,6 +185,8 @@
     edge_out[2] = weight_scratch[:, length - 1, :]
     edge_out[3] = u_out[:, length - 1, :]
     edge_out[4] = w_out[:, length - 1, :]
+    u_out[...] = scale_out[...] * from_left
+    w_out[...] = scale_out[...] * from_right
 
 
 def lat_faces(kappa_ref, mask_ref, axis):
@@ -198,7 +200,7 @@
 
 
 def lat_rhs_kernel(index_ref, gathered_ref, p_ref, u_ref, w_ref, kappa_ref, mask_ref,
-                   matrix_edge_ref, p_out, edge_out):
+                   matrix_edge_ref, scale_ref, p_out, edge_out):
     axis = 1
     terms = [gathered_ref[:, k, :] for k in range(TERMS)]
     flux = flux_system(terms, True, lambda values, shift, along: shifted(values, shift, along))
@@ -231,6 +233,7 @@
     edge_out[0] = mask_ref[:, 0, :].astype(jnp.float32) * p_out[:, 0, :]
     edge_out[1:TERMS - 1] = matrix_edge_ref[...]
     edge_out[TERMS - 1] = p_out[:, length - 1, :]
+    p_out[...] = scale_ref[...] * particular
 
 
 def lat_matrix(kappa_lat, sea_mask, kappa_lon):
@@ -336,10 +339,10 @@
     u_lat, w_lat, matrix_edge, scale = lat_matrix(kappa_lat, sea_mask, kappa_lon)
     gathered = lax.all_to_all(edge_lon, "lon", 0, 0, tiled=True)
     p_lat, edge_lat = lat_rhs(
-        gathered, p_lon, u_lon, w_lon, kappa_lat, sea_mask, matrix_edge,
+        gathered, p_lon, u_lon, w_lon, kappa_lat, sea_mask, matrix_edge, scale,
     )
     before, here = interface_flux(edge_lat, 0, "lat", False, "all_gather")
-    return scale * (p_lat - u_lat * before[:, None, :] + w_lat * here[:, None, :])
+    return p_lat - u_lat * before[:, None, :] + w_lat * here[:, None, :]
 
 
 def solution(mesh):

time: 65 us -> 65.1 us (level)
    mul x1 -> x0, other arithmetic: 0.7 us -> none  [shards(): scale * (p_lat - u_lat * before[:, None, :] + w_lat * here[:, None, :])]
    add x0 -> x1, other arithmetic: none -> 0.69 us  [shards(): return p_lat - u_lat * before[:, None, :] + w_lat * here[:, None, :]]
    unnamed x10 -> x8, local copies, waits for them, and re-layouts: 1.6 us -> 1.55 us
where the time goes in v13:
time: 65.1 us; the launch traced here: 64.8 us
  blocking collectives  40.9 us (63%)
  Pallas kernels  8.35 us (13%)
  starting transfers between devices  7.57 us (12%)
  waiting for transfers between devices  4.06 us (6%)
  local copies, waits for them, and re-layouts  1.99 us (3%)
  other arithmetic  1.5 us (2%)
    all_gather x1, blocking collectives, interface_flux(): gathered = lax.all_gather(terms[None], mesh_axis, axis=0, tiled=True)  40.9 us
    all_to_all x1, starting transfers between devices, shards(): gathered = lax.all_to_all(edge_lon, 'lon', 0, 0, tiled=True)  7.57 us
    all_to_all x1, waiting for transfers between devices, shards(): gathered = lax.all_to_all(edge_lon, 'lon', 0, 0, tiled=True)  4.06 us
    pallas_call x1, Pallas kernels, lon_pass(): pl.pallas_call(lon_kernel, out_shape=(full, full, full, edge))  2.96 us
    pallas_call x1, Pallas kernels, lat_rhs(): pl.pallas_call(lat_rhs_kernel, out_shape=(jax.ShapeDtypeStruct(shape, jnp...  2.78 us
    pallas_call x1, Pallas kernels, lat_matrix(): pl.pallas_call(lat_matrix_kernel, out_shape=(full, full, edge, full), scr...  2.61 us
    unnamed x8, local copies, waits for them, and re-layouts  1.55 us
  transfers between devices with their start and end apart: 1, of which 1 were waited for; matrix products, arithmetic and copies ran while one was open for 0% of the time, Pallas kernels for 4%

profile of v13, /device:TPU:1, one launch (start us, length us, event | category | flops | bytes accessed | tf_op | source)
XLA Modules:
  0.0 64.8 jit_solution(5921569850326740062)
XLA Ops:
  0.0 3.0 %shard_map.46 = (f32[8,32,128]{2,1,0:T(8,128)}, f32[8,32,128]{2,1,0:T(8,128)}, f32[8,32,128]{2,1,0:T(8,128)}, f32[16,7,256]{2,1,0:T(8,128)}) custom-call(f32[8,32,128]{2,1,0:T(8,128)} %source_ref.1, bf16[8,32,128]{2,1,0:T(8,128)(2,1)} %lon_kappa_ref.1, s32[8,32,128]{2,1,0:T(8,128)} %mask_ref.5), custom_call_target="tpu_custom_call" | custom-call | tf_op jit(solution)/shard_map/pallas_call | solution.py:161
  3.0 7.6 %all-to-all-start = ((f32[16,7,256]{2,1,0:T(8,128)}), f32[16,7,256]{2,1,0:T(8,128)S(1)}, u32[]{:S(2)}, u32[]{:S(2)}) async-start(f32[16,7,256]{2,1,0:T(8,128)} %get-tuple-element.15), calls=%async_computation | async-start | bytes 262144 | tf_op jit(solution)/shard_map/all_to_all | solution.py:340
  10.6 2.6 %shard_map.47 = (f32[8,32,128]{2,1,0:T(8,128)}, f32[8,32,128]{2,1,0:T(8,128)}, f32[5,8,128]{2,1,0:T(8,128)}, f32[8,32,128]{2,1,0:T(8,128)}) custom-call(bf16[8,32,128]{2,1,0:T(8,128)(2,1)} %kappa_ref.5, s32[8,32,128]{2,1,0:T(8,128)} %mask_ref.5, bf16[8,32,128]{2,1,0:T(8,128)(2,1)} %lon_kappa_ref.1), custom_call_target="tpu_custom_call" | custom-call | tf_op jit(solution)/shard_map/pallas_call | solution.py:243
  13.2 4.1 %all-to-all-done.gathered_ref = f32[16,7,256]{2,1,0:T(8,128)S(1)} async-done(((f32[16,7,256]{2,1,0:T(8,128)}), f32[16,7,256]{2,1,0:T(8,128)S(1)}, u32[]{:S(2)}, u32[]{:S(2)}) %all-to-all-start) | async-done | bytes 114720 | tf_op jit(solution)/shard_map/all_to_all | solution.py:340
  17.2 0.0 copy-start
  17.2 0.6 copy-done
  17.9 2.8 %shard_map.48 = (f32[8,32,128]{2,1,0:T(8,128)}, f32[7,8,128]{2,1,0:T(8,128)}) custom-call(s32[1]{0:T(128)} %bitcast.index_ref, f32[16,7,256]{2,1,0:T(8,128)} %copy-done, f32[8,32,128]{2,1,0:T(8,128)} %get-tuple-element.16.p_ref, f32[8,32,128]{2,1,0:T(8,128)} %get-tuple-element.17.u_ref, f32[8,32,128]{2,1,0:T(8,128)} %get-tuple-element.18.w_ref, ...), custom_call_target="tpu_custom_call" | custom-call | tf_op jit(solution)/shard_map/pallas_call | solution.py:254
  20.7 40.9 %all-gather = f32[224,8,128]{2,1,0:T(8,128)S(1)} all-gather(f32[7,8,128]{2,1,0:T(8,128)} %get-tuple-element.23), channel_id=2, replica_groups=mesh['lat'=32,'lon'=16] {'lat'}, dimensions={0}, use_global_device_ids=true | all-gather | bytes 946176 | tf_op jit(solution)/shard_map/all_gather | solution.py:317
  61.6 0.2 subtract_divide_fusion.4
  61.9 0.1 fusion.8
  62.0 0.1 subtract_divide_fusion.3
  62.2 0.1 fusion.12
  62.4 0.1 subtract_divide_fusion.2
  62.5 0.1 fusion.16
  62.7 0.1 subtract_divide_fusion.1
  62.9 0.1 subtract_divide_fusion
  63.1 0.0 copy-start.1
  63.1 0.0 copy-start.2
  63.1 0.0 copy-start.3
  63.1 0.1 add_divide_fusion
  63.2 0.8 %copy-done.1 = f32[8,32,128]{2,1,0:T(8,128)S(1)} copy-done((f32[8,32,128]{2,1,0:T(8,128)S(1)}, f32[8,32,128]{2,1,0:T(8,128)}, u32[]{:S(2)}) %copy-start.1) | copy-done | bytes 131096
  64.0 0.1 copy-done.2
  64.1 0.1 copy-done.3
  64.1 0.7 %multiply_add_fusion = f32[8,32,128]{2,1,0:T(8,128)} fusion(f32[8,32,128]{2,1,0:T(8,128)S(1)} %copy-done.2, f32[8,32,128]{2,1,0:T(8,128)S(1)} %copy-done.3, f32[8,32,128]{2,1,0:T(8,128)S(1)} %copy-done.1, f32[8,128]{1,0:T(8,128)S(1)} %get-tuple-element.53, f32[8,128]{1,0:T(8,128)S(1)} %get-tuple-element.52), kind=kLoop, calls=%fused_computation.65 | loop fusion | flops 131072 | bytes 532480 | tf_op jit(solution)/shard_map/add | solution.py:345
  (46 shorter events, 0.5 us)
Async XLA Ops:
  3.0 14.3 %all-to-all-start = ((f32[16,7,256]{2,1,0:T(8,128)}), f32[16,7,256]{2,1,0:T(8,128)S(1)}, u32[]{:S(2)}, u32[]{:S(2)}) async-start(f32[16,7,256]{2,1,0:T(8,128)} %get-tuple-element.15), calls=%async_computation | async-start | bytes 262144 | tf_op jit(solution)/shard_map/all_to_all | solution.py:340
  17.2 0.6 %copy-start = (f32[16,7,256]{2,1,0:T(8,128)}, f32[16,7,256]{2,1,0:T(8,128)S(1)}, u32[]{:S(2)}) copy-start(f32[16,7,256]{2,1,0:T(8,128)S(1)} %all-to-all-done.gathered_ref) | copy-start | bytes 344068
  63.1 0.9 %copy-start.1 = (f32[8,32,128]{2,1,0:T(8,128)S(1)}, f32[8,32,128]{2,1,0:T(8,128)}, u32[]{:S(2)}) copy-start(f32[8,32,128]{2,1,0:T(8,128)} %get-tuple-element.22) | copy-start | bytes 393220
  63.1 1.0 %copy-start.2 = (f32[8,32,128]{2,1,0:T(8,128)S(1)}, f32[8,32,128]{2,1,0:T(8,128)}, u32[]{:S(2)}) copy-start(f32[8,32,128]{2,1,0:T(8,128)} %get-tuple-element.24) | copy-start | bytes 393220
  63.1 1.0 %copy-start.3 = (f32[8,32,128]{2,1,0:T(8,128)S(1)}, f32[8,32,128]{2,1,0:T(8,128)}, u32[]{:S(2)}) copy-start(f32[8,32,128]{2,1,0:T(8,128)} %get-tuple-element.21) | copy-start | bytes 393220

commit v14 on v12

--- a/solution.py
+++ b/solution.py
@@ -299,6 +299,21 @@
     lower = -face * tail_u
     upper = -tail_kappa * next_of(head_w)
     diagonal = 1.0 + tail_kappa * next_of(head_u) + face * tail_w
+    if not periodic:
+        sources = tail_kappa * next_of(head_p) - face * tail_p
+        ratios, reduced = [], []
+        for place in range(devices):
+            pivot = diagonal[place]
+            source = sources[place]
+            if place > 0:
+                pivot = pivot - lower[place] * ratios[-1]
+                source = source - lower[place] * reduced[-1]
+            ratios.append(upper[place] / pivot)
+            reduced.append(source / pivot)
+        solved = [reduced[-1]]
+        for place in range(devices - 2, -1, -1):
+            solved.append(reduced[place] - ratios[place] * solved[-1])
+        return jnp.stack(solved[::-1], 0)
     return circular_solve(
         lower, upper, diagonal + lower + upper, tail_kappa * next_of(head_p) - face * tail_p, roll
     )

time: 65 us -> 64.3 us (0.989)
    unnamed x10 -> x25, local copies, waits for them, and re-layouts: 1.6 us -> 1.47 us
where the time goes in v14:
time: 64.3 us; the launch traced here: 64 us
  blocking collectives  40.9 us (64%)
  Pallas kernels  8.27 us (13%)
  starting transfers between devices  7.57 us (12%)
  waiting for transfers between devices  4.04 us (6%)
  local copies, waits for them, and re-layouts  1.51 us (2%)
  other arithmetic  1.39 us (2%)
    all_gather x1, blocking collectives, interface_flux(): gathered = lax.all_gather(terms[None], mesh_axis, axis=0, tiled=True)  40.9 us
    all_to_all x1, starting transfers between devices, shards(): gathered = lax.all_to_all(edge_lon, 'lon', 0, 0, tiled=True)  7.57 us
    all_to_all x1, waiting for transfers between devices, shards(): gathered = lax.all_to_all(edge_lon, 'lon', 0, 0, tiled=True)  4.04 us
    pallas_call x1, Pallas kernels, lon_pass(): pl.pallas_call(lon_kernel, out_shape=(full, full, full, edge))  2.96 us
    pallas_call x1, Pallas kernels, lat_rhs(): pl.pallas_call(lat_rhs_kernel, out_shape=(jax.ShapeDtypeStruct(shape, jnp...  2.68 us
    pallas_call x1, Pallas kernels, lat_matrix(): pl.pallas_call(lat_matrix_kernel, out_shape=(full, full, edge, full), scr...  2.63 us
    unnamed x25, local copies, waits for them, and re-layouts  1.47 us
  transfers between devices with their start and end apart: 1, of which 1 were waited for; matrix products, arithmetic and copies ran while one was open for 0% of the time, Pallas kernels for 4%

profile of v14, /device:TPU:1, one launch (start us, length us, event | category | flops | bytes accessed | tf_op | source)
XLA Modules:
  0.0 64.0 jit_solution(1852678462783597241)
XLA Ops:
  0.0 3.0 %shard_map.47 = (f32[8,32,128]{2,1,0:T(8,128)}, f32[8,32,128]{2,1,0:T(8,128)}, f32[8,32,128]{2,1,0:T(8,128)}, f32[16,7,256]{2,1,0:T(8,128)}) custom-call(f32[8,32,128]{2,1,0:T(8,128)} %source_ref.1, bf16[8,32,128]{2,1,0:T(8,128)(2,1)} %kappa_ref.4, s32[8,32,128]{2,1,0:T(8,128)} %mask_ref.5), custom_call_target="tpu_custom_call" | custom-call | tf_op jit(solution)/shard_map/pallas_call | solution.py:161
  3.0 7.6 %all-to-all-start = ((f32[16,7,256]{2,1,0:T(8,128)}), f32[16,7,256]{2,1,0:T(8,128)S(1)}, u32[]{:S(2)}, u32[]{:S(2)}) async-start(f32[16,7,256]{2,1,0:T(8,128)} %get-tuple-element.16), calls=%async_computation | async-start | bytes 262144 | tf_op jit(solution)/shard_map/all_to_all | solution.py:352
  10.6 2.6 %shard_map.46 = (f32[8,32,128]{2,1,0:T(8,128)}, f32[8,32,128]{2,1,0:T(8,128)}, f32[5,8,128]{2,1,0:T(8,128)}, f32[8,32,128]{2,1,0:T(8,128)}) custom-call(bf16[8,32,128]{2,1,0:T(8,128)(2,1)} %kappa_ref.5, s32[8,32,128]{2,1,0:T(8,128)} %mask_ref.5, bf16[8,32,128]{2,1,0:T(8,128)(2,1)} %kappa_ref.4), custom_call_target="tpu_custom_call" | custom-call | tf_op jit(solution)/shard_map/pallas_call | solution.py:240
  13.2 4.0 %all-to-all-done.gathered_ref = f32[16,7,256]{2,1,0:T(8,128)S(1)} async-done(((f32[16,7,256]{2,1,0:T(8,128)}), f32[16,7,256]{2,1,0:T(8,128)S(1)}, u32[]{:S(2)}, u32[]{:S(2)}) %all-to-all-start) | async-done | bytes 114720 | tf_op jit(solution)/shard_map/all_to_all | solution.py:352
  17.2 0.0 copy-start
  17.2 0.7 %copy-done = f32[16,7,256]{2,1,0:T(8,128)} copy-done((f32[16,7,256]{2,1,0:T(8,128)}, f32[16,7,256]{2,1,0:T(8,128)S(1)}, u32[]{:S(2)}) %copy-start) | copy-done | bytes 114712
  17.9 2.7 %shard_map.48 = (f32[8,32,128]{2,1,0:T(8,128)}, f32[7,8,128]{2,1,0:T(8,128)}) custom-call(s32[1]{0:T(128)} %bitcast.index_ref, f32[16,7,256]{2,1,0:T(8,128)} %copy-done, f32[8,32,128]{2,1,0:T(8,128)} %get-tuple-element.17.p_ref, f32[8,32,128]{2,1,0:T(8,128)} %get-tuple-element.18.u_ref, f32[8,32,128]{2,1,0:T(8,128)} %get-tuple-element.19.w_ref, ...), custom_call_target="tpu_custom_call" | custom-call | tf_op jit(solution)/shard_map/pallas_call | solution.py:251
  20.6 40.9 %all-gather = f32[224,8,128]{2,1,0:T(8,128)S(1)} all-gather(f32[7,8,128]{2,1,0:T(8,128)} %get-tuple-element.23), channel_id=2, replica_groups=mesh['lat'=32,'lon'=16] {'lat'}, dimensions={0}, use_global_device_ids=true | all-gather | bytes 946176 | tf_op jit(solution)/shard_map/all_gather | solution.py:329
  61.5 0.1 fusion
  61.7 0.3 fusion.8
  61.9 0.0 copy-start.4
  62.0 0.1 constant_dynamic-update-slice_fusion.31
  62.2 0.0 copy-start.3
  62.3 0.0 copy-start.2
  62.3 0.0 copy-start.1
  62.5 0.3 copy-done.4
  62.9 0.2 copy-done.3
  63.1 0.1 copy-done.2
  63.2 0.1 copy-done.1
  63.3 0.7 %add_multiply_fusion = f32[8,32,128]{2,1,0:T(8,128)} fusion(f32[8,32,128]{2,1,0:T(8,128)S(1)} %copy-done.3, f32[8,32,128]{2,1,0:T(8,128)S(1)} %copy-done.2, f32[8,32,128]{2,1,0:T(8,128)S(1)} %copy-done.4, f32[8,32,128]{2,1,0:T(8,128)S(1)} %copy-done.1, f32[8,128]{1,0:T(8,128)S(1)} %get-tuple-element.113, f32[8,128]{1,0:T(8,128)S(1)} %get-tuple-element.112), kind=kLoop, calls=%fused_computation.12 | loop fusion | flops 163840 | bytes 663552 | tf_op jit(solution)/shard_map/mul | solution.py:357
  (35 shorter events, 0.2 us)
Async XLA Ops:
  3.0 14.3 %all-to-all-start = ((f32[16,7,256]{2,1,0:T(8,128)}), f32[16,7,256]{2,1,0:T(8,128)S(1)}, u32[]{:S(2)}, u32[]{:S(2)}) async-start(f32[16,7,256]{2,1,0:T(8,128)} %get-tuple-element.16), calls=%async_computation | async-start | bytes 262144 | tf_op jit(solution)/shard_map/all_to_all | solution.py:352
  17.2 0.7 %copy-start = (f32[16,7,256]{2,1,0:T(8,128)}, f32[16,7,256]{2,1,0:T(8,128)S(1)}, u32[]{:S(2)}) copy-start(f32[16,7,256]{2,1,0:T(8,128)S(1)} %all-to-all-done.gathered_ref) | copy-start | bytes 344068
  61.9 0.9 %copy-start.4 = (f32[8,32,128]{2,1,0:T(8,128)S(1)}, f32[8,32,128]{2,1,0:T(8,128)}, u32[]{:S(2)}) copy-start(f32[8,32,128]{2,1,0:T(8,128)} %get-tuple-element.21) | copy-start | bytes 393220
  62.2 0.9 %copy-start.3 = (f32[8,32,128]{2,1,0:T(8,128)S(1)}, f32[8,32,128]{2,1,0:T(8,128)}, u32[]{:S(2)}) copy-start(f32[8,32,128]{2,1,0:T(8,128)} %get-tuple-element.15) | copy-start | bytes 393220
  62.3 0.9 %copy-start.2 = (f32[8,32,128]{2,1,0:T(8,128)S(1)}, f32[8,32,128]{2,1,0:T(8,128)}, u32[]{:S(2)}) copy-start(f32[8,32,128]{2,1,0:T(8,128)} %get-tuple-element.24) | copy-start | bytes 393220
  62.3 1.0 %copy-start.1 = (f32[8,32,128]{2,1,0:T(8,128)S(1)}, f32[8,32,128]{2,1,0:T(8,128)}, u32[]{:S(2)}) copy-start(f32[8,32,128]{2,1,0:T(8,128)} %get-tuple-element.22) | copy-start | bytes 393220

commit v15 on v14

--- a/solution.py
+++ b/solution.py
@@ -42,7 +42,10 @@
     diagonal = excess - lower_band - upper_band
     if weights is not None:
         weights.append(diagonal)
-    return [member / diagonal for member in sources]
+    if len(sources) == 1:
+        return [sources[0] / diagonal]
+    inverse = 1.0 / diagonal
+    return [member * inverse for member in sources]
 
 
 def pass_kernel(axis, corrected, *refs):

time: 64.3 us -> 64.3 us (level)
  no operation moved by 1% of the time
where the time goes in v15:
time: 64.3 us; the launch traced here: 64 us
  blocking collectives  40.9 us (64%)
  Pallas kernels  8.27 us (13%)
  starting transfers between devices  7.57 us (12%)
  waiting for transfers between devices  4.04 us (6%)
  local copies, waits for them, and re-layouts  1.51 us (2%)
  other arithmetic  1.39 us (2%)
    all_gather x1, blocking collectives, interface_flux(): gathered = lax.all_gather(terms[None], mesh_axis, axis=0, tiled=True)  40.9 us
    all_to_all x1, starting transfers between devices, shards(): gathered = lax.all_to_all(edge_lon, 'lon', 0, 0, tiled=True)  7.57 us
    all_to_all x1, waiting for transfers between devices, shards(): gathered = lax.all_to_all(edge_lon, 'lon', 0, 0, tiled=True)  4.04 us
    pallas_call x1, Pallas kernels, lon_pass(): pl.pallas_call(lon_kernel, out_shape=(full, full, full, edge))  2.96 us
    pallas_call x1, Pallas kernels, lat_rhs(): pl.pallas_call(lat_rhs_kernel, out_shape=(jax.ShapeDtypeStruct(shape, jnp...  2.68 us
    pallas_call x1, Pallas kernels, lat_matrix(): pl.pallas_call(lat_matrix_kernel, out_shape=(full, full, edge, full), scr...  2.63 us
    unnamed x25, local copies, waits for them, and re-layouts  1.47 us
  transfers between devices with their start and end apart: 1, of which 1 were waited for; matrix products, arithmetic and copies ran while one was open for 0% of the time, Pallas kernels for 4%

profile of v15, /device:TPU:1, one launch (start us, length us, event | category | flops | bytes accessed | tf_op | source)
XLA Modules:
  0.0 64.0 jit_solution(1852678462783597241)
XLA Ops:
  0.0 3.0 %shard_map.47 = (f32[8,32,128]{2,1,0:T(8,128)}, f32[8,32,128]{2,1,0:T(8,128)}, f32[8,32,128]{2,1,0:T(8,128)}, f32[16,7,256]{2,1,0:T(8,128)}) custom-call(f32[8,32,128]{2,1,0:T(8,128)} %source_ref.1, bf16[8,32,128]{2,1,0:T(8,128)(2,1)} %kappa_ref.4, s32[8,32,128]{2,1,0:T(8,128)} %mask_ref.5), custom_call_target="tpu_custom_call" | custom-call | tf_op jit(solution)/shard_map/pallas_call | solution.py:164
  3.0 7.6 %all-to-all-start = ((f32[16,7,256]{2,1,0:T(8,128)}), f32[16,7,256]{2,1,0:T(8,128)S(1)}, u32[]{:S(2)}, u32[]{:S(2)}) async-start(f32[16,7,256]{2,1,0:T(8,128)} %get-tuple-element.16), calls=%async_computation | async-start | bytes 262144 | tf_op jit(solution)/shard_map/all_to_all | solution.py:355
  10.6 2.6 %shard_map.46 = (f32[8,32,128]{2,1,0:T(8,128)}, f32[8,32,128]{2,1,0:T(8,128)}, f32[5,8,128]{2,1,0:T(8,128)}, f32[8,32,128]{2,1,0:T(8,128)}) custom-call(bf16[8,32,128]{2,1,0:T(8,128)(2,1)} %kappa_ref.5, s32[8,32,128]{2,1,0:T(8,128)} %mask_ref.5, bf16[8,32,128]{2,1,0:T(8,128)(2,1)} %kappa_ref.4), custom_call_target="tpu_custom_call" | custom-call | tf_op jit(solution)/shard_map/pallas_call | solution.py:243
  13.2 4.0 %all-to-all-done.gathered_ref = f32[16,7,256]{2,1,0:T(8,128)S(1)} async-done(((f32[16,7,256]{2,1,0:T(8,128)}), f32[16,7,256]{2,1,0:T(8,128)S(1)}, u32[]{:S(2)}, u32[]{:S(2)}) %all-to-all-start) | async-done | bytes 114720 | tf_op jit(solution)/shard_map/all_to_all | solution.py:355
  17.2 0.0 copy-start
  17.2 0.7 %copy-done = f32[16,7,256]{2,1,0:T(8,128)} copy-done((f32[16,7,256]{2,1,0:T(8,128)}, f32[16,7,256]{2,1,0:T(8,128)S(1)}, u32[]{:S(2)}) %copy-start) | copy-done | bytes 114712
  17.9 2.7 %shard_map.48 = (f32[8,32,128]{2,1,0:T(8,128)}, f32[7,8,128]{2,1,0:T(8,128)}) custom-call(s32[1]{0:T(128)} %bitcast.index_ref, f32[16,7,256]{2,1,0:T(8,128)} %copy-done, f32[8,32,128]{2,1,0:T(8,128)} %get-tuple-element.17.p_ref, f32[8,32,128]{2,1,0:T(8,128)} %get-tuple-element.18.u_ref, f32[8,32,128]{2,1,0:T(8,128)} %get-tuple-element.19.w_ref, ...), custom_call_target="tpu_custom_call" | custom-call | tf_op jit(solution)/shard_map/pallas_call | solution.py:254
  20.6 40.9 %all-gather = f32[224,8,128]{2,1,0:T(8,128)S(1)} all-gather(f32[7,8,128]{2,1,0:T(8,128)} %get-tuple-element.23), channel_id=2, replica_groups=mesh['lat'=32,'lon'=16] {'lat'}, dimensions={0}, use_global_device_ids=true | all-gather | bytes 946176 | tf_op jit(solution)/shard_map/all_gather | solution.py:332
  61.5 0.1 fusion
  61.7 0.3 fusion.8
  61.9 0.0 copy-start.4
  62.0 0.1 constant_dynamic-update-slice_fusion.31
  62.2 0.0 copy-start.3
  62.3 0.0 copy-start.2
  62.3 0.0 copy-start.1
  62.5 0.3 copy-done.4
  62.9 0.2 copy-done.3
  63.1 0.1 copy-done.2
  63.2 0.1 copy-done.1
  63.3 0.7 %add_multiply_fusion = f32[8,32,128]{2,1,0:T(8,128)} fusion(f32[8,32,128]{2,1,0:T(8,128)S(1)} %copy-done.3, f32[8,32,128]{2,1,0:T(8,128)S(1)} %copy-done.2, f32[8,32,128]{2,1,0:T(8,128)S(1)} %copy-done.4, f32[8,32,128]{2,1,0:T(8,128)S(1)} %copy-done.1, f32[8,128]{1,0:T(8,128)S(1)} %get-tuple-element.113, f32[8,128]{1,0:T(8,128)S(1)} %get-tuple-element.112), kind=kLoop, calls=%fused_computation.12 | loop fusion | flops 163840 | bytes 663552 | tf_op jit(solution)/shard_map/mul | solution.py:360
  (35 shorter events, 0.2 us)
Async XLA Ops:
  3.0 14.3 %all-to-all-start = ((f32[16,7,256]{2,1,0:T(8,128)}), f32[16,7,256]{2,1,0:T(8,128)S(1)}, u32[]{:S(2)}, u32[]{:S(2)}) async-start(f32[16,7,256]{2,1,0:T(8,128)} %get-tuple-element.16), calls=%async_computation | async-start | bytes 262144 | tf_op jit(solution)/shard_map/all_to_all | solution.py:355
  17.2 0.7 %copy-start = (f32[16,7,256]{2,1,0:T(8,128)}, f32[16,7,256]{2,1,0:T(8,128)S(1)}, u32[]{:S(2)}) copy-start(f32[16,7,256]{2,1,0:T(8,128)S(1)} %all-to-all-done.gathered_ref) | copy-start | bytes 344068
  61.9 0.9 %copy-start.4 = (f32[8,32,128]{2,1,0:T(8,128)S(1)}, f32[8,32,128]{2,1,0:T(8,128)}, u32[]{:S(2)}) copy-start(f32[8,32,128]{2,1,0:T(8,128)} %get-tuple-element.21) | copy-start | bytes 393220
  62.2 0.9 %copy-start.3 = (f32[8,32,128]{2,1,0:T(8,128)S(1)}, f32[8,32,128]{2,1,0:T(8,128)}, u32[]{:S(2)}) copy-start(f32[8,32,128]{2,1,0:T(8,128)} %get-tuple-element.15) | copy-start | bytes 393220
  62.3 0.9 %copy-start.2 = (f32[8,32,128]{2,1,0:T(8,128)S(1)}, f32[8,32,128]{2,1,0:T(8,128)}, u32[]{:S(2)}) copy-start(f32[8,32,128]{2,1,0:T(8,128)} %get-tuple-element.24) | copy-start | bytes 393220
  62.3 1.0 %copy-start.1 = (f32[8,32,128]{2,1,0:T(8,128)S(1)}, f32[8,32,128]{2,1,0:T(8,128)}, u32[]{:S(2)}) copy-start(f32[8,32,128]{2,1,0:T(8,128)} %get-tuple-element.22) | copy-start | bytes 393220
